TPU v7x, 32 devices: a whole 2x2x4 slice. The times are simulated.
32 devices in a mesh: face: 4 (over y, x), tile: 8 (over z, core).
Axes of the slice: x: 2, y: 2, z: 4, core: 2. Of those that a mesh axis runs over, the one named last changes fastest.
Arguments:
- inputs: bfloat16 [4, 8, 8, 16, 192], P('face', 'tile'), may hold values from -6 to 6
- upstream: bfloat16 [4, 8, 8, 16, 384], P('face', 'tile'), may hold values from -6 to 6
- weight_in: bfloat16 [3, 3, 192, 384], replicated, may hold values from -0.15625 to 0.15625
- weight_out: bfloat16 [3, 3, 384, 384], replicated, may hold values from -0.109375 to 0.109375
- seam_link: int32 [4, 4], replicated, may hold values from 0 to 15, as said below
- seam_turn: int32 [4, 4], replicated, may hold values from 0 to 1, as said below
Outputs:
- grad_hidden: bfloat16 [4, 8, 8, 16, 384], P('face', 'tile')
- update_in: bfloat16 [3, 3, 192, 384], replicated
- update_out: bfloat16 [3, 3, 384, 384], replicated
Inputs may be any that keep to these rules, and one draw needn't show every extreme that they name: The seams pair all 16 sides: if seam_link[f, s] = 4 g + q then (g, q) differs from (f, s) and seam_link[g, q] = 4 f + s. seam_turn is equal on the two sides of every seam.
All inputs are finite; a program needn't handle non-finite values.
Results may differ from a plain program's by a relative error of at most 0.0062.
Values may be sent and summed in bfloat16 or wider, within the bound.
No kernel may reach another device: no remote copies, remote signals or barrier semaphores. Data moves between devices by JAX's collectives and lax.ppermute only.
A program may use at most 128 MiB of HBM per device.

v0:
```python
import jax
import jax.numpy as jnp
from jax import lax
from jax.sharding import PartitionSpec as P

root_half = 0.7071067811865476
inv_root_tau = 0.3989422804014327
epsilon = 1e-06


def gelu_value(pre):
    return pre * 0.5 * (1.0 + lax.erf(pre * root_half))


def gelu_slope(pre):
    return 0.5 * (1.0 + lax.erf(pre * root_half)) + pre * jnp.exp(-0.5 * pre * pre) * inv_root_tau


def rim_of(cells):
    return jnp.concatenate([cells[0], cells[-1], cells[:, 0], cells[:, -1]], axis=0)


def face_edges(rim_set, height, breadth, across):
    depth = rim_set.shape[-1]
    layout = rim_set.reshape(4, across, rim_set.shape[1], depth)
    upper = layout[0, :, 0:breadth].reshape(-1, depth)
    lower = layout[3, :, breadth : 2 * breadth].reshape(-1, depth)
    left_side = layout[:, 0, 2 * breadth : 2 * breadth + height].reshape(-1, depth)
    right_side = layout[:, across - 1, 2 * breadth + height :].reshape(-1, depth)
    return jnp.stack([upper, lower, left_side, right_side])


def halo_lookup(edge_set, link_row, turn_row):
    side_len = edge_set.shape[2]
    depth = edge_set.shape[3]
    flattened = edge_set.reshape(-1, side_len, depth)
    picked = jnp.take(flattened, link_row, axis=0)
    return jnp.where((turn_row == 1)[:, None, None], picked[:, ::-1], picked)


def cycle_parts(rim_set, halo_set, geometry):
    row_pos, col_pos, height, breadth, across = geometry
    depth = rim_set.shape[-1]
    side_len = across * breadth
    layout = rim_set.reshape(4, across, rim_set.shape[1], depth)
    nothing = jnp.zeros((1, depth), rim_set.dtype)
    at_top = row_pos == 0
    at_bottom = row_pos == 3
    above = lax.dynamic_index_in_dim(layout, jnp.maximum(row_pos - 1, 0), 0, False)
    below = lax.dynamic_index_in_dim(layout, jnp.minimum(row_pos + 1, 3), 0, False)
    above_row = jnp.where(
        at_top, halo_set[0], above[:, breadth : 2 * breadth].reshape(side_len, depth)
    )
    below_row = jnp.where(at_bottom, halo_set[1], below[:, 0:breadth].reshape(side_len, depth))
    start_up = row_pos * height - 1
    start_down = (row_pos + 1) * height
    above_left = jnp.where(at_top, nothing, lax.dynamic_slice_in_dim(halo_set[2], start_up, 1, 0))
    above_right = jnp.where(at_top, nothing, lax.dynamic_slice_in_dim(halo_set[3], start_up, 1, 0))
    below_left = jnp.where(
        at_bottom, nothing, lax.dynamic_slice_in_dim(halo_set[2], start_down, 1, 0)
    )
    below_right = jnp.where(
        at_bottom, nothing, lax.dynamic_slice_in_dim(halo_set[3], start_down, 1, 0)
    )
    upper_line = jnp.concatenate([above_left, above_row, above_right], axis=0)
    lower_line = jnp.concatenate([below_left, below_row, below_right], axis=0)
    upper = lax.dynamic_slice_in_dim(upper_line, col_pos * breadth, breadth + 2, 0)
    lower = lax.dynamic_slice_in_dim(lower_line, col_pos * breadth, breadth + 2, 0)
    place = row_pos * across + col_pos
    tile_count = 4 * across
    left_tile = lax.dynamic_index_in_dim(rim_set, jnp.maximum(place - 1, 0), 0, False)
    right_tile = lax.dynamic_index_in_dim(rim_set, jnp.minimum(place + 1, tile_count - 1), 0, False)
    left_face = lax.dynamic_slice_in_dim(halo_set[2], row_pos * height, height, 0)
    right_face = lax.dynamic_slice_in_dim(halo_set[3], row_pos * height, height, 0)
    left_side = jnp.where(col_pos == 0, left_face, left_tile[2 * breadth + height :])
    right_side = jnp.where(
        col_pos == across - 1, right_face, right_tile[2 * breadth : 2 * breadth + height]
    )
    return (upper, lower, left_side, right_side)


def assemble(cells, parts):
    upper, lower, left_side, right_side = parts
    middle = jnp.concatenate([left_side[:, None], cells, right_side[:, None]], axis=1)
    return jnp.concatenate([upper[None], middle, lower[None]], axis=0)


def padded_tile(cells, link_row, turn_row, geometry):
    height, breadth, across = (geometry[2], geometry[3], geometry[4])
    rim_set = lax.all_gather(rim_of(cells)[None], "tile", axis=0, tiled=True)
    edges = face_edges(rim_set, height, breadth, across)
    edge_set = lax.all_gather(edges[None], "face", axis=0, tiled=True)
    halo_set = halo_lookup(edge_set, link_row, turn_row)
    return assemble(cells, cycle_parts(rim_set, halo_set, geometry))


def return_cycle(cycle_grads, link_row, turn_row, geometry, face_count):
    height, breadth, across = (geometry[2], geometry[3], geometry[4])
    depth = cycle_grads[0].shape[-1]
    side_len = across * breadth
    rims_zero = jnp.zeros((4 * across, 2 * (height + breadth), depth), jnp.float32)
    halo_zero = jnp.zeros((4, side_len, depth), jnp.float32)
    edges_zero = jnp.zeros((face_count, 4, side_len, depth), jnp.float32)
    _, cycle_back = jax.vjp(
        lambda rim_set, halo_set: cycle_parts(rim_set, halo_set, geometry), rims_zero, halo_zero
    )
    rims_part, halo_part = cycle_back(cycle_grads)
    _, lookup_back = jax.vjp(lambda edge_set: halo_lookup(edge_set, link_row, turn_row), edges_zero)
    (edges_part,) = lookup_back(halo_part)
    own_edges = lax.psum_scatter(edges_part, "face", scatter_dimension=0, tiled=True)
    _, edges_back = jax.vjp(lambda rim_set: face_edges(rim_set, height, breadth, across), rims_zero)
    (edge_rims,) = edges_back(own_edges[0])
    own_rim = lax.psum_scatter(rims_part + edge_rims, "tile", scatter_dimension=0, tiled=True)
    return own_rim[0]


def unfold(padded, height, breadth):
    depth = padded.shape[2]
    windows = []
    for down_step in range(3):
        for side_step in range(3):
            windows.append(
                padded[down_step : down_step + height, side_step : side_step + breadth].reshape(
                    height * breadth, depth
                )
            )
    return jnp.concatenate(windows, axis=1)


def body(inputs, upstream, weight_in, weight_out, seam_link, seam_turn):
    cells = inputs[0, 0]
    height, breadth, width_in = cells.shape
    width_out = weight_out.shape[3]
    across = lax.axis_size("tile") // 4
    place = lax.axis_index("tile")
    row_pos = place // across
    col_pos = place % across
    face_pos = lax.axis_index("face")
    link_row = lax.dynamic_index_in_dim(seam_link, face_pos, 0, False)
    turn_row = lax.dynamic_index_in_dim(seam_turn, face_pos, 0, False)
    geometry = (row_pos, col_pos, height, breadth, across)
    unfolded_in = unfold(padded_tile(cells, link_row, turn_row, geometry), height, breadth)
    pre_one = jnp.dot(
        unfolded_in, weight_in.reshape(-1, width_out), preferred_element_type=jnp.float32
    )
    act = gelu_value(pre_one).astype(jnp.bfloat16)
    padded_act = padded_tile(act.reshape(height, breadth, width_out), link_row, turn_row, geometry)
    unfolded_act = unfold(padded_act, height, breadth)
    kernel_out = weight_out.reshape(-1, width_out)
    pre_two = jnp.dot(unfolded_act, kernel_out, preferred_element_type=jnp.float32)
    grad_two = (upstream[0, 0].reshape(-1, width_out) * gelu_slope(pre_two)).astype(jnp.bfloat16)
    grad_w_out = lax.dot_general(
        unfolded_act, grad_two, (((0,), (0,)), ((), ())), preferred_element_type=jnp.float32
    )
    spread = lax.dot_general(
        grad_two, kernel_out, (((1,), (1,)), ((), ())), preferred_element_type=jnp.float32
    )
    frame = jnp.zeros((height + 2, breadth + 2, width_out), jnp.float32)
    for down_step in range(3):
        for side_step in range(3):
            offset = (down_step * 3 + side_step) * width_out
            piece = spread[:, offset : offset + width_out].reshape(height, breadth, width_out)
            frame = frame + jnp.pad(
                piece, ((down_step, 2 - down_step), (side_step, 2 - side_step), (0, 0))
            )
    cycle_grads = (frame[0], frame[-1], frame[1:-1, 0], frame[1:-1, -1])
    own_rim = return_cycle(cycle_grads, link_row, turn_row, geometry, lax.axis_size("face"))
    _, rim_back = jax.vjp(rim_of, jnp.zeros((height, breadth, width_out), jnp.float32))
    (rim_add,) = rim_back(own_rim)
    grad_act = frame[1:-1, 1:-1] + rim_add
    grad_one = (grad_act * gelu_slope(pre_one.reshape(height, breadth, width_out))).astype(
        jnp.bfloat16
    )
    grad_w_in = lax.dot_general(
        unfolded_in,
        grad_one.reshape(-1, width_out),
        (((0,), (0,)), ((), ())),
        preferred_element_type=jnp.float32,
    )
    size_in = grad_w_in.size
    entries = size_in + grad_w_out.size
    total_in, total_out = lax.psum((grad_w_in, grad_w_out), ("face", "tile"))
    squares = jnp.sum(total_in * total_in) + jnp.sum(total_out * total_out)
    factor = lax.rsqrt(squares / entries + epsilon)
    update_in = (total_in * factor).astype(jnp.bfloat16)
    update_out = (total_out * factor).astype(jnp.bfloat16)
    update_in = update_in.reshape(3, 3, width_in, width_out)
    update_out = update_out.reshape(3, 3, width_out, width_out)
    return (grad_one[None, None], update_in, update_out)


def solution(mesh):
    placed = (
        P("face", "tile", None, None, None),
        P("face", "tile", None, None, None),
        P(),
        P(),
        P(),
        P(),
    )
    return jax.shard_map(
        body,
        mesh=mesh,
        in_specs=placed,
        out_specs=(P("face", "tile", None, None, None), P(), P()),
        check_vma=False,
    )
```

profile of v0, /device:TPU:0, one launch (start us, length us, event | category | flops | bytes accessed | tf_op | source)
XLA Modules:
  0.0 394.6 jit_solution(12386751299314245899)
XLA Ops:
  7.3 0.8 compare_and_fusion
  8.1 0.7 fusion.66
  8.8 0.7 slice_bitcast_fusion.11
  9.6 0.8 fusion.90
  10.4 15.9 %all-gather = bf16[384,192]{1,0:T(8,128)(2,1)S(1)} all-gather(bf16[48,192]{1,0:T(8,128)(2,1)S(1)} %pad_maximum_fusion.9), channel_id=2, replica_groups=mesh['face'=4,'tile'=8] {'tile'}, dimensions={0}, use_global_device_ids=true | all-gather | bytes 165888 | tf_op jit(solution)/shard_map/all_gather | solution.py:90
  26.3 0.7 compare_bitcast_fusion
  27.1 9.0 %all-gather.1 = bf16[16,32,192]{2,1,0:T(8,128)(2,1)S(1)} all-gather(bf16[4,32,192]{2,1,0:T(8,128)(2,1)S(1)} %pad_maximum_fusion.7), channel_id=3, replica_groups=mesh['face'=4,'tile'=8] {'face'}, dimensions={0}, use_global_device_ids=true | all-gather | bytes 245760 | tf_op jit(solution)/shard_map/all_gather | solution.py:92
  37.1 1.0 pad_maximum_fusion.5
  38.2 1.0 pad_maximum_fusion.1
  39.2 0.7 fusion.83
  39.9 1.1 concatenate.72
  41.1 2.6 multiply_convert_fusion.2
  43.7 14.3 %all-gather.2 = bf16[384,384]{1,0:T(8,128)(2,1)S(1)} all-gather(bf16[48,384]{1,0:T(8,128)(2,1)S(1)} %pad_maximum_fusion.8), channel_id=4, replica_groups=mesh['face'=4,'tile'=8] {'tile'}, dimensions={0}, use_global_device_ids=true | all-gather | bytes 331776 | tf_op jit(solution)/shard_map/all_gather | solution.py:90
  58.1 10.1 %all-gather.3 = bf16[16,32,384]{2,1,0:T(8,128)(2,1)} all-gather(bf16[4,32,384]{2,1,0:T(8,128)(2,1)S(1)} %pad_maximum_fusion.4), channel_id=5, replica_groups=mesh['face'=4,'tile'=8] {'face'}, dimensions={0}, use_global_device_ids=true | all-gather | bytes 491520 | tf_op jit(solution)/shard_map/all_gather | solution.py:92
  68.3 2.3 gather_fusion.1
  70.6 1.6 broadcast_select_fusion.1
  72.2 2.2 rev.10
  74.4 1.0 broadcast_select_fusion.2
  76.1 0.9 constant_dynamic-update-slice_fusion.4
  77.7 0.9 fusion.14
  79.0 0.8 broadcast_select_fusion.6
  79.8 0.6 slice_bitcast_fusion.1
  80.4 0.6 broadcast.364.clone.1
  81.1 1.4 dynamic_update_slice.51
  82.5 1.3 fusion.58
  83.8 1.5 slice_select_fusion.1
  85.3 0.6 broadcast.364.clone
  85.9 1.4 dynamic_update_slice.54
  87.4 1.3 fusion.60
  88.7 1.5 slice_select_fusion
  90.1 0.6 broadcast_in_dim.189.clone.4
  90.8 1.3 copy_dynamic-update-slice_fusion
  92.7 1.3 copy_dynamic-update-slice_fusion.1
  94.6 1.3 dynamic_update_slice.60
  96.6 1.3 dynamic_update_slice.61
  98.5 1.3 dynamic_update_slice.58
  100.4 1.3 dynamic_update_slice.59
  101.8 1.7 broadcast_select_fusion
  103.5 2.4 rev.11
  105.9 1.8 select_add_fusion
  107.7 1.0 broadcast_in_dim.187
  108.6 2.5 scatter_fusion
  111.2 1.3 copy.103
  113.1 1.3 dynamic-slice.14
  114.4 0.9 broadcast_in_dim.179
  115.2 1.3 bitcast_dynamic-update-slice_fusion.1
  116.6 1.5 fusion.27
  118.1 0.8 broadcast_in_dim.183
  119.0 1.5 bitcast_dynamic-update-slice_fusion
  120.4 1.6 fusion.16
  122.0 37.9 %all-reduce.34.cloned.1.call-done = f32[4,4,32,384]{3,2,1,0:T(8,128)} async-done(((f32[4,4,32,384]{3,2,1,0:T(8,128)}), f32[4,4,32,384]{3,2,1,0:T(8,128)}) %all-reduce.34.cloned.1.call-update) | async-done | bytes 786448
  159.9 1.6 dynamic-slice_bitcast_fusion.3
  161.5 2.2 bitcast_add_fusion
  163.7 4.3 %fusion.12 = f32[3456,384]{1,0:T(8,128)} fusion(bf16[128,3456]{1,0:T(8,128)(2,1)S(1)} %constant_dynamic-update-slice_fusion, f32[128,384]{1,0:T(8,128)} %copy-done.5, bf16[128,384]{1,0:T(8,128)(2,1)} %bitcast.248), kind=kOutput, calls=%fused_computation.28 | convolution fusion | flops 340279296 | bytes 6488064 | tf_op jit(solution)/shard_map/dot_general | solution.py:152
  168.0 27.4 %reduce-scatter.2.cloned.1.call-done = f32[1,48,384]{2,1,0:T(8,128)} async-done(((f32[8,48,384]{2,1,0:T(8,128)}), f32[1,48,384]{2,1,0:T(8,128)}) %reduce-scatter.2.cloned.1.call-update) | async-done | bytes 73744 | tf_op jit(solution)/shard_map/reduce_scatter | solution.py:113
  195.4 0.7 fusion.87
  196.1 0.8 fusion.88
  196.9 1.2 fusion.11
  198.1 3.1 fusion.92
  201.2 173.8 %all-reduce.36.cloned.1.call-done = (f32[1728,384]{1,0:T(8,128)}, f32[3456,384]{1,0:T(8,128)}) async-done(((f32[1728,384]{1,0:T(8,128)}, f32[3456,384]{1,0:T(8,128)}), (f32[1728,384]{1,0:T(8,128)}, f32[3456,384]{1,0:T(8,128)})) %all-reduce.36.cloned.1.call-update) | async-done | bytes 7962640 | tf_op jit(solution)/shard_map/psum | solution.py:182
  375.0 4.6 %multiply_reduce_fusion = f32[]{:T(128)} fusion(f32[3456,384]{1,0:T(8,128)} %get-tuple-element.4), kind=kLoop, calls=%fused_computation.4 | loop fusion | flops 2654207 | bytes 5308420 | tf_op jit(solution)/shard_map/reduce_sum | solution.py:183
  379.6 1.3 multiply_reduce_fusion.1
  382.3 4.6 %multiply_convert_fusion = bf16[3456,384]{1,0:T(8,128)(2,1)} fusion(f32[3456,384]{1,0:T(8,128)} %get-tuple-element.4, f32[]{:T(128)S(6)} %rsqrt.3), kind=kLoop, calls=%fused_computation.3 | loop fusion | flops 2654208 | bytes 7962628 | tf_op jit(solution)/shard_map/convert_element_type | solution.py:186
  386.8 1.3 multiply_convert_fusion.1
  (103 shorter events, 6.8 us)
Async XLA Ops:
  7.2 69.9 %copy-start = (bf16[3,3,384,384]{3,2,1,0:T(8,128)(2,1)S(1)}, bf16[3,3,384,384]{3,2,1,0:T(8,128)(2,1)}, u32[]{:S(2)}) copy-start(bf16[3,3,384,384]{3,2,1,0:T(8,128)(2,1)} %param.9) | copy-start | bytes 7962628
  7.2 32.8 %copy-start.7 = (bf16[1,1,8,16,192]{4,3,2,1,0:T(8,128)(2,1)S(1)}, bf16[1,1,8,16,192]{4,3,2,1,0:T(8,128)(2,1)}, u32[]{:S(2)}) copy-start(bf16[1,1,8,16,192]{4,3,2,1,0:T(8,128)(2,1)} %param.6) | copy-start | bytes 147460
  7.2 152.7 %all-reduce.34.cloned.1.call-start = ((), (), s32[]{:S(2)}) async-start(), calls=%async_computation.2 | async-start | bytes 1572864
  8.1 31.0 %copy-start.10 = (pred[4]{0:T(512)(128)(4,1)}, pred[4]{0:T(512)(128)(4,1)S(1)}, u32[]{:S(2)}) copy-start(pred[4]{0:T(512)(128)(4,1)S(1)} %compare_and_fusion) | copy-start | bytes 16
  8.8 18.1 %copy-start.14 = (s32[4]{0:T(128)}, s32[4]{0:T(128)S(1)}, u32[]{:S(2)}) copy-start(s32[4]{0:T(128)S(1)} %fusion.66) | copy-start | bytes 52
  27.0 12.2 %copy-start.11 = (pred[4]{0:T(512)(128)(4,1)}, pred[4]{0:T(512)(128)(4,1)S(1)}, u32[]{:S(2)}) copy-start(pred[4]{0:T(512)(128)(4,1)S(1)} %compare_bitcast_fusion) | copy-start | bytes 16
  27.0 9.6 %copy-start.13 = (s32[1024]{0:T(1024)}, s32[1024]{0:T(1024)S(1)}, u32[]{:S(2)}) copy-start(s32[1024]{0:T(1024)S(1)} %pad_clamp_fusion) | copy-start | bytes 12292
  41.1 34.6 %copy-start.3 = (bf16[128,1728]{1,0:T(8,128)(2,1)}, bf16[128,1728]{1,0:T(8,128)(2,1)S(1)}, u32[]{:S(2)}) copy-start(bf16[128,1728]{1,0:T(8,128)(2,1)S(1)} %concatenate.72) | copy-start | bytes 1327108
  43.6 32.3 %copy-start.4 = (bf16[128,384]{1,0:T(8,128)(2,1)}, bf16[128,384]{1,0:T(8,128)(2,1)S(1)}, u32[]{:S(2)}) copy-start(bf16[128,384]{1,0:T(8,128)(2,1)S(1)} %get-tuple-element.96) | copy-start | bytes 294916
  76.0 1.8 copy-start.8
  77.7 1.1 copy-start.5
  78.7 23.1 %copy-start.12 = (pred[4]{0:T(512)(128)(4,1)S(1)}, pred[4]{0:T(512)(128)(4,1)}, u32[]{:S(2)}) copy-start(pred[4]{0:T(512)(128)(4,1)} %copy-done.11) | copy-start | bytes 16
  79.0 0.8 copy-start.6
  111.1 84.2 %reduce-scatter.2.cloned.1.call-start = ((), (), s32[]{:S(2)}) async-start(), calls=%async_computation.1 | async-start | bytes 663552 | tf_op jit(solution)/shard_map/reduce_scatter | solution.py:113
  163.7 211.3 %all-reduce.36.cloned.1.call-start = ((), (), s32[]{:S(2)}) async-start(), calls=%async_computation.3 | async-start | bytes 15925248 | tf_op jit(solution)/shard_map/psum | solution.py:182
  198.1 3.1 copy-start.9
  375.0 4.6 %copy-start.1 = (f32[1728,384]{1,0:T(8,128)S(1)}, f32[1728,384]{1,0:T(8,128)}, u32[]{:S(2)}) copy-start(f32[1728,384]{1,0:T(8,128)} %get-tuple-element.3) | copy-start | bytes 7962628
  382.3 4.6 %copy-start.2 = (f32[1728,384]{1,0:T(8,128)S(1)}, f32[1728,384]{1,0:T(8,128)}, u32[]{:S(2)}) copy-start(f32[1728,384]{1,0:T(8,128)} %get-tuple-element.3) | copy-start | bytes 7962628
Sparse Core Ops, SparseCore 0:
  111.2 48.5 all-reduce.33
  163.8 31.4 reduce-scatter.1
  201.9 173.0 all-reduce.35
where the time goes:
time: 397 us; the launch traced here: 395 us
  waiting for transfers between devices  239 us (60%)
  blocking collectives  49.3 us (12%)
  local copies, waits for them, and re-layouts  40.5 us (10%)
  other arithmetic  38.3 us (10%)
  between operations  15.8 us (4%)
  matrix products  11.4 us (3%)
    psum x1, waiting for transfers between devices, body(): total_in, total_out = lax.psum((grad_w_in, grad_w_out), ('face', 'tile'))  174 us
    unnamed x4, waiting for transfers between devices  37.9 us
    all_gather x2, blocking collectives, padded_tile(): rim_set = lax.all_gather(rim_of(cells)[None], 'tile', axis=0, tiled=True)  30.2 us
    reduce_scatter x1, waiting for transfers between devices, return_cycle(): lax.psum_scatter(rims_part + edge_rims, 'tile', scatter_dimension=0, tile...  27.4 us
    all_gather x2, blocking collectives, padded_tile(): edge_set = lax.all_gather(edges[None], 'face', axis=0, tiled=True)  19.1 us
  transfers between devices with their start and end apart: 3, of which 3 were waited for; matrix products, arithmetic and copies ran while one was open for 4% of the time, Pallas kernels for 0%

commit v1 on v0

v1 whole, which is shorter than its diff:
```python
import numpy as np
import jax
import jax.numpy as jnp
from jax import lax
from jax.sharding import PartitionSpec as P

root_half = 0.7071067811865476
inv_root_tau = 0.3989422804014327
epsilon = 1e-06
both = ("face", "tile")


def gelu_value(pre):
    return pre * 0.5 * (1.0 + lax.erf(pre * root_half))


def gelu_slope(pre):
    return 0.5 * (1.0 + lax.erf(pre * root_half)) + pre * jnp.exp(-0.5 * pre * pre) * inv_root_tau


def rim_of(cells):
    return jnp.concatenate([cells[0], cells[-1], cells[:, 0], cells[:, -1]], axis=0)


def border_of(frame):
    return jnp.concatenate([frame[0], frame[-1], frame[1:-1, 0], frame[1:-1, -1]], axis=0)


def halo_sources(seam_link, seam_turn, faces, tiles, height, breadth):
    across = tiles // 4
    side = across * breadth
    rim_len = 2 * (height + breadth)
    a = np.array([0] * (breadth + 2) + [height + 1] * (breadth + 2) + list(range(1, height + 1)) * 2)
    b = np.array(list(range(breadth + 2)) * 2 + [0] * height + [breadth + 1] * height)
    dev = np.arange(faces * tiles)
    f = dev // tiles
    t = dev % tiles
    i = (t // across)[:, None] * height - 1 + a[None, :]
    j = (t % across)[:, None] * breadth - 1 + b[None, :]
    out_i = (i < 0) | (i >= side)
    out_j = (j < 0) | (j >= side)
    corner = out_i & out_j
    seam = (out_i | out_j) & ~corner
    s = np.where(i < 0, 0, np.where(i >= side, 1, np.where(j < 0, 2, 3)))
    p = np.where(out_i, j, i)
    fb = np.broadcast_to(f[:, None], i.shape)
    link = seam_link[fb, s]
    turn = seam_turn[fb, s]
    g = link // 4
    q = link % 4
    pp = jnp.where(turn == 1, side - 1 - p, p)
    si = jnp.where(q == 0, 0, jnp.where(q == 1, side - 1, pp))
    sj = jnp.where(q == 2, 0, jnp.where(q == 3, side - 1, pp))
    src_face = jnp.where(seam, g, fb)
    src_i = jnp.clip(jnp.where(seam, si, i), 0, side - 1)
    src_j = jnp.clip(jnp.where(seam, sj, j), 0, side - 1)
    li = src_i % height
    lj = src_j % breadth
    rim_idx = jnp.where(
        li == 0,
        lj,
        jnp.where(
            li == height - 1,
            breadth + lj,
            jnp.where(lj == 0, 2 * breadth + li, 2 * breadth + height + li),
        ),
    )
    tile_of = (src_i // height) * across + src_j // breadth
    gid = (src_face * tiles + tile_of) * rim_len + rim_idx
    return jnp.where(corner, -1, gid).astype(jnp.int32)


def padded_tile(cells, own_src):
    height, breadth, depth = cells.shape
    rims = lax.all_gather(rim_of(cells), both, axis=0, tiled=True)
    count = rims.shape[0]
    rims = jnp.concatenate([rims, jnp.zeros((1, depth), rims.dtype)], axis=0)
    halo = jnp.take(rims, jnp.where(own_src < 0, count, own_src), axis=0)
    upper = halo[: breadth + 2]
    lower = halo[breadth + 2 : 2 * breadth + 4]
    left_side = halo[2 * breadth + 4 : 2 * breadth + 4 + height]
    right_side = halo[2 * breadth + 4 + height :]
    middle = jnp.concatenate([left_side[:, None], cells, right_side[:, None]], axis=1)
    return jnp.concatenate([upper[None], middle, lower[None]], axis=0)


def unfold(padded, height, breadth):
    depth = padded.shape[2]
    windows = []
    for down_step in range(3):
        for side_step in range(3):
            windows.append(
                padded[down_step : down_step + height, side_step : side_step + breadth].reshape(
                    height * breadth, depth
                )
            )
    return jnp.concatenate(windows, axis=1)


def body(inputs, upstream, weight_in, weight_out, seam_link, seam_turn):
    cells = inputs[0, 0]
    height, breadth, width_in = cells.shape
    width_out = weight_out.shape[3]
    faces = lax.axis_size("face")
    tiles = lax.axis_size("tile")
    rim_len = 2 * (height + breadth)
    device = lax.axis_index("face") * tiles + lax.axis_index("tile")
    sources = halo_sources(seam_link, seam_turn, faces, tiles, height, breadth)
    own_src = lax.dynamic_index_in_dim(sources, device, 0, False)
    unfolded_in = unfold(padded_tile(cells, own_src), height, breadth)
    pre_one = jnp.dot(
        unfolded_in, weight_in.reshape(-1, width_out), preferred_element_type=jnp.float32
    )
    act = gelu_value(pre_one).astype(jnp.bfloat16)
    padded_act = padded_tile(act.reshape(height, breadth, width_out), own_src)
    unfolded_act = unfold(padded_act, height, breadth)
    kernel_out = weight_out.reshape(-1, width_out)
    pre_two = jnp.dot(unfolded_act, kernel_out, preferred_element_type=jnp.float32)
    grad_two = (upstream[0, 0].reshape(-1, width_out) * gelu_slope(pre_two)).astype(jnp.bfloat16)
    grad_w_out = lax.dot_general(
        unfolded_act, grad_two, (((0,), (0,)), ((), ())), preferred_element_type=jnp.float32
    )
    spread = lax.dot_general(
        grad_two, kernel_out, (((1,), (1,)), ((), ())), preferred_element_type=jnp.float32
    )
    frame = jnp.zeros((height + 2, breadth + 2, width_out), jnp.float32)
    for down_step in range(3):
        for side_step in range(3):
            offset = (down_step * 3 + side_step) * width_out
            piece = spread[:, offset : offset + width_out].reshape(height, breadth, width_out)
            frame = frame + jnp.pad(
                piece, ((down_step, 2 - down_step), (side_step, 2 - side_step), (0, 0))
            )
    borders = lax.all_gather(border_of(frame), both, axis=0, tiled=True)
    borders, grad_w_out = lax.optimization_barrier((borders, grad_w_out))
    total_out = lax.psum(grad_w_out, both)
    own_cells = device * rim_len + jnp.arange(rim_len, dtype=jnp.int32)
    picker = (sources.reshape(1, -1) == own_cells[:, None]).astype(jnp.float32)
    own_rim = jnp.dot(picker, borders, precision=lax.Precision.HIGHEST)
    _, rim_back = jax.vjp(rim_of, jnp.zeros((height, breadth, width_out), jnp.float32))
    (rim_add,) = rim_back(own_rim)
    grad_act = frame[1:-1, 1:-1] + rim_add
    grad_one = (grad_act * gelu_slope(pre_one.reshape(height, breadth, width_out))).astype(
        jnp.bfloat16
    )
    grad_w_in = lax.dot_general(
        unfolded_in,
        grad_one.reshape(-1, width_out),
        (((0,), (0,)), ((), ())),
        preferred_element_type=jnp.float32,
    )
    total_out, grad_w_in = lax.optimization_barrier((total_out, grad_w_in))
    total_in = lax.psum(grad_w_in, both)
    entries = total_in.size + total_out.size
    squares = jnp.sum(total_in * total_in) + jnp.sum(total_out * total_out)
    factor = lax.rsqrt(squares / entries + epsilon)
    update_in = (total_in * factor).astype(jnp.bfloat16)
    update_out = (total_out * factor).astype(jnp.bfloat16)
    update_in = update_in.reshape(3, 3, width_in, width_out)
    update_out = update_out.reshape(3, 3, width_out, width_out)
    return (grad_one[None, None], update_in, update_out)


def solution(mesh):
    placed = (
        P("face", "tile", None, None, None),
        P("face", "tile", None, None, None),
        P(),
        P(),
        P(),
        P(),
    )
    return jax.shard_map(
        body,
        mesh=mesh,
        in_specs=placed,
        out_specs=(P("face", "tile", None, None, None), P(), P()),
        check_vma=False,
    )
```

time: 397 us -> 523 us (1.32)
  waiting for transfers between devices: 239 us -> 384 us
  other arithmetic: 38.3 us -> 17.2 us
    psum x1 -> x2, waiting for transfers between devices: 174 us -> 280 us  [the longest x1 144 us: body(): total_out = lax.psum(grad_w_out, both)]
    all_gather x0 -> x2, waiting for transfers between devices: none -> 103 us  [the longest x1 52.9 us: body(): borders = lax.all_gather(border_of(frame), both, axis=0, tiled=True)]
    unnamed x4, waiting for transfers between devices: 37.9 us -> 0.07 us
    gather x2 -> x5, local copies, waits for them, and re-layouts: 2.87 us -> 30.9 us  [the longest x2 14.1 us: halo_sources(): link = seam_link[fb, s]]
    reduce_scatter x1 -> x0, waiting for transfers between devices: 27.4 us -> none  [return_cycle(): lax.psum_scatter(rims_part + edge_rims, 'tile', scatter_dimension=0, tile...]
    dynamic_update_slice x10 -> x0, local copies, waits for them, and re-layouts: 13.6 us -> none  [the longest x1 1.46 us: cycle_parts(): lax.dynamic_index_in_dim(layout, jnp.minimum(row_pos + 1, 3), 0, False)]
    select_n x17 -> x5, other arithmetic: 9.08 us -> 0.88 us  [the longest x3 0.8 us: padded_tile(): halo = jnp.take(rims, jnp.where(own_src < 0, count, own_src), axis=0)]
    broadcast_in_dim x9 -> x11, local copies, waits for them, and re-layouts: 6.4 us -> 0.11 us  [the longest x4 0.05 us: padded_tile(): return jnp.concatenate([upper[None], middle, lower[None]], axis=0)]
  transfers between devices with their start and end apart: 3 -> 4, of which waited for: 3 -> 4; matrix products, arithmetic and copies ran while one was open for 4% -> 3% of each run, Pallas kernels for 0% -> 0%
where the time goes in v1:
time: 523 us; the launch traced here: 522 us
  waiting for transfers between devices  384 us (73%)
  blocking collectives  46.6 us (9%)
  local copies, waits for them, and re-layouts  45.5 us (9%)
  other arithmetic  17.2 us (3%)
  between operations  15.7 us (3%)
  matrix products  13.3 us (3%)
    psum x1, waiting for transfers between devices, body(): total_out = lax.psum(grad_w_out, both)  144 us
    psum x1, waiting for transfers between devices, body(): total_in = lax.psum(grad_w_in, both)  136 us
    all_gather x1, waiting for transfers between devices, body(): borders = lax.all_gather(border_of(frame), both, axis=0, tiled=True)  52.9 us
    all_gather x1, waiting for transfers between devices, padded_tile(): rims = lax.all_gather(rim_of(cells), both, axis=0, tiled=True)  50.4 us
    all_gather x1, blocking collectives, padded_tile(): rims = lax.all_gather(rim_of(cells), both, axis=0, tiled=True)  46.6 us
    gather x2, local copies, waits for them, and re-layouts, halo_sources(): link = seam_link[fb, s]  14.1 us
    gather x1, local copies, waits for them, and re-layouts, halo_sources(): turn = seam_turn[fb, s]  13.8 us
  transfers between devices with their start and end apart: 4, of which 4 were waited for; matrix products, arithmetic and copies ran while one was open for 3% of the time, Pallas kernels for 0%

profile of v1, /device:TPU:0, one launch (start us, length us, event | category | flops | bytes accessed | tf_op | source)
XLA Modules:
  0.0 522.1 jit_solution(16228750601630795592)
XLA Ops:
  7.2 0.0 copy-start
  7.2 0.0 all-gather.4.cloned.1.call-start
  7.2 1.0 copy.73
  8.3 0.7 slice_bitcast_fusion.9
  9.0 14.0 %gather_fusion = s32[1664]{0:T(1024)S(1)} fusion(s32[4,4]{1,0:T(4,128)S(1)} %copy-done.1, s32[1664]{0:T(1024)} %constant.247), kind=kCustom, calls=%fused_computation | custom fusion | bytes 26624 | tf_op jit(solution)/shard_map/gather | solution.py:47
  23.0 0.0 copy-start.2
  23.0 0.1 reshape.188
  23.1 0.6 copy-done.2
  23.7 0.0 copy-start.17
  23.7 0.0 copy-start.20
  23.7 0.0 copy-start.21
  23.7 13.8 %gather_fusion.1 = s32[1664]{0:T(1024)S(1)} fusion(s32[4,4]{1,0:T(4,128)S(1)} %copy-done.2, s32[1664]{0:T(1024)S(1)} %copy-done.3), kind=kCustom, calls=%fused_computation.1 | custom fusion | bytes 26624 | tf_op jit(solution)/shard_map/gather | solution.py:48
  37.6 0.1 reshape.217
  37.7 0.1 fusion.35
  37.8 0.5 compare_and_fusion
  38.4 46.6 %all_gather.9 = bf16[1536,192]{1,0:T(8,128)(2,1)S(1)} all-gather(bf16[48,192]{1,0:T(8,128)(2,1)S(1)} %pad_maximum_fusion.7), channel_id=1, replica_groups=mesh['face'=4,'tile'=8] {'face','tile'}, dimensions={0}, use_global_device_ids=true | all-gather | bytes 608256 | tf_op jit(solution)/shard_map/all_gather | solution.py:75
  84.9 0.6 pad_clamp_fusion
  85.5 0.1 concatenate.70
  85.7 0.8 gather_fusion.2
  86.5 0.7 broadcast_select_fusion.1
  87.3 0.1 pad_maximum_fusion.1
  87.5 0.6 copy.52
  88.2 0.6 copy.56
  88.8 0.6 copy.57
  89.5 1.1 concatenate.76
  90.6 2.6 multiply_convert_fusion.2
  93.2 0.6 pad_maximum_fusion.6
  93.8 0.0 all-gather.4.cloned.1.call-update
  93.9 0.0 all-gather.6.cloned.1.call-start
  93.9 50.4 %all-gather.4.cloned.1.call-done = bf16[1536,384]{1,0:T(8,128)(2,1)} async-done(((bf16[48,384]{1,0:T(8,128)(2,1)}), bf16[1536,384]{1,0:T(8,128)(2,1)}) %all-gather.4.cloned.1.call-update) | async-done | bytes 1179664 | tf_op jit(solution)/shard_map/all_gather | solution.py:75
  144.3 2.4 concatenate.78
  146.7 2.2 gather_fusion.3
  148.9 0.1 broadcast_select_fusion
  149.1 0.1 pad_maximum_fusion.2
  149.2 0.1 pad_maximum_fusion
  149.3 0.1 fusion.58
  149.5 0.0 copy-start.12
  149.5 0.9 constant_dynamic-update-slice_fusion.4
  150.4 0.1 fusion.57
  150.6 0.6 fusion.64
  151.2 0.9 fusion.16
  152.2 0.1 fusion.55
  152.3 0.2 pad_add_fusion
  152.6 0.7 copy-done.9
  153.3 0.7 maximum_bitcast_fusion
  153.9 0.0 all-gather.6.cloned.1.call-update
  154.0 0.0 all-reduce.18.cloned.1.call-start
  154.0 4.3 fusion.14
  158.3 52.9 %all-gather.6.cloned.1.call-done = f32[32,52,384]{2,1,0:T(8,128)} async-done(((f32[1,52,384]{2,1,0:T(8,128)}), f32[32,52,384]{2,1,0:T(8,128)}) %all-gather.6.cloned.1.call-update) | async-done | bytes 2555920 | tf_op jit(solution)/shard_map/all_gather | solution.py:134
  211.2 3.5 reshape.219
  214.7 0.0 all-reduce.18.cloned.1.call-update
  214.7 0.0 all-reduce.20.cloned.1.call-start
  214.8 0.1 eq.53
  214.9 2.9 fusion
  217.9 0.1 fusion.13
  218.0 0.6 copy-done.13
  218.6 2.0 fusion.65
  220.7 143.9 %all-reduce.18.cloned.1.call-done = f32[3456,384]{1,0:T(8,128)} async-done(((f32[3456,384]{1,0:T(8,128)}), f32[3456,384]{1,0:T(8,128)}) %all-reduce.18.cloned.1.call-update) | async-done | bytes 5308432 | tf_op jit(solution)/shard_map/psum | solution.py:136
  364.5 0.0 all-reduce.20.cloned.1.call-update
  364.6 4.4 multiply_reduce_fusion
  369.0 136.4 %all-reduce.20.cloned.1.call-done = f32[1728,384]{1,0:T(8,128)} async-done(((f32[1728,384]{1,0:T(8,128)}), f32[1728,384]{1,0:T(8,128)}) %all-reduce.20.cloned.1.call-update) | async-done | bytes 2654224 | tf_op jit(solution)/shard_map/psum | solution.py:153
  505.4 3.0 multiply_reduce_fusion.1
  509.7 4.6 multiply_convert_fusion
  514.3 1.3 multiply_convert_fusion.1
  (77 shorter events, 0.6 us)
Async XLA Ops:
  7.2 143.4 %copy-start = (bf16[3,3,384,384]{3,2,1,0:T(8,128)(2,1)S(1)}, bf16[3,3,384,384]{3,2,1,0:T(8,128)(2,1)}, u32[]{:S(2)}) copy-start(bf16[3,3,384,384]{3,2,1,0:T(8,128)(2,1)} %param.21) | copy-start | bytes 7962628
  7.2 1.8 copy-start.1
  7.2 137.1 %all-gather.4.cloned.1.call-start = ((), (), s32[]{:S(2)}) async-start(), calls=%async_computation | async-start | bytes 1216512 | tf_op jit(solution)/shard_map/all_gather | solution.py:75
  9.0 14.2 %copy-start.3 = (s32[1664]{0:T(1024)S(1)}, s32[1664]{0:T(1024)}, u32[]{:S(2)}) copy-start(s32[1664]{0:T(1024)} %constant.247) | copy-start | bytes 19972
  23.0 0.7 copy-start.2
  23.7 13.8 %copy-start.18 = (s32[1664]{0:T(1024)S(1)}, s32[1664]{0:T(1024)}, u32[]{:S(2)}) copy-start(s32[1664]{0:T(1024)} %constant.256) | copy-start | bytes 19972
  23.7 13.8 %copy-start.19 = (s32[1664]{0:T(1024)S(1)}, s32[1664]{0:T(1024)}, u32[]{:S(2)}) copy-start(s32[1664]{0:T(1024)} %constant.257) | copy-start | bytes 19972
  23.7 14.0 %copy-start.15 = (s32[32,52]{1,0:T(8,128)S(1)}, s32[32,52]{1,0:T(8,128)}, u32[]{:S(2)}) copy-start(s32[32,52]{1,0:T(8,128)} %constant.170.clone) | copy-start | bytes 19972
  23.7 14.0 %copy-start.16 = (s32[32,52]{1,0:T(8,128)S(1)}, s32[32,52]{1,0:T(8,128)}, u32[]{:S(2)}) copy-start(s32[32,52]{1,0:T(8,128)} %constant.177.clone) | copy-start | bytes 19972
  23.7 14.0 %copy-start.17 = (s32[32,52]{1,0:T(8,128)S(1)}, s32[32,52]{1,0:T(8,128)}, u32[]{:S(2)}) copy-start(s32[32,52]{1,0:T(8,128)} %constant.176.clone) | copy-start | bytes 19972
  23.7 14.0 %copy-start.20 = (pred[32,52]{1,0:T(32,128)(4,1)S(1)}, pred[32,52]{1,0:T(32,128)(4,1)}, u32[]{:S(2)}) copy-start(pred[32,52]{1,0:T(32,128)(4,1)} %constant.178.clone) | copy-start | bytes 4996
  23.7 14.0 %copy-start.21 = (pred[32,52]{1,0:T(32,128)(4,1)S(1)}, pred[32,52]{1,0:T(32,128)(4,1)}, u32[]{:S(2)}) copy-start(pred[32,52]{1,0:T(32,128)(4,1)} %constant.175.clone) | copy-start | bytes 4996
  86.4 3.0 copy-start.14
  90.6 58.5 %copy-start.5 = (bf16[128,1728]{1,0:T(8,128)(2,1)}, bf16[128,1728]{1,0:T(8,128)(2,1)S(1)}, u32[]{:S(2)}) copy-start(bf16[128,1728]{1,0:T(8,128)(2,1)S(1)} %concatenate.76) | copy-start | bytes 1327108
  90.6 58.3 %copy-start.22 = (pred[52]{0:T(512)(128)(4,1)S(1)}, pred[52]{0:T(512)(128)(4,1)}, u32[]{:S(2)}) copy-start(pred[52]{0:T(512)(128)(4,1)} %compare_and_fusion) | copy-start | bytes 160
  93.2 56.2 %copy-start.7 = (bf16[128,384]{1,0:T(8,128)(2,1)}, bf16[128,384]{1,0:T(8,128)(2,1)S(1)}, u32[]{:S(2)}) copy-start(bf16[128,384]{1,0:T(8,128)(2,1)S(1)} %get-tuple-element.64) | copy-start | bytes 294916
  93.9 117.3 %all-gather.6.cloned.1.call-start = ((), (), s32[]{:S(2)}) async-start(), calls=%async_computation.3 | async-start | bytes 2838528 | tf_op jit(solution)/shard_map/all_gather | solution.py:134
  149.5 1.8 copy-start.12
  151.2 1.1 copy-start.8
  152.5 0.7 copy-start.9
  154.0 210.6 %all-reduce.18.cloned.1.call-start = ((), (), s32[]{:S(2)}) async-start(), calls=%async_computation.1 | async-start | bytes 10616832 | tf_op jit(solution)/shard_map/psum | solution.py:136
  214.7 3.2 copy-start.10
  214.7 3.9 copy-start.6
  214.7 290.7 %all-reduce.20.cloned.1.call-start = ((), (), s32[]{:S(2)}) async-start(), calls=%async_computation.2 | async-start | bytes 5308416 | tf_op jit(solution)/shard_map/psum | solution.py:153
  214.9 3.0 copy-start.11
  218.0 0.6 copy-start.13
  509.7 4.6 copy-start.4
Sparse Core Ops, SparseCore 0:
  94.0 50.2 all-gather.3
  154.1 57.0 all-gather.5
  216.9 147.5 all-reduce.17
  370.5 134.8 all-reduce.19

commit v2 on v1

v2 whole, which is shorter than its diff:
```python
import numpy as np
import jax
import jax.numpy as jnp
from jax import lax
from jax.sharding import PartitionSpec as P

root_half = 0.7071067811865476
inv_root_tau = 0.3989422804014327
epsilon = 1e-06


def gelu_value(pre):
    return pre * 0.5 * (1.0 + lax.erf(pre * root_half))


def gelu_slope(pre):
    return 0.5 * (1.0 + lax.erf(pre * root_half)) + pre * jnp.exp(-0.5 * pre * pre) * inv_root_tau


def rim_of(cells):
    return jnp.concatenate([cells[0], cells[-1], cells[:, 0], cells[:, -1]], axis=0)


def border_of(frame):
    return jnp.concatenate([frame[0], frame[-1], frame[1:-1, 0], frame[1:-1, -1]], axis=0)


def rim_index(li, lj, height, breadth):
    return np.where(
        li == 0,
        lj,
        np.where(
            li == height - 1,
            breadth + lj,
            np.where(lj == 0, 2 * breadth + li, 2 * breadth + height + li),
        ),
    )


def face_maps(tiles, height, breadth):
    across = tiles // 4
    side = across * breadth
    rim_len = 2 * (height + breadth)
    a = np.array([0] * (breadth + 2) + [height + 1] * (breadth + 2) + list(range(1, height + 1)) * 2)
    b = np.array(list(range(breadth + 2)) * 2 + [0] * height + [breadth + 1] * height)
    t = np.arange(tiles)
    i = (t // across)[:, None] * height - 1 + a[None, :]
    j = (t % across)[:, None] * breadth - 1 + b[None, :]
    out_i = (i < 0) | (i >= side)
    out_j = (j < 0) | (j >= side)
    inside = ~out_i & ~out_j
    seam = out_i ^ out_j
    ci = np.clip(i, 0, side - 1)
    cj = np.clip(j, 0, side - 1)
    owner = (ci // height) * across + cj // breadth
    intra = np.where(inside, owner * rim_len + rim_index(ci % height, cj % breadth, height, breadth), -1)
    s = np.where(i < 0, 0, np.where(i >= side, 1, np.where(j < 0, 2, 3)))
    p = np.where(out_i, cj, ci)
    seam_cell = np.where(seam, s * side + p, -1)
    pos = np.arange(side)
    ei = np.concatenate([np.zeros(side, int), np.full(side, side - 1), pos, pos])
    ej = np.concatenate([pos, pos, np.zeros(side, int), np.full(side, side - 1)])
    sides = np.repeat(np.arange(4), side)
    li = ei % height
    lj = ej % breadth
    k = np.where(sides == 0, lj, np.where(sides == 1, breadth + lj, np.where(sides == 2, 2 * breadth + li, 2 * breadth + height + li)))
    edge = ((ei // height) * across + ej // breadth) * rim_len + k
    return intra.astype(np.int32), seam_cell.astype(np.int32), edge.astype(np.int32)


def one_hot(rows, cols, dtype):
    return (rows[:, None] == cols[None, :]).astype(dtype)


def halo_lookup(edge_set, link_row, turn_row):
    side_len = edge_set.shape[2]
    depth = edge_set.shape[3]
    flattened = edge_set.reshape(-1, side_len, depth)
    picked = jnp.take(flattened, link_row, axis=0)
    return jnp.where((turn_row == 1)[:, None, None], picked[:, ::-1], picked)


def padded_tile(cells, maps, place, link_row, turn_row):
    height, breadth, depth = cells.shape
    intra, seam_cell, edge = maps
    rim_len = 2 * (height + breadth)
    tiles = intra.shape[0]
    side = edge.shape[0] // 4
    rims = lax.all_gather(rim_of(cells), "tile", axis=0, tiled=True)
    edges = jnp.dot(
        one_hot(jnp.asarray(edge), jnp.arange(tiles * rim_len), cells.dtype),
        rims,
        preferred_element_type=jnp.float32,
    ).astype(cells.dtype)
    edge_set = lax.all_gather(edges.reshape(1, 4, side, depth), "face", axis=0, tiled=True)
    seam_halo = halo_lookup(edge_set, link_row, turn_row).reshape(4 * side, depth)
    own_intra = lax.dynamic_index_in_dim(jnp.asarray(intra), place, 0, False)
    own_seam = lax.dynamic_index_in_dim(jnp.asarray(seam_cell), place, 0, False)
    pool = jnp.concatenate([rims, seam_halo], axis=0)
    source = jnp.where(own_intra >= 0, own_intra, jnp.where(own_seam >= 0, tiles * rim_len + own_seam, -1))
    halo = jnp.dot(
        one_hot(source, jnp.arange(pool.shape[0]), cells.dtype),
        pool,
        preferred_element_type=jnp.float32,
    ).astype(cells.dtype)
    upper = halo[: breadth + 2]
    lower = halo[breadth + 2 : 2 * breadth + 4]
    left_side = halo[2 * breadth + 4 : 2 * breadth + 4 + height]
    right_side = halo[2 * breadth + 4 + height :]
    middle = jnp.concatenate([left_side[:, None], cells, right_side[:, None]], axis=1)
    return jnp.concatenate([upper[None], middle, lower[None]], axis=0)


def return_border(border, maps, place, link_row, turn_row):
    intra, seam_cell, edge = maps
    tiles, frame_len = intra.shape
    depth = border.shape[-1]
    rim_len = frame_len - 4
    side = edge.shape[0] // 4
    exact = lax.Precision.HIGHEST
    borders = lax.all_gather(border, "tile", axis=0, tiled=True)
    seam_sum = jnp.dot(
        one_hot(jnp.arange(4 * side), jnp.asarray(seam_cell.reshape(-1)), jnp.float32),
        borders,
        precision=exact,
    )
    seam_set = lax.all_gather(seam_sum.reshape(1, 4, side, depth), "face", axis=0, tiled=True)
    own_edges = halo_lookup(seam_set, link_row, turn_row).reshape(4 * side, depth)
    own_cells = place * rim_len + jnp.arange(rim_len)
    from_tiles = jnp.dot(
        one_hot(own_cells, jnp.asarray(intra.reshape(-1)), jnp.float32), borders, precision=exact
    )
    from_seams = jnp.dot(
        one_hot(own_cells, jnp.asarray(edge), jnp.float32), own_edges, precision=exact
    )
    return from_tiles + from_seams


def unfold(padded, height, breadth):
    depth = padded.shape[2]
    windows = []
    for down_step in range(3):
        for side_step in range(3):
            windows.append(
                padded[down_step : down_step + height, side_step : side_step + breadth].reshape(
                    height * breadth, depth
                )
            )
    return jnp.concatenate(windows, axis=1)


def body(inputs, upstream, weight_in, weight_out, seam_link, seam_turn):
    cells = inputs[0, 0]
    height, breadth, width_in = cells.shape
    width_out = weight_out.shape[3]
    tiles = lax.axis_size("tile")
    place = lax.axis_index("tile")
    face_pos = lax.axis_index("face")
    link_row = lax.dynamic_index_in_dim(seam_link, face_pos, 0, False)
    turn_row = lax.dynamic_index_in_dim(seam_turn, face_pos, 0, False)
    maps = face_maps(tiles, height, breadth)
    unfolded_in = unfold(padded_tile(cells, maps, place, link_row, turn_row), height, breadth)
    pre_one = jnp.dot(
        unfolded_in, weight_in.reshape(-1, width_out), preferred_element_type=jnp.float32
    )
    act = gelu_value(pre_one).astype(jnp.bfloat16)
    padded_act = padded_tile(
        act.reshape(height, breadth, width_out), maps, place, link_row, turn_row
    )
    unfolded_act = unfold(padded_act, height, breadth)
    kernel_out = weight_out.reshape(-1, width_out)
    pre_two = jnp.dot(unfolded_act, kernel_out, preferred_element_type=jnp.float32)
    grad_two = (upstream[0, 0].reshape(-1, width_out) * gelu_slope(pre_two)).astype(jnp.bfloat16)
    grad_w_out = lax.dot_general(
        unfolded_act, grad_two, (((0,), (0,)), ((), ())), preferred_element_type=jnp.float32
    )
    spread = lax.dot_general(
        grad_two, kernel_out, (((1,), (1,)), ((), ())), preferred_element_type=jnp.float32
    )
    frame = jnp.zeros((height + 2, breadth + 2, width_out), jnp.float32)
    for down_step in range(3):
        for side_step in range(3):
            offset = (down_step * 3 + side_step) * width_out
            piece = spread[:, offset : offset + width_out].reshape(height, breadth, width_out)
            frame = frame + jnp.pad(
                piece, ((down_step, 2 - down_step), (side_step, 2 - side_step), (0, 0))
            )
    own_rim = return_border(border_of(frame), maps, place, link_row, turn_row)
    _, rim_back = jax.vjp(rim_of, jnp.zeros((height, breadth, width_out), jnp.float32))
    (rim_add,) = rim_back(own_rim)
    grad_act = frame[1:-1, 1:-1] + rim_add
    grad_one = (grad_act * gelu_slope(pre_one.reshape(height, breadth, width_out))).astype(
        jnp.bfloat16
    )
    grad_w_in = lax.dot_general(
        unfolded_in,
        grad_one.reshape(-1, width_out),
        (((0,), (0,)), ((), ())),
        preferred_element_type=jnp.float32,
    )
    size_in = grad_w_in.shape[0]
    total = lax.psum(jnp.concatenate([grad_w_in, grad_w_out], axis=0), ("face", "tile"))
    factor = lax.rsqrt(jnp.sum(total * total) / total.size + epsilon)
    update = (total * factor).astype(jnp.bfloat16)
    update_in = update[:size_in].reshape(3, 3, width_in, width_out)
    update_out = update[size_in:].reshape(3, 3, width_out, width_out)
    return (grad_one[None, None], update_in, update_out)


def solution(mesh):
    placed = (
        P("face", "tile", None, None, None),
        P("face", "tile", None, None, None),
        P(),
        P(),
        P(),
        P(),
    )
    return jax.shard_map(
        body,
        mesh=mesh,
        in_specs=placed,
        out_specs=(P("face", "tile", None, None, None), P(), P()),
        check_vma=False,
    )
```

time: 523 us -> 330 us (0.63)
  waiting for transfers between devices: 384 us -> 175 us
  blocking collectives: 46.6 us -> 78.5 us
  local copies, waits for them, and re-layouts: 45.5 us -> 21.9 us
  other arithmetic: 17.2 us -> 25.8 us
    psum x2 -> x1, waiting for transfers between devices: 280 us -> 175 us  [body(): lax.psum(jnp.concatenate([grad_w_in, grad_w_out], axis=0), ('face', 'tile'))]
    all_gather x2 -> x0, waiting for transfers between devices: 103 us -> none  [the longest x1 52.9 us: body(): borders = lax.all_gather(border_of(frame), both, axis=0, tiled=True)]
    all_gather x1 -> x6, blocking collectives: 46.6 us -> 78.5 us  [the longest x2 30.2 us: padded_tile(): rims = lax.all_gather(rim_of(cells), 'tile', axis=0, tiled=True)]
    gather x5 -> x3, local copies, waits for them, and re-layouts: 30.9 us -> 5.25 us  [halo_lookup(): picked = jnp.take(flattened, link_row, axis=0)]
    select_n x5 -> x8, other arithmetic: 0.88 us -> 7.01 us  [the longest x4 4.07 us: halo_lookup(): picked = jnp.take(flattened, link_row, axis=0)]
  transfers between devices with their start and end apart: 4 -> 1, of which waited for: 4 -> 1; matrix products, arithmetic and copies ran while one was open for 3% -> 0% of each run, Pallas kernels for 0% -> 0%
where the time goes in v2:
time: 330 us; the launch traced here: 328 us
  waiting for transfers between devices  175 us (53%)
  blocking collectives  78.5 us (24%)
  other arithmetic  25.8 us (8%)
  local copies, waits for them, and re-layouts  21.9 us (7%)
  between operations  15.3 us (5%)
  matrix products  12.1 us (4%)
    psum x1, waiting for transfers between devices, body(): lax.psum(jnp.concatenate([grad_w_in, grad_w_out], axis=0), ('face', 'tile'))  175 us
    all_gather x2, blocking collectives, padded_tile(): rims = lax.all_gather(rim_of(cells), 'tile', axis=0, tiled=True)  30.2 us
    all_gather x2, blocking collectives, padded_tile(): lax.all_gather(edges.reshape(1, 4, side, depth), 'face', axis=0, tiled=True)  19.1 us
    all_gather x1, blocking collectives, return_border(): borders = lax.all_gather(border, 'tile', axis=0, tiled=True)  16.4 us
    all_gather x1, blocking collectives, return_border(): lax.all_gather(seam_sum.reshape(1, 4, side, depth), 'face', axis=0, tiled...  12.8 us
  transfers between devices with their start and end apart: 1, of which 1 were waited for; matrix products, arithmetic and copies ran while one was open for 0% of the time, Pallas kernels for 0%

profile of v2, /device:TPU:0, one launch (start us, length us, event | category | flops | bytes accessed | tf_op | source)
XLA Modules:
  0.0 328.3 jit_solution(3603432614913608665)
XLA Ops:
  7.2 0.0 all-reduce.15.cloned.1.call-start
  7.2 0.8 compare_and_fusion
  8.1 0.7 fusion.47
  8.8 0.7 compare_bitcast_fusion
  9.5 0.7 slice_bitcast_fusion.9
  10.2 0.8 fusion.69
  11.0 15.9 %all_gather.18 = bf16[384,192]{1,0:T(8,128)(2,1)S(1)} all-gather(bf16[48,192]{1,0:T(8,128)(2,1)S(1)} %pad_maximum_fusion.8), channel_id=1, replica_groups=mesh['face'=4,'tile'=8] {'tile'}, dimensions={0}, use_global_device_ids=true | all-gather | bytes 165888 | tf_op jit(solution)/shard_map/all_gather | solution.py:89
  26.9 0.9 convolution_convert_fusion.1
  27.9 0.1 copy.44
  28.0 9.0 %all_gather.19 = bf16[4,4,32,192]{3,2,1,0:T(8,128)(2,1)S(1)} all-gather(bf16[1,4,32,192]{3,2,1,0:T(8,128)(2,1)S(1)} %bitcast.161), channel_id=1, replica_groups=mesh['face'=4,'tile'=8] {'face'}, dimensions={0}, use_global_device_ids=true | all-gather | bytes 245760 | tf_op jit(solution)/shard_map/all_gather | solution.py:95
  37.0 0.6 gather_fusion
  37.5 0.1 broadcast_select_fusion.4
  37.6 0.1 rev.9
  37.7 0.1 broadcast_select_fusion.5
  37.8 0.7 compare_select_fusion.2
  38.5 0.2 convolution_convert_fusion.3
  38.8 1.0 pad_maximum_fusion.5
  39.8 1.0 pad_maximum_fusion.2
  40.8 0.7 fusion.65
  41.5 1.1 concatenate.71
  42.7 2.6 multiply_convert_fusion.1
  45.3 14.3 %all_gather.20 = bf16[384,384]{1,0:T(8,128)(2,1)S(1)} all-gather(bf16[48,384]{1,0:T(8,128)(2,1)S(1)} %pad_maximum_fusion.7), channel_id=1, replica_groups=mesh['face'=4,'tile'=8] {'tile'}, dimensions={0}, use_global_device_ids=true | all-gather | bytes 331776 | tf_op jit(solution)/shard_map/all_gather | solution.py:89
  59.6 0.3 convolution_convert_fusion
  59.9 10.1 %all_gather.21 = bf16[4,4,32,384]{3,2,1,0:T(8,128)(2,1)} all-gather(bf16[1,4,32,384]{3,2,1,0:T(8,128)(2,1)S(1)} %bitcast.160), channel_id=1, replica_groups=mesh['face'=4,'tile'=8] {'face'}, dimensions={0}, use_global_device_ids=true | all-gather | bytes 491520 | tf_op jit(solution)/shard_map/all_gather | solution.py:95
  70.1 2.2 gather_fusion.1
  72.2 1.6 broadcast_select_fusion.1
  73.9 2.2 rev.10
  76.0 1.0 broadcast_select_fusion.3
  77.1 0.2 convolution_convert_fusion.2
  77.4 0.1 pad_maximum_fusion.3
  77.5 0.1 pad_maximum_fusion.1
  77.6 0.1 fusion.62
  77.6 0.1 fusion.63
  77.8 0.9 constant_dynamic-update-slice_fusion.4
  78.8 0.6 fusion.70
  79.5 0.9 fusion.21
  80.4 0.1 fusion.60
  80.6 0.2 pad_add_fusion
  80.8 0.7 fusion.61
  81.4 0.1 copy-done.5
  81.5 0.6 slice_bitcast_fusion.1
  82.1 0.5 iota_add_fusion
  82.7 0.7 copy.68
  83.4 0.8 maximum_bitcast_fusion
  84.2 16.4 %all-gather = f32[8,52,384]{2,1,0:T(8,128)} all-gather(f32[1,52,384]{2,1,0:T(8,128)S(1)} %maximum_bitcast_fusion), channel_id=1, replica_groups=mesh['face'=4,'tile'=8] {'tile'}, dimensions={0}, use_global_device_ids=true | all-gather | bytes 718848 | tf_op jit(solution)/shard_map/all_gather | solution.py:121
  100.5 2.0 reshape.280
  102.6 1.5 fusion.6
  104.1 12.8 %all_gather.23 = f32[4,4,32,384]{3,2,1,0:T(8,128)} all-gather(f32[1,4,32,384]{3,2,1,0:T(8,128)S(1)} %bitcast.144), channel_id=1, replica_groups=mesh['face'=4,'tile'=8] {'face'}, dimensions={0}, use_global_device_ids=true | all-gather | bytes 983040 | tf_op jit(solution)/shard_map/all_gather | solution.py:127
  116.9 2.5 gather_fusion.2
  119.4 1.7 broadcast_select_fusion
  121.1 2.4 rev.11
  123.4 1.1 broadcast_select_fusion.2
  124.6 1.5 fusion.36
  126.0 0.8 convolution_add_fusion
  126.9 2.0 fusion.19
  129.0 0.1 fusion.18
  129.1 0.5 fusion.71
  129.7 3.6 %pad_maximum_fusion = f32[5184,384]{1,0:T(8,128)} fusion(f32[3456,384]{1,0:T(8,128)S(1)} %fusion.19, f32[1728,384]{1,0:T(8,128)S(1)} %fusion.71), kind=kLoop, calls=%fused_computation.3 | loop fusion | flops 1990656 | bytes 15925248 | tf_op jit(solution)/shard_map/concatenate | solution.py:202
  133.3 0.0 all-reduce.15.cloned.1.call-update
  133.3 174.8 %all-reduce.15.cloned.1.call-done = f32[5184,384]{1,0:T(8,128)} async-done(((f32[5184,384]{1,0:T(8,128)}), f32[5184,384]{1,0:T(8,128)}) %all-reduce.15.cloned.1.call-update) | async-done | bytes 7962640 | tf_op jit(solution)/shard_map/psum | solution.py:202
  308.0 5.9 %multiply_reduce_fusion = f32[]{:T(128)} fusion(f32[5184,384]{1,0:T(8,128)} %all-reduce.15.cloned.1.call-done), kind=kLoop, calls=%fused_computation.5 | loop fusion | flops 3981311 | bytes 7962628 | tf_op jit(solution)/shard_map/reduce_sum | solution.py:203
  314.7 3.9 %multiply_convert_fusion = bf16[5184,384]{1,0:T(8,128)(2,1)S(1)} fusion(f32[5184,384]{1,0:T(8,128)} %all-reduce.15.cloned.1.call-done, f32[]{:T(128)S(6)} %rsqrt.3), kind=kLoop, calls=%fused_computation.4 | loop fusion | flops 3981312 | bytes 11943940 | tf_op jit(solution)/shard_map/convert_element_type | solution.py:204
  318.5 1.2 slice.258
  319.7 1.8 slice.259
  (63 shorter events, 0.4 us)
Async XLA Ops:
  7.2 71.7 %copy-start = (bf16[3,3,384,384]{3,2,1,0:T(8,128)(2,1)S(1)}, bf16[3,3,384,384]{3,2,1,0:T(8,128)(2,1)}, u32[]{:S(2)}) copy-start(bf16[3,3,384,384]{3,2,1,0:T(8,128)(2,1)} %param.14) | copy-start | bytes 7962628
  7.2 34.4 %copy-start.7 = (bf16[1,1,8,16,192]{4,3,2,1,0:T(8,128)(2,1)S(1)}, bf16[1,1,8,16,192]{4,3,2,1,0:T(8,128)(2,1)}, u32[]{:S(2)}) copy-start(bf16[1,1,8,16,192]{4,3,2,1,0:T(8,128)(2,1)} %param.11) | copy-start | bytes 147460
  7.2 300.9 %all-reduce.15.cloned.1.call-start = ((), (), s32[]{:S(2)}) async-start(), calls=%async_computation | async-start | bytes 15925248 | tf_op jit(solution)/shard_map/psum | solution.py:202
  9.5 66.6 %copy-start.14 = (pred[4]{0:T(512)(128)(4,1)}, pred[4]{0:T(512)(128)(4,1)S(1)}, u32[]{:S(2)}) copy-start(pred[4]{0:T(512)(128)(4,1)S(1)} %compare_bitcast_fusion) | copy-start | bytes 16
  9.5 60.6 %copy-start.11 = (s32[1024]{0:T(1024)}, s32[1024]{0:T(1024)S(1)}, u32[]{:S(2)}) copy-start(s32[1024]{0:T(1024)S(1)} %pad_clamp_fusion) | copy-start | bytes 12292
  38.7 20.9 %copy-start.12 = (s32[128]{0:T(128)S(1)}, s32[128]{0:T(128)}, u32[]{:S(2)}) copy-start(s32[128]{0:T(128)} %constant.110.clone) | copy-start | bytes 1540
  42.6 34.8 %copy-start.1 = (bf16[128,1728]{1,0:T(8,128)(2,1)}, bf16[128,1728]{1,0:T(8,128)(2,1)S(1)}, u32[]{:S(2)}) copy-start(bf16[128,1728]{1,0:T(8,128)(2,1)S(1)} %concatenate.71) | copy-start | bytes 1327108
  45.2 32.5 %copy-start.3 = (bf16[128,384]{1,0:T(8,128)(2,1)}, bf16[128,384]{1,0:T(8,128)(2,1)S(1)}, u32[]{:S(2)}) copy-start(bf16[128,384]{1,0:T(8,128)(2,1)S(1)} %get-tuple-element.56) | copy-start | bytes 294916
  77.7 1.8 copy-start.9
  79.5 1.1 copy-start.4
  80.8 0.7 copy-start.5
  83.4 40.1 %copy-start.15 = (pred[4]{0:T(512)(128)(4,1)S(1)}, pred[4]{0:T(512)(128)(4,1)}, u32[]{:S(2)}) copy-start(pred[4]{0:T(512)(128)(4,1)} %copy-done.14) | copy-start | bytes 16
  100.5 24.0 %copy-start.16 = (s32[416]{0:T(512)S(1)}, s32[416]{0:T(512)}, u32[]{:S(2)}) copy-start(s32[416]{0:T(512)} %constant.114.clone) | copy-start | bytes 4996
  100.5 25.5 %copy-start.13 = (s32[128]{0:T(128)S(1)}, s32[128]{0:T(128)}, u32[]{:S(2)}) copy-start(s32[128]{0:T(128)} %constant.110.clone) | copy-start | bytes 1540
  126.9 2.0 copy-start.6
  126.9 2.0 copy-start.8
  126.9 2.2 copy-start.2
  129.1 4.2 %copy-start.10 = (bf16[8,16,384]{2,1,0:T(8,128)(2,1)}, bf16[8,16,384]{2,1,0:T(8,128)(2,1)S(1)}, u32[]{:S(2)}) copy-start(bf16[8,16,384]{2,1,0:T(8,128)(2,1)S(1)} %fusion.18) | copy-start | bytes 294916
Sparse Core Ops, SparseCore 0:
  133.4 174.5 all-reduce.14

commit v3 on v2

--- a/solution.py
+++ b/solution.py
@@ -199,7 +199,8 @@
         preferred_element_type=jnp.float32,
     )
     size_in = grad_w_in.shape[0]
-    total = lax.psum(jnp.concatenate([grad_w_in, grad_w_out], axis=0), ("face", "tile"))
+    partial = jnp.concatenate([grad_w_in, grad_w_out], axis=0).astype(jnp.bfloat16)
+    total = lax.psum(partial, ("face", "tile")).astype(jnp.float32)
     factor = lax.rsqrt(jnp.sum(total * total) / total.size + epsilon)
     update = (total * factor).astype(jnp.bfloat16)
     update_in = update[:size_in].reshape(3, 3, width_in, width_out)

time: 330 us -> 287 us (0.87)
  waiting for transfers between devices: 175 us -> 141 us
  other arithmetic: 25.8 us -> 21.3 us
    psum x1, waiting for transfers between devices: 175 us -> 141 us  [body(): total = lax.psum(partial, ('face', 'tile')).astype(jnp.float32)]
where the time goes in v3:
time: 287 us; the launch traced here: 286 us
  waiting for transfers between devices  141 us (49%)
  blocking collectives  78.5 us (27%)
  other arithmetic  21.3 us (7%)
  local copies, waits for them, and re-layouts  18.7 us (7%)
  between operations  15.3 us (5%)
  matrix products  10.8 us (4%)
    psum x1, waiting for transfers between devices, body(): total = lax.psum(partial, ('face', 'tile')).astype(jnp.float32)  141 us
    all_gather x2, blocking collectives, padded_tile(): rims = lax.all_gather(rim_of(cells), 'tile', axis=0, tiled=True)  30.2 us
    all_gather x2, blocking collectives, padded_tile(): lax.all_gather(edges.reshape(1, 4, side, depth), 'face', axis=0, tiled=True)  19.1 us
    all_gather x1, blocking collectives, return_border(): borders = lax.all_gather(border, 'tile', axis=0, tiled=True)  16.4 us
    all_gather x1, blocking collectives, return_border(): lax.all_gather(seam_sum.reshape(1, 4, side, depth), 'face', axis=0, tiled...  12.8 us
  transfers between devices with their start and end apart: 1, of which 1 were waited for; matrix products, arithmetic and copies ran while one was open for 0% of the time, Pallas kernels for 0%

profile of v3, /device:TPU:0, one launch (start us, length us, event | category | flops | bytes accessed | tf_op | source)
XLA Modules:
  0.0 286.0 jit_solution(12245970750825822959)
XLA Ops:
  7.2 0.0 copy-start
  7.2 0.0 all-reduce.15.cloned.1.call-start
  7.2 0.8 compare_and_fusion
  8.1 0.7 fusion.48
  8.8 0.7 compare_bitcast_fusion
  9.5 0.7 slice_bitcast_fusion.9
  10.2 0.8 fusion.70
  11.0 15.9 %all_gather.18 = bf16[384,192]{1,0:T(8,128)(2,1)S(1)} all-gather(bf16[48,192]{1,0:T(8,128)(2,1)S(1)} %pad_maximum_fusion.8), channel_id=1, replica_groups=mesh['face'=4,'tile'=8] {'tile'}, dimensions={0}, use_global_device_ids=true | all-gather | bytes 165888 | tf_op jit(solution)/shard_map/all_gather | solution.py:89
  26.9 0.9 convolution_convert_fusion.3
  27.8 0.1 copy.44
  27.9 9.0 %all_gather.19 = bf16[4,4,32,192]{3,2,1,0:T(8,128)(2,1)S(1)} all-gather(bf16[1,4,32,192]{3,2,1,0:T(8,128)(2,1)S(1)} %bitcast.161), channel_id=1, replica_groups=mesh['face'=4,'tile'=8] {'face'}, dimensions={0}, use_global_device_ids=true | all-gather | bytes 245760 | tf_op jit(solution)/shard_map/all_gather | solution.py:95
  36.9 0.6 gather_fusion
  37.5 0.1 broadcast_select_fusion.4
  37.6 0.1 rev.9
  37.7 0.1 broadcast_select_fusion.5
  37.8 0.7 compare_select_fusion.2
  38.5 0.6 copy-done.10
  39.1 0.2 convolution_convert_fusion.5
  39.3 0.0 copy-start.7
  39.3 1.0 pad_maximum_fusion.5
  40.3 1.0 pad_maximum_fusion.2
  41.4 0.7 fusion.66
  42.1 1.1 concatenate.72
  43.2 0.0 copy-start.2
  43.2 2.6 multiply_convert_fusion
  45.9 14.3 %all_gather.20 = bf16[384,384]{1,0:T(8,128)(2,1)S(1)} all-gather(bf16[48,384]{1,0:T(8,128)(2,1)S(1)} %pad_maximum_fusion.7), channel_id=1, replica_groups=mesh['face'=4,'tile'=8] {'tile'}, dimensions={0}, use_global_device_ids=true | all-gather | bytes 331776 | tf_op jit(solution)/shard_map/all_gather | solution.py:89
  60.2 0.3 convolution_convert_fusion.2
  60.5 10.1 %all_gather.21 = bf16[4,4,32,384]{3,2,1,0:T(8,128)(2,1)} all-gather(bf16[1,4,32,384]{3,2,1,0:T(8,128)(2,1)S(1)} %bitcast.160), channel_id=1, replica_groups=mesh['face'=4,'tile'=8] {'face'}, dimensions={0}, use_global_device_ids=true | all-gather | bytes 491520 | tf_op jit(solution)/shard_map/all_gather | solution.py:95
  70.6 2.2 gather_fusion.1
  72.8 1.6 broadcast_select_fusion.1
  74.4 2.2 rev.10
  76.6 1.0 broadcast_select_fusion.3
  77.7 0.2 convolution_convert_fusion.4
  78.0 0.1 pad_maximum_fusion.3
  78.1 0.1 pad_maximum_fusion.1
  78.2 0.1 fusion.63
  78.2 0.1 fusion.64
  78.5 0.6 fusion.71
  79.2 0.0 copy-done.5
  79.2 2.4 convolution_convert_fusion
  81.6 0.9 fusion.22
  82.5 0.1 fusion.61
  82.7 0.0 copy-start.9
  82.7 0.2 pad_add_fusion
  82.9 0.7 copy-done.3
  83.7 16.4 %all-gather = f32[8,52,384]{2,1,0:T(8,128)} all-gather(f32[1,52,384]{2,1,0:T(8,128)S(1)} %maximum_bitcast_fusion), channel_id=1, replica_groups=mesh['face'=4,'tile'=8] {'tile'}, dimensions={0}, use_global_device_ids=true | all-gather | bytes 718848 | tf_op jit(solution)/shard_map/all_gather | solution.py:121
  100.0 1.2 reshape.280
  101.2 0.5 fusion.8
  101.7 12.8 %all_gather.23 = f32[4,4,32,384]{3,2,1,0:T(8,128)} all-gather(f32[1,4,32,384]{3,2,1,0:T(8,128)S(1)} %bitcast.144), channel_id=1, replica_groups=mesh['face'=4,'tile'=8] {'face'}, dimensions={0}, use_global_device_ids=true | all-gather | bytes 983040 | tf_op jit(solution)/shard_map/all_gather | solution.py:127
  114.4 1.7 gather_fusion.2
  116.1 0.8 broadcast_select_fusion
  116.9 2.4 rev.11
  119.3 1.2 broadcast_select_fusion.2
  120.5 0.4 fusion.37
  120.9 0.2 convolution_add_fusion
  121.2 1.2 fusion.20
  122.4 1.6 convolution_convert_fusion.1
  124.0 2.3 pad_maximum_fusion
  126.3 0.0 all-reduce.15.cloned.1.call-update
  126.3 141.5 %all-reduce.15.cloned.1.call-done = bf16[5184,384]{1,0:T(8,128)(2,1)} async-done(((bf16[5184,384]{1,0:T(8,128)(2,1)}), bf16[5184,384]{1,0:T(8,128)(2,1)}) %all-reduce.15.cloned.1.call-update) | async-done | bytes 3981328 | tf_op jit(solution)/shard_map/psum | solution.py:203
  267.8 4.8 %fusion = f32[]{:T(128)} fusion(bf16[5184,384]{1,0:T(8,128)(2,1)} %all-reduce.15.cloned.1.call-done), kind=kLoop, calls=%fused_computation.5 | loop fusion | flops 5971967 | bytes 3981316 | tf_op jit(solution)/shard_map/reduce_sum | solution.py:204
  273.3 2.9 %fusion.1 = bf16[5184,384]{1,0:T(8,128)(2,1)S(1)} fusion(bf16[5184,384]{1,0:T(8,128)(2,1)} %all-reduce.15.cloned.1.call-done, f32[]{:T(128)S(6)} %rsqrt.3), kind=kLoop, calls=%fused_computation.6 | loop fusion | flops 5971968 | bytes 7962628 | tf_op jit(solution)/shard_map/convert_element_type | solution.py:205
  276.2 1.2 slice.258
  277.4 1.8 slice.259
  (53 shorter events, 0.5 us)
Async XLA Ops:
  7.2 71.4 %copy-start = (bf16[3,3,384,384]{3,2,1,0:T(8,128)(2,1)S(1)}, bf16[3,3,384,384]{3,2,1,0:T(8,128)(2,1)}, u32[]{:S(2)}) copy-start(bf16[3,3,384,384]{3,2,1,0:T(8,128)(2,1)} %param.14) | copy-start | bytes 7962628
  7.2 34.9 %copy-start.4 = (bf16[1,1,8,16,192]{4,3,2,1,0:T(8,128)(2,1)S(1)}, bf16[1,1,8,16,192]{4,3,2,1,0:T(8,128)(2,1)}, u32[]{:S(2)}) copy-start(bf16[1,1,8,16,192]{4,3,2,1,0:T(8,128)(2,1)} %param.11) | copy-start | bytes 147460
  7.2 260.6 %all-reduce.15.cloned.1.call-start = ((), (), s32[]{:S(2)}) async-start(), calls=%async_computation | async-start | bytes 7962624 | tf_op jit(solution)/shard_map/psum | solution.py:203
  38.5 0.6 copy-start.10
  39.3 20.9 %copy-start.7 = (s32[128]{0:T(128)S(1)}, s32[128]{0:T(128)}, u32[]{:S(2)}) copy-start(s32[128]{0:T(128)} %constant.110.clone) | copy-start | bytes 1540
  43.2 34.9 %copy-start.2 = (bf16[128,1728]{1,0:T(8,128)(2,1)}, bf16[128,1728]{1,0:T(8,128)(2,1)S(1)}, u32[]{:S(2)}) copy-start(bf16[128,1728]{1,0:T(8,128)(2,1)S(1)} %concatenate.72) | copy-start | bytes 1327108
  43.2 34.4 %copy-start.11 = (s32[52]{0:T(128)S(1)}, s32[52]{0:T(128)}, u32[]{:S(2)}) copy-start(s32[52]{0:T(128)} %copy-done.10) | copy-start | bytes 628
  78.3 0.9 copy-start.5
  82.7 18.5 %copy-start.9 = (s32[416]{0:T(512)S(1)}, s32[416]{0:T(512)}, u32[]{:S(2)}) copy-start(s32[416]{0:T(512)} %constant.113.clone) | copy-start | bytes 4996
  82.9 0.7 copy-start.3
  100.0 20.5 %copy-start.8 = (s32[416]{0:T(512)S(1)}, s32[416]{0:T(512)}, u32[]{:S(2)}) copy-start(s32[416]{0:T(512)} %constant.114.clone) | copy-start | bytes 4996
  119.3 4.7 %copy-start.1 = (bf16[3456,384]{1,0:T(8,128)(2,1)S(1)}, bf16[3456,384]{1,0:T(8,128)(2,1)}, u32[]{:S(2)}) copy-start(bf16[3456,384]{1,0:T(8,128)(2,1)} %convolution_convert_fusion) | copy-start | bytes 7962628
  122.4 3.9 %copy-start.6 = (bf16[8,16,384]{2,1,0:T(8,128)(2,1)}, bf16[8,16,384]{2,1,0:T(8,128)(2,1)S(1)}, u32[]{:S(2)}) copy-start(bf16[8,16,384]{2,1,0:T(8,128)(2,1)S(1)} %fusion.20) | copy-start | bytes 294916
Sparse Core Ops, SparseCore 0:
  126.5 141.2 all-reduce.14

commit v4 on v2

--- a/solution.py
+++ b/solution.py
@@ -149,6 +149,19 @@
     return jnp.concatenate(windows, axis=1)
 
 
+def weight_slice(padded, grads, tiles):
+    rows, cols, depth = padded.shape
+    part = depth // tiles
+    pieces = padded.reshape(rows, cols, tiles, part).transpose(2, 0, 1, 3)
+    mine = lax.all_to_all(pieces, "tile", 0, 0, tiled=True)
+    every_grad = lax.all_gather(grads, "tile", axis=0, tiled=True)
+    windows = jax.vmap(lambda one: unfold(one, rows - 2, cols - 2))(mine)
+    windows = windows.reshape(-1, windows.shape[-1])
+    return lax.dot_general(
+        windows, every_grad, (((0,), (0,)), ((), ())), preferred_element_type=jnp.float32
+    )
+
+
 def body(inputs, upstream, weight_in, weight_out, seam_link, seam_turn):
     cells = inputs[0, 0]
     height, breadth, width_in = cells.shape
@@ -159,7 +172,8 @@
     link_row = lax.dynamic_index_in_dim(seam_link, face_pos, 0, False)
     turn_row = lax.dynamic_index_in_dim(seam_turn, face_pos, 0, False)
     maps = face_maps(tiles, height, breadth)
-    unfolded_in = unfold(padded_tile(cells, maps, place, link_row, turn_row), height, breadth)
+    padded_tile_in = padded_tile(cells, maps, place, link_row, turn_row)
+    unfolded_in = unfold(padded_tile_in, height, breadth)
     pre_one = jnp.dot(
         unfolded_in, weight_in.reshape(-1, width_out), preferred_element_type=jnp.float32
     )
@@ -171,9 +185,6 @@
     kernel_out = weight_out.reshape(-1, width_out)
     pre_two = jnp.dot(unfolded_act, kernel_out, preferred_element_type=jnp.float32)
     grad_two = (upstream[0, 0].reshape(-1, width_out) * gelu_slope(pre_two)).astype(jnp.bfloat16)
-    grad_w_out = lax.dot_general(
-        unfolded_act, grad_two, (((0,), (0,)), ((), ())), preferred_element_type=jnp.float32
-    )
     spread = lax.dot_general(
         grad_two, kernel_out, (((1,), (1,)), ((), ())), preferred_element_type=jnp.float32
     )
@@ -192,18 +203,19 @@
     grad_one = (grad_act * gelu_slope(pre_one.reshape(height, breadth, width_out))).astype(
         jnp.bfloat16
     )
-    grad_w_in = lax.dot_general(
-        unfolded_in,
-        grad_one.reshape(-1, width_out),
-        (((0,), (0,)), ((), ())),
-        preferred_element_type=jnp.float32,
-    )
-    size_in = grad_w_in.shape[0]
-    total = lax.psum(jnp.concatenate([grad_w_in, grad_w_out], axis=0), ("face", "tile"))
-    factor = lax.rsqrt(jnp.sum(total * total) / total.size + epsilon)
-    update = (total * factor).astype(jnp.bfloat16)
-    update_in = update[:size_in].reshape(3, 3, width_in, width_out)
-    update_out = update[size_in:].reshape(3, 3, width_out, width_out)
+    tile_in = weight_slice(padded_tile_in, grad_one.reshape(-1, width_out), tiles)
+    tile_out = weight_slice(padded_act, grad_two, tiles)
+    size_in = tile_in.shape[0]
+    face_sum = lax.psum(jnp.concatenate([tile_in, tile_out], axis=0), "face")
+    total = lax.all_gather(face_sum, "tile", axis=0, tiled=False)
+    total_in = total[:, :size_in].reshape(tiles, 9, width_in // tiles, width_out)
+    total_out = total[:, size_in:].reshape(tiles, 9, width_out // tiles, width_out)
+    total_in = total_in.transpose(1, 0, 2, 3)
+    total_out = total_out.transpose(1, 0, 2, 3)
+    squares = jnp.sum(total_in * total_in) + jnp.sum(total_out * total_out)
+    factor = lax.rsqrt(squares / (total_in.size + total_out.size) + epsilon)
+    update_in = (total_in * factor).astype(jnp.bfloat16).reshape(3, 3, width_in, width_out)
+    update_out = (total_out * factor).astype(jnp.bfloat16).reshape(3, 3, width_out, width_out)
     return (grad_one[None, None], update_in, update_out)
 
 

time: 330 us -> 359 us (1.088)
  waiting for transfers between devices: 175 us -> 133 us
  blocking collectives: 78.5 us -> 111 us
  local copies, waits for them, and re-layouts: 21.9 us -> 52.4 us
  starting transfers between devices: 0.04 us -> 9.83 us
  other arithmetic: 25.8 us -> 21.9 us
    psum x1, waiting for transfers between devices: 175 us -> 52.2 us  [body(): face_sum = lax.psum(jnp.concatenate([tile_in, tile_out], axis=0), 'face')]
    all_gather x0 -> x1, waiting for transfers between devices: none -> 80.4 us  [body(): total = lax.all_gather(face_sum, 'tile', axis=0, tiled=False)]
    all_gather x0 -> x2, blocking collectives: none -> 33.2 us  [weight_slice(): every_grad = lax.all_gather(grads, 'tile', axis=0, tiled=True)]
    concatenate x2 -> x13, local copies, waits for them, and re-layouts: 1.12 us -> 19 us  [unfold(): return jnp.concatenate(windows, axis=1)]
    unnamed x48, local copies, waits for them, and re-layouts: 3.94 us -> 13.5 us
    all_to_all x0 -> x2, starting transfers between devices: none -> 9.57 us  [weight_slice(): mine = lax.all_to_all(pieces, 'tile', 0, 0, tiled=True)]
    concatenate x0 -> x16, local copies, waits for them, and re-layouts: none -> 5.13 us  [the longest x9 4.04 us: padded_tile(): jnp.concatenate([left_side[:, None], cells, right_side[:, None]], axis=1)]
    slice x4 -> x13, local copies, waits for them, and re-layouts: 0.83 us -> 5.09 us  [unfold(): padded[down_step:down_step + height, side_step:side_step + breadth]]
  transfers between devices with their start and end apart: 1 -> 4, of which waited for: 1 -> 2; matrix products, arithmetic and copies ran while one was open for 0% -> 14% of each run, Pallas kernels for 0% -> 0%
where the time goes in v4:
time: 359 us; the launch traced here: 357 us
  waiting for transfers between devices  133 us (37%)
  blocking collectives  111 us (31%)
  local copies, waits for them, and re-layouts  52.4 us (15%)
  other arithmetic  21.9 us (6%)
  between operations  16.1 us (4%)
  matrix products  12.6 us (4%)
  starting transfers between devices  9.83 us (3%)
    all_gather x1, waiting for transfers between devices, body(): total = lax.all_gather(face_sum, 'tile', axis=0, tiled=False)  80.4 us
    psum x1, waiting for transfers between devices, body(): face_sum = lax.psum(jnp.concatenate([tile_in, tile_out], axis=0), 'face')  52.2 us
    all_gather x2, blocking collectives, weight_slice(): every_grad = lax.all_gather(grads, 'tile', axis=0, tiled=True)  33.2 us
    all_gather x2, blocking collectives, padded_tile(): rims = lax.all_gather(rim_of(cells), 'tile', axis=0, tiled=True)  30.7 us
    concatenate x13, local copies, waits for them, and re-layouts, unfold(): return jnp.concatenate(windows, axis=1)  19 us
    all_gather x2, blocking collectives, padded_tile(): lax.all_gather(edges.reshape(1, 4, side, depth), 'face', axis=0, tiled=True)  18.5 us
    all_gather x1, blocking collectives, return_border(): borders = lax.all_gather(border, 'tile', axis=0, tiled=True)  16.3 us
    unnamed x48, local copies, waits for them, and re-layouts  13.5 us
  transfers between devices with their start and end apart: 4, of which 2 were waited for; matrix products, arithmetic and copies ran while one was open for 14% of the time, Pallas kernels for 0%

profile of v4, /device:TPU:0, one launch (start us, length us, event | category | flops | bytes accessed | tf_op | source)
XLA Modules:
  0.0 356.9 jit_solution(5357735208790200516)
XLA Ops:
  7.2 0.8 compare_and_fusion
  9.4 0.9 copy.139
  11.0 15.9 %all_gather.30 = bf16[384,192]{1,0:T(8,128)(2,1)S(1)} all-gather(bf16[48,192]{1,0:T(8,128)(2,1)S(1)} %pad_maximum_fusion.8), channel_id=1, replica_groups=mesh['face'=4,'tile'=8] {'tile'}, dimensions={0}, use_global_device_ids=true | all-gather | bytes 165888 | tf_op jit(solution)/shard_map/all_gather | solution.py:89
  26.9 0.9 convolution_convert_fusion.1
  28.0 9.0 %all_gather.31 = bf16[4,4,32,192]{3,2,1,0:T(8,128)(2,1)S(1)} all-gather(bf16[1,4,32,192]{3,2,1,0:T(8,128)(2,1)S(1)} %bitcast.220), channel_id=1, replica_groups=mesh['face'=4,'tile'=8] {'face'}, dimensions={0}, use_global_device_ids=true | all-gather | bytes 245760 | tf_op jit(solution)/shard_map/all_gather | solution.py:95
  38.8 1.1 concatenate.159
  40.5 1.0 reshape.373
  41.5 4.6 %all-to-all-start = ((bf16[8,2,2160]{2,1,0:T(2,128)(2,1)}), bf16[8,2,2160]{2,1,0:T(2,128)(2,1)}, u32[]{:S(2)}, u32[]{:S(2)}) async-start(bf16[8,2,2160]{2,1,0:T(2,128)(2,1)} %reshape.373), calls=%async_computation | async-start | bytes 139264 | tf_op jit(solution)/shard_map/all_to_all | solution.py:156
  48.4 1.1 concatenate.147
  49.5 2.4 multiply_convert_fusion.2
  51.9 0.9 concatenate.176
  52.9 14.8 %all_gather.32 = bf16[384,384]{1,0:T(8,128)(2,1)S(1)} all-gather(bf16[48,384]{1,0:T(8,128)(2,1)S(1)} %pad_maximum_fusion.7), channel_id=1, replica_groups=mesh['face'=4,'tile'=8] {'tile'}, dimensions={0}, use_global_device_ids=true | all-gather | bytes 331776 | tf_op jit(solution)/shard_map/all_gather | solution.py:89
  68.0 9.5 %all_gather.33 = bf16[4,4,32,384]{3,2,1,0:T(8,128)(2,1)S(1)} all-gather(bf16[1,4,32,384]{3,2,1,0:T(8,128)(2,1)S(1)} %bitcast.218), channel_id=1, replica_groups=mesh['face'=4,'tile'=8] {'face'}, dimensions={0}, use_global_device_ids=true | all-gather | bytes 491520 | tf_op jit(solution)/shard_map/all_gather | solution.py:95
  78.4 0.9 convolution_convert_fusion.2
  79.9 1.4 fusion.12
  81.2 0.9 fusion.19
  83.8 16.3 %all-gather = f32[8,52,384]{2,1,0:T(8,128)} all-gather(f32[1,52,384]{2,1,0:T(8,128)S(1)} %maximum_bitcast_fusion.2), channel_id=1, replica_groups=mesh['face'=4,'tile'=8] {'tile'}, dimensions={0}, use_global_device_ids=true | all-gather | bytes 718848 | tf_op jit(solution)/shard_map/all_gather | solution.py:121
  100.2 1.2 reshape.370
  101.8 12.8 %all_gather.35 = f32[4,4,32,384]{3,2,1,0:T(8,128)} all-gather(f32[1,4,32,384]{3,2,1,0:T(8,128)S(1)} %bitcast.200), channel_id=1, replica_groups=mesh['face'=4,'tile'=8] {'face'}, dimensions={0}, use_global_device_ids=true | all-gather | bytes 983040 | tf_op jit(solution)/shard_map/all_gather | solution.py:127
  114.6 1.7 gather_fusion.2
  116.3 0.8 broadcast_select_fusion
  117.0 2.4 rev.11
  119.4 1.0 broadcast_select_fusion.2
  120.4 1.1 fusion.29
  121.5 0.9 convolution_add_fusion
  122.4 1.0 copy.113
  125.1 16.6 %all_gather.37 = bf16[1024,384]{1,0:T(8,128)(2,1)} all-gather(bf16[128,384]{1,0:T(8,128)(2,1)} %get-tuple-element.84), channel_id=1, replica_groups=mesh['face'=4,'tile'=8] {'tile'}, dimensions={0}, use_global_device_ids=true | all-gather | bytes 884736 | tf_op jit(solution)/shard_map/all_gather | solution.py:157
  141.7 1.2 fusion.18
  142.9 16.6 %all_gather.36 = bf16[1024,384]{1,0:T(8,128)(2,1)} all-gather(bf16[128,384]{1,0:T(8,128)(2,1)S(1)} %bitcast.216), channel_id=1, replica_groups=mesh['face'=4,'tile'=8] {'tile'}, dimensions={0}, use_global_device_ids=true | all-gather | bytes 884736 | tf_op jit(solution)/shard_map/all_gather | solution.py:157
  159.5 1.1 maximum_bitcast_fusion.1
  160.6 1.2 reshape.371
  161.8 5.0 %all-to-all-start.1 = ((bf16[8,2,4320]{2,1,0:T(2,128)(2,1)}), bf16[8,2,4320]{2,1,0:T(2,128)(2,1)}, u32[]{:S(2)}, u32[]{:S(2)}) async-start(bf16[8,2,4320]{2,1,0:T(2,128)(2,1)} %reshape.371), calls=%async_computation.1 | async-start | bytes 278528 | tf_op jit(solution)/shard_map/all_to_all | solution.py:156
  166.9 1.3 reshape.374
  168.3 1.5 fusion.49
  169.8 1.1 copy.127
  170.9 1.1 copy.126
  172.0 1.7 copy.125
  173.7 1.7 copy.124
  175.3 1.7 copy.123
  177.0 1.7 copy.122
  178.7 1.7 copy.121
  180.4 1.7 copy.120
  182.0 1.7 copy.119
  183.7 0.8 constant_dynamic-update-slice_fusion.17
  184.5 0.8 constant_dynamic-update-slice_fusion.16
  185.3 0.8 constant_dynamic-update-slice_fusion.15
  186.1 0.8 constant_dynamic-update-slice_fusion.14
  186.9 0.8 constant_dynamic-update-slice_fusion.13
  187.7 0.8 constant_dynamic-update-slice_fusion.12
  188.5 0.8 constant_dynamic-update-slice_fusion.11
  189.4 1.1 fusion.63
  190.5 1.5 reshape.372
  192.0 1.5 fusion.50
  193.4 4.0 %concatenate.190 = bf16[1024,432]{1,0:T(8,128)(2,1)} concatenate(bf16[1024,48]{1,0:T(8,128)(2,1)} %bitcast.189, bf16[1024,48]{1,0:T(8,128)(2,1)} %bitcast.188, bf16[1024,48]{1,0:T(8,128)(2,1)} %bitcast.187, bf16[1024,48]{1,0:T(8,128)(2,1)} %bitcast.186, bf16[1024,48]{1,0:T(8,128)(2,1)} %bitcast.185, bf16[1024,48]{1,0:T(8,128)(2,1)} %bitcast.184, bf16[1024,48]{1,0:T(8,128)(2,1)} %bitcast.183, ...), dimensions={1} | concatenate | bytes 1769472 | tf_op jit(solution)/shard_map/vmap()/concatenate | solution.py:149
  197.4 2.1 fusion.64
  199.6 1.0 maximum_bitcast_fusion
  200.6 52.2 %all-reduce.15.cloned.1.call-done = f32[1,648,384]{2,1,0:T(8,128)} async-done(((f32[1,648,384]{2,1,0:T(8,128)}), f32[1,648,384]{2,1,0:T(8,128)}) %all-reduce.15.cloned.1.call-update) | async-done | bytes 995344 | tf_op jit(solution)/shard_map/psum | solution.py:209
  252.9 80.4 %all-gather.3.cloned.1.call-done = f32[8,648,384]{2,1,0:T(8,128)} async-done(((f32[1,648,384]{2,1,0:T(8,128)}), f32[8,648,384]{2,1,0:T(8,128)}) %all-gather.3.cloned.1.call-update) | async-done | bytes 7962640 | tf_op jit(solution)/shard_map/all_gather | solution.py:210
  333.3 4.5 %multiply_reduce_fusion = f32[]{:T(128)} fusion(f32[8,648,384]{2,1,0:T(8,128)} %all-gather.3.cloned.1.call-done), kind=kLoop, calls=%fused_computation.4 | loop fusion | flops 2654207 | bytes 5308420 | tf_op jit(solution)/shard_map/reduce_sum | solution.py:215
  337.7 3.0 multiply_reduce_fusion.1
  342.1 2.9 multiply_convert_fusion
  345.0 1.8 copy.118
  346.9 2.0 multiply_convert_fusion.1
  348.8 1.3 copy.117
  (112 shorter events, 12.5 us)
Async XLA Ops:
  7.2 72.7 %copy-start = (bf16[3,3,384,384]{3,2,1,0:T(8,128)(2,1)S(1)}, bf16[3,3,384,384]{3,2,1,0:T(8,128)(2,1)}, u32[]{:S(2)}) copy-start(bf16[3,3,384,384]{3,2,1,0:T(8,128)(2,1)} %param.14) | copy-start | bytes 7962628
  11.0 67.3 %copy-start.8 = (pred[4]{0:T(512)(128)(4,1)}, pred[4]{0:T(512)(128)(4,1)S(1)}, u32[]{:S(2)}) copy-start(pred[4]{0:T(512)(128)(4,1)S(1)} %compare_bitcast_fusion) | copy-start | bytes 16
  38.5 1.7 copy-start.10
  38.7 9.6 %copy-start.4 = (bf16[1,1,8,16,192]{4,3,2,1,0:T(8,128)(2,1)S(1)}, bf16[1,1,8,16,192]{4,3,2,1,0:T(8,128)(2,1)}, u32[]{:S(2)}) copy-start(bf16[1,1,8,16,192]{4,3,2,1,0:T(8,128)(2,1)} %param.11) | copy-start | bytes 147460
  41.5 120.3 %all-to-all-start = ((bf16[8,2,2160]{2,1,0:T(2,128)(2,1)}), bf16[8,2,2160]{2,1,0:T(2,128)(2,1)}, u32[]{:S(2)}, u32[]{:S(2)}) async-start(bf16[8,2,2160]{2,1,0:T(2,128)(2,1)} %reshape.373), calls=%async_computation | async-start | bytes 139264 | tf_op jit(solution)/shard_map/all_to_all | solution.py:156
  46.3 21.4 %copy-start.7 = (s32[128]{0:T(128)S(1)}, s32[128]{0:T(128)}, u32[]{:S(2)}) copy-start(s32[128]{0:T(128)} %constant.110.clone) | copy-start | bytes 1540
  78.0 1.8 copy-start.6
  82.3 19.0 %copy-start.9 = (s32[416]{0:T(512)S(1)}, s32[416]{0:T(512)}, u32[]{:S(2)}) copy-start(s32[416]{0:T(512)} %constant.113.clone) | copy-start | bytes 4996
  82.5 0.7 copy-start.3
  142.9 26.9 %copy-start.5 = (bf16[8,16,384]{2,1,0:T(8,128)(2,1)}, bf16[8,16,384]{2,1,0:T(8,128)(2,1)S(1)}, u32[]{:S(2)}) copy-start(bf16[8,16,384]{2,1,0:T(8,128)(2,1)S(1)} %fusion.18) | copy-start | bytes 294916
  161.8 28.7 %all-to-all-start.1 = ((bf16[8,2,4320]{2,1,0:T(2,128)(2,1)}), bf16[8,2,4320]{2,1,0:T(2,128)(2,1)}, u32[]{:S(2)}, u32[]{:S(2)}) async-start(bf16[8,2,4320]{2,1,0:T(2,128)(2,1)} %reshape.371), calls=%async_computation.1 | async-start | bytes 278528 | tf_op jit(solution)/shard_map/all_to_all | solution.py:156
  166.7 86.2 %all-reduce.15.cloned.1.call-start = ((), (), s32[]{:S(2)}) async-start(), calls=%async_computation.2 | async-start | bytes 1990656 | tf_op jit(solution)/shard_map/psum | solution.py:209
  169.8 19.6 %copy-start.1 = (bf16[1024,384]{1,0:T(8,128)(2,1)S(1)}, bf16[1024,384]{1,0:T(8,128)(2,1)}, u32[]{:S(2)}) copy-start(bf16[1024,384]{1,0:T(8,128)(2,1)} %all_gather.36) | copy-start | bytes 2359300
  197.4 2.2 copy-start.2
  200.6 132.7 %all-gather.3.cloned.1.call-start = ((), (), s32[]{:S(2)}) async-start(), calls=%async_computation.3 | async-start | bytes 8957952 | tf_op jit(solution)/shard_map/all_gather | solution.py:210
Sparse Core Ops, SparseCore 0:
  200.7 52.1 all-reduce.14
  254.5 78.7 all-gather.2

commit v5 on v2

--- a/solution.py
+++ b/solution.py
@@ -65,24 +65,30 @@
     lj = ej % breadth
     k = np.where(sides == 0, lj, np.where(sides == 1, breadth + lj, np.where(sides == 2, 2 * breadth + li, 2 * breadth + height + li)))
     edge = ((ei // height) * across + ej // breadth) * rim_len + k
-    return intra.astype(np.int32), seam_cell.astype(np.int32), edge.astype(np.int32)
+    edge_of_rim = np.full((tiles, rim_len), -1)
+    edge_of_rim[edge // rim_len, edge % rim_len] = np.arange(4 * side)
+    maps = (intra, seam_cell, edge, edge_of_rim)
+    return tuple(m.astype(np.int32) for m in maps)
 
 
 def one_hot(rows, cols, dtype):
     return (rows[:, None] == cols[None, :]).astype(dtype)
 
 
-def halo_lookup(edge_set, link_row, turn_row):
-    side_len = edge_set.shape[2]
-    depth = edge_set.shape[3]
-    flattened = edge_set.reshape(-1, side_len, depth)
-    picked = jnp.take(flattened, link_row, axis=0)
-    return jnp.where((turn_row == 1)[:, None, None], picked[:, ::-1], picked)
+def seam_source(cell, link_row, turn_row, side):
+    which = cell // side
+    pos = cell % side
+    link = jnp.zeros_like(cell)
+    turn = jnp.zeros_like(cell)
+    for k in range(4):
+        link = jnp.where(which == k, link_row[k], link)
+        turn = jnp.where(which == k, turn_row[k], turn)
+    return link * side + jnp.where(turn == 1, side - 1 - pos, pos)
 
 
 def padded_tile(cells, maps, place, link_row, turn_row):
     height, breadth, depth = cells.shape
-    intra, seam_cell, edge = maps
+    intra, seam_cell, edge, _ = maps
     rim_len = 2 * (height + breadth)
     tiles = intra.shape[0]
     side = edge.shape[0] // 4
@@ -92,12 +98,12 @@
         rims,
         preferred_element_type=jnp.float32,
     ).astype(cells.dtype)
-    edge_set = lax.all_gather(edges.reshape(1, 4, side, depth), "face", axis=0, tiled=True)
-    seam_halo = halo_lookup(edge_set, link_row, turn_row).reshape(4 * side, depth)
+    edge_set = lax.all_gather(edges, "face", axis=0, tiled=True)
     own_intra = lax.dynamic_index_in_dim(jnp.asarray(intra), place, 0, False)
     own_seam = lax.dynamic_index_in_dim(jnp.asarray(seam_cell), place, 0, False)
-    pool = jnp.concatenate([rims, seam_halo], axis=0)
-    source = jnp.where(own_intra >= 0, own_intra, jnp.where(own_seam >= 0, tiles * rim_len + own_seam, -1))
+    pool = jnp.concatenate([rims, edge_set], axis=0)
+    glued = tiles * rim_len + seam_source(jnp.maximum(own_seam, 0), link_row, turn_row, side)
+    source = jnp.where(own_intra >= 0, own_intra, jnp.where(own_seam >= 0, glued, -1))
     halo = jnp.dot(
         one_hot(source, jnp.arange(pool.shape[0]), cells.dtype),
         pool,
@@ -112,9 +118,8 @@
 
 
 def return_border(border, maps, place, link_row, turn_row):
-    intra, seam_cell, edge = maps
+    intra, seam_cell, edge, edge_of_rim = maps
     tiles, frame_len = intra.shape
-    depth = border.shape[-1]
     rim_len = frame_len - 4
     side = edge.shape[0] // 4
     exact = lax.Precision.HIGHEST
@@ -124,14 +129,16 @@
         borders,
         precision=exact,
     )
-    seam_set = lax.all_gather(seam_sum.reshape(1, 4, side, depth), "face", axis=0, tiled=True)
-    own_edges = halo_lookup(seam_set, link_row, turn_row).reshape(4 * side, depth)
+    seam_set = lax.all_gather(seam_sum, "face", axis=0, tiled=True)
     own_cells = place * rim_len + jnp.arange(rim_len)
     from_tiles = jnp.dot(
         one_hot(own_cells, jnp.asarray(intra.reshape(-1)), jnp.float32), borders, precision=exact
     )
+    own_edge = lax.dynamic_index_in_dim(jnp.asarray(edge_of_rim), place, 0, False)
+    glued = seam_source(jnp.maximum(own_edge, 0), link_row, turn_row, side)
+    glued = jnp.where(own_edge >= 0, glued, -1)
     from_seams = jnp.dot(
-        one_hot(own_cells, jnp.asarray(edge), jnp.float32), own_edges, precision=exact
+        one_hot(glued, jnp.arange(seam_set.shape[0]), jnp.float32), seam_set, precision=exact
     )
     return from_tiles + from_seams
 
@@ -201,9 +208,10 @@
     size_in = grad_w_in.shape[0]
     total = lax.psum(jnp.concatenate([grad_w_in, grad_w_out], axis=0), ("face", "tile"))
     factor = lax.rsqrt(jnp.sum(total * total) / total.size + epsilon)
-    update = (total * factor).astype(jnp.bfloat16)
-    update_in = update[:size_in].reshape(3, 3, width_in, width_out)
-    update_out = update[size_in:].reshape(3, 3, width_out, width_out)
+    update_in = (total[:size_in] * factor).astype(jnp.bfloat16)
+    update_out = (total[size_in:] * factor).astype(jnp.bfloat16)
+    update_in = update_in.reshape(3, 3, width_in, width_out)
+    update_out = update_out.reshape(3, 3, width_out, width_out)
     return (grad_one[None, None], update_in, update_out)
 
 

time: 330 us -> 321 us (0.973)
  local copies, waits for them, and re-layouts: 21.9 us -> 10.5 us
  other arithmetic: 25.8 us -> 32.6 us
    gather x3 -> x0, local copies, waits for them, and re-layouts: 5.25 us -> none  [halo_lookup(): picked = jnp.take(flattened, link_row, axis=0)]
    select_n x8 -> x2, other arithmetic: 7.01 us -> 11.8 us  [the longest x1 6.14 us: return_border(): glued = jnp.where(own_edge >= 0, glued, -1)]
    rev x3 -> x0, local copies, waits for them, and re-layouts: 4.65 us -> none  [halo_lookup(): return jnp.where((turn_row == 1)[:, None, None], picked[:, ::-1], picked)]
    convert_element_type x1 -> x2, other arithmetic: 3.88 us -> 7.43 us  [the longest x1 4.42 us: body(): update_out = (total[size_in:] * factor).astype(jnp.bfloat16)]
where the time goes in v5:
time: 321 us; the launch traced here: 320 us
  waiting for transfers between devices  175 us (55%)
  blocking collectives  76.2 us (24%)
  other arithmetic  32.6 us (10%)
  between operations  15.2 us (5%)
  matrix products  10.7 us (3%)
  local copies, waits for them, and re-layouts  10.5 us (3%)
    psum x1, waiting for transfers between devices, body(): lax.psum(jnp.concatenate([grad_w_in, grad_w_out], axis=0), ('face', 'tile'))  175 us
    all_gather x2, blocking collectives, padded_tile(): rims = lax.all_gather(rim_of(cells), 'tile', axis=0, tiled=True)  30.2 us
    all_gather x2, blocking collectives, padded_tile(): edge_set = lax.all_gather(edges, 'face', axis=0, tiled=True)  18.2 us
    all_gather x1, blocking collectives, return_border(): borders = lax.all_gather(border, 'tile', axis=0, tiled=True)  16.4 us
    all_gather x1, blocking collectives, return_border(): seam_set = lax.all_gather(seam_sum, 'face', axis=0, tiled=True)  11.4 us
  transfers between devices with their start and end apart: 1, of which 1 were waited for; matrix products, arithmetic and copies ran while one was open for 0% of the time, Pallas kernels for 0%

profile of v5, /device:TPU:0, one launch (start us, length us, event | category | flops | bytes accessed | tf_op | source)
XLA Modules:
  0.0 320.1 jit_solution(12319919677867705034)
XLA Ops:
  7.2 0.0 copy-start
  7.2 0.0 copy-start.7
  7.2 0.0 all-reduce.15.cloned.1.call-start
  7.2 0.9 constant_dynamic-slice_fusion.1
  8.1 0.6 fusion.75
  8.7 0.7 fusion.74
  9.4 0.7 slice_bitcast_fusion.9
  10.1 0.8 fusion.73
  10.9 15.9 %all_gather.18 = bf16[384,192]{1,0:T(8,128)(2,1)S(1)} all-gather(bf16[48,192]{1,0:T(8,128)(2,1)S(1)} %pad_maximum_fusion.8), channel_id=1, replica_groups=mesh['face'=4,'tile'=8] {'tile'}, dimensions={0}, use_global_device_ids=true | all-gather | bytes 165888 | tf_op jit(solution)/shard_map/all_gather | solution.py:95
  26.8 0.1 copy.47
  27.0 0.9 convolution_convert_fusion.1
  27.9 8.7 %all_gather.19 = bf16[512,192]{0,1:T(8,128)(2,1)S(1)} all-gather(bf16[128,192]{0,1:T(8,128)(2,1)S(1)} %convolution_convert_fusion.1), channel_id=1, replica_groups=mesh['face'=4,'tile'=8] {'face'}, dimensions={0}, use_global_device_ids=true | all-gather | bytes 245760 | tf_op jit(solution)/shard_map/all_gather | solution.py:101
  36.6 5.6 %compare_select_fusion = s32[52]{0:T(128)S(1)} fusion(s32[8,52]{1,0:T(8,128)} %constant.142.clone, s32[]{:T(128)S(6)} %select_n.218, s32[8,52]{1,0:T(8,128)} %constant.143.clone, s32[]{:T(128)} %bitcast.13, s32[]{:T(128)} %bitcast.12, s32[]{:T(128)} %bitcast.11, s32[]{:T(128)} %bitcast.10, s32[]{:T(128)} %bitcast.9, s32[]{:T(128)} %bitcast.8, s32[]{:T(128)} %bitcast.7, ...), kind=kLoop, calls=%fused_computation.101 | loop fusion | flops 1820 | bytes 660 | tf_op jit(solution)/shard_map/jit(_where)/select_n | solution.py:106
  42.3 0.3 convolution_convert_fusion.3
  42.5 0.0 copy-start.13
  42.6 1.0 pad_maximum_fusion.5
  43.6 1.0 pad_maximum_fusion.2
  44.7 0.7 fusion.69
  45.4 1.1 concatenate.71
  46.5 0.0 copy-start.1
  46.5 2.6 multiply_convert_fusion
  49.1 14.3 %all_gather.20 = bf16[384,384]{1,0:T(8,128)(2,1)S(1)} all-gather(bf16[48,384]{1,0:T(8,128)(2,1)S(1)} %pad_maximum_fusion.7), channel_id=1, replica_groups=mesh['face'=4,'tile'=8] {'tile'}, dimensions={0}, use_global_device_ids=true | all-gather | bytes 331776 | tf_op jit(solution)/shard_map/all_gather | solution.py:95
  63.5 0.3 convolution_convert_fusion
  63.8 9.5 %all_gather.21 = bf16[512,384]{1,0:T(8,128)(2,1)S(1)} all-gather(bf16[128,384]{1,0:T(8,128)(2,1)S(1)} %convolution_convert_fusion), channel_id=1, replica_groups=mesh['face'=4,'tile'=8] {'face'}, dimensions={0}, use_global_device_ids=true | all-gather | bytes 491520 | tf_op jit(solution)/shard_map/all_gather | solution.py:101
  73.3 0.3 convolution_convert_fusion.2
  73.6 0.1 pad_maximum_fusion.3
  73.7 0.1 pad_maximum_fusion.1
  73.8 0.0 copy-done.1
  73.8 0.1 fusion.66
  73.9 0.1 fusion.67
  73.9 0.0 copy-start.9
  74.2 0.6 fusion.76
  74.8 0.0 copy-done.9
  74.8 0.9 fusion.23
  75.7 0.1 fusion.64
  75.9 0.2 pad_add_fusion
  76.1 0.0 copy-start.12
  76.1 0.6 fusion.65
  76.7 0.1 copy-done.5
  76.9 0.6 slice_bitcast_fusion.1
  77.5 0.5 iota_add_fusion
  78.0 6.1 %bitcast_select_fusion = s32[48]{0:T(128)} fusion(s32[8,48]{1,0:T(8,128)} %constant.146.clone, s32[]{:T(128)S(6)} %select_n.218, s32[]{:T(128)} %bitcast.13, s32[]{:T(128)} %bitcast.12, s32[]{:T(128)} %bitcast.11, s32[]{:T(128)} %bitcast.10, s32[]{:T(128)} %bitcast.9, s32[]{:T(128)} %bitcast.8, s32[]{:T(128)} %bitcast.7, s32[]{:T(128)} %bitcast.6), kind=kLoop, calls=%fused_computation.104 | loop fusion | flops 1536 | bytes 420 | tf_op jit(solution)/shard_map/jit(_where)/select_n | solution.py:139
  84.2 0.7 copy.71
  84.9 0.8 maximum_bitcast_fusion
  85.7 16.4 %all-gather = f32[8,52,384]{2,1,0:T(8,128)} all-gather(f32[1,52,384]{2,1,0:T(8,128)S(1)} %maximum_bitcast_fusion), channel_id=1, replica_groups=mesh['face'=4,'tile'=8] {'tile'}, dimensions={0}, use_global_device_ids=true | all-gather | bytes 718848 | tf_op jit(solution)/shard_map/all_gather | solution.py:126
  102.0 2.0 reshape.283
  104.0 1.6 fusion.8
  105.6 11.4 %all_gather.23 = f32[512,384]{1,0:T(8,128)S(1)} all-gather(f32[128,384]{1,0:T(8,128)S(1)} %fusion.8), channel_id=1, replica_groups=mesh['face'=4,'tile'=8] {'face'}, dimensions={0}, use_global_device_ids=true | all-gather | bytes 983040 | tf_op jit(solution)/shard_map/all_gather | solution.py:132
  117.1 1.5 fusion.40
  118.6 0.4 convolution_add_fusion
  119.0 0.0 copy-start.2
  119.1 0.9 fusion.21
  120.0 0.0 copy-done.6
  120.0 0.0 copy-done.8
  120.1 0.1 fusion.20
  120.2 0.0 copy-start.11
  120.2 0.0 copy-done.2
  120.3 0.5 fusion.77
  120.8 3.6 %pad_maximum_fusion = f32[5184,384]{1,0:T(8,128)} fusion(f32[3456,384]{1,0:T(8,128)S(1)} %fusion.21, f32[1728,384]{1,0:T(8,128)S(1)} %fusion.77), kind=kLoop, calls=%fused_computation | loop fusion | flops 1990656 | bytes 15925248 | tf_op jit(solution)/shard_map/concatenate | solution.py:209
  124.4 0.0 all-reduce.15.cloned.1.call-update
  124.4 174.8 %all-reduce.15.cloned.1.call-done = f32[5184,384]{1,0:T(8,128)} async-done(((f32[5184,384]{1,0:T(8,128)}), f32[5184,384]{1,0:T(8,128)}) %all-reduce.15.cloned.1.call-update) | async-done | bytes 7962640 | tf_op jit(solution)/shard_map/psum | solution.py:209
  299.2 5.9 %multiply_reduce_fusion = f32[]{:T(128)} fusion(f32[5184,384]{1,0:T(8,128)} %all-reduce.15.cloned.1.call-done), kind=kLoop, calls=%fused_computation.1 | loop fusion | flops 3981311 | bytes 7962628 | tf_op jit(solution)/shard_map/reduce_sum | solution.py:210
  305.8 3.0 fusion.1
  308.8 4.4 %fusion = bf16[3456,384]{1,0:T(8,128)(2,1)} fusion(f32[5184,384]{1,0:T(8,128)} %all-reduce.15.cloned.1.call-done, f32[]{:T(128)S(6)} %rsqrt.3), kind=kLoop, calls=%fused_computation.3 | loop fusion | flops 2654208 | bytes 7962628 | tf_op jit(solution)/shard_map/convert_element_type | solution.py:212
  (48 shorter events, 0.4 us)
Async XLA Ops:
  7.2 67.0 %copy-start = (bf16[3,3,384,384]{3,2,1,0:T(8,128)(2,1)S(1)}, bf16[3,3,384,384]{3,2,1,0:T(8,128)(2,1)}, u32[]{:S(2)}) copy-start(bf16[3,3,384,384]{3,2,1,0:T(8,128)(2,1)} %param.15) | copy-start | bytes 7962628
  7.2 38.2 %copy-start.7 = (bf16[1,1,8,16,192]{4,3,2,1,0:T(8,128)(2,1)S(1)}, bf16[1,1,8,16,192]{4,3,2,1,0:T(8,128)(2,1)}, u32[]{:S(2)}) copy-start(bf16[1,1,8,16,192]{4,3,2,1,0:T(8,128)(2,1)} %param.12) | copy-start | bytes 147460
  7.2 292.0 %all-reduce.15.cloned.1.call-start = ((), (), s32[]{:S(2)}) async-start(), calls=%async_computation | async-start | bytes 15925248 | tf_op jit(solution)/shard_map/psum | solution.py:209
  42.5 20.9 %copy-start.13 = (s32[128]{0:T(128)S(1)}, s32[128]{0:T(128)}, u32[]{:S(2)}) copy-start(s32[128]{0:T(128)} %constant.141.clone) | copy-start | bytes 1540
  46.5 27.3 %copy-start.1 = (bf16[128,1728]{1,0:T(8,128)(2,1)}, bf16[128,1728]{1,0:T(8,128)(2,1)S(1)}, u32[]{:S(2)}) copy-start(bf16[128,1728]{1,0:T(8,128)(2,1)S(1)} %concatenate.71) | copy-start | bytes 1327108
  73.9 0.9 copy-start.9
  74.8 1.1 copy-start.3
  76.1 0.8 copy-start.5
  76.1 41.0 %copy-start.12 = (s32[416]{0:T(512)S(1)}, s32[416]{0:T(512)}, u32[]{:S(2)}) copy-start(s32[416]{0:T(512)} %constant.145.clone) | copy-start | bytes 4996
  84.9 32.2 %copy-start.15 = (s32[48]{0:T(128)S(1)}, s32[48]{0:T(128)}, u32[]{:S(2)}) copy-start(s32[48]{0:T(128)} %iota_add_fusion) | copy-start | bytes 580
  84.9 33.7 %copy-start.14 = (s32[48]{0:T(128)S(1)}, s32[48]{0:T(128)}, u32[]{:S(2)}) copy-start(s32[48]{0:T(128)} %bitcast_select_fusion) | copy-start | bytes 580
  104.0 15.0 %copy-start.4 = (f32[128,384]{1,0:T(8,128)S(1)}, f32[128,384]{1,0:T(8,128)}, u32[]{:S(2)}) copy-start(f32[128,384]{1,0:T(8,128)} %copy-done.3) | copy-start | bytes 589828
  104.0 15.0 %copy-start.10 = (bf16[1,1,8,16,384]{4,3,2,1,0:T(8,128)(2,1)S(1)}, bf16[1,1,8,16,384]{4,3,2,1,0:T(8,128)(2,1)}, u32[]{:S(2)}) copy-start(bf16[1,1,8,16,384]{4,3,2,1,0:T(8,128)(2,1)} %param.13) | copy-start | bytes 294916
  119.0 1.0 copy-start.6
  119.0 1.0 copy-start.8
  119.0 1.2 copy-start.2
  120.2 4.2 %copy-start.11 = (bf16[8,16,384]{2,1,0:T(8,128)(2,1)}, bf16[8,16,384]{2,1,0:T(8,128)(2,1)S(1)}, u32[]{:S(2)}) copy-start(bf16[8,16,384]{2,1,0:T(8,128)(2,1)S(1)} %fusion.20) | copy-start | bytes 294916
Sparse Core Ops, SparseCore 0:
  124.6 174.5 all-reduce.14

commit v6 on v5

--- a/solution.py
+++ b/solution.py
@@ -7,6 +7,7 @@
 root_half = 0.7071067811865476
 inv_root_tau = 0.3989422804014327
 epsilon = 1e-06
+factor_budget = 48 * 2**20
 
 
 def gelu_value(pre):
@@ -156,6 +157,15 @@
     return jnp.concatenate(windows, axis=1)
 
 
+def gather_all(block, faces):
+    local = lax.all_gather(block, "tile", axis=0, tiled=True)
+    parts = [local]
+    for shift in range(1, faces):
+        pairs = [(i, (i + shift) % faces) for i in range(faces)]
+        parts.append(lax.ppermute(local, "face", pairs))
+    return jnp.concatenate(parts, axis=0)
+
+
 def body(inputs, upstream, weight_in, weight_out, seam_link, seam_turn):
     cells = inputs[0, 0]
     height, breadth, width_in = cells.shape
@@ -166,7 +176,8 @@
     link_row = lax.dynamic_index_in_dim(seam_link, face_pos, 0, False)
     turn_row = lax.dynamic_index_in_dim(seam_turn, face_pos, 0, False)
     maps = face_maps(tiles, height, breadth)
-    unfolded_in = unfold(padded_tile(cells, maps, place, link_row, turn_row), height, breadth)
+    padded_tile_in = padded_tile(cells, maps, place, link_row, turn_row)
+    unfolded_in = unfold(padded_tile_in, height, breadth)
     pre_one = jnp.dot(
         unfolded_in, weight_in.reshape(-1, width_out), preferred_element_type=jnp.float32
     )
@@ -199,17 +210,41 @@
     grad_one = (grad_act * gelu_slope(pre_one.reshape(height, breadth, width_out))).astype(
         jnp.bfloat16
     )
-    grad_w_in = lax.dot_general(
-        unfolded_in,
-        grad_one.reshape(-1, width_out),
-        (((0,), (0,)), ((), ())),
-        preferred_element_type=jnp.float32,
-    )
-    size_in = grad_w_in.shape[0]
-    total = lax.psum(jnp.concatenate([grad_w_in, grad_w_out], axis=0), ("face", "tile"))
-    factor = lax.rsqrt(jnp.sum(total * total) / total.size + epsilon)
-    update_in = (total[:size_in] * factor).astype(jnp.bfloat16)
-    update_out = (total[size_in:] * factor).astype(jnp.bfloat16)
+    faces = lax.axis_size("face")
+    gathered = faces * tiles * (padded_tile_in.size + grad_one.size) * 2
+    if gathered <= factor_budget:
+        total_out = lax.psum(grad_w_out, ("face", "tile"))
+        every_pad = gather_all(padded_tile_in[None], faces)
+        every_grad = gather_all(grad_one.reshape(1, -1, width_out), faces)
+        every_grad = every_grad.reshape(-1, width_out)
+        blocks = []
+        for down_step in range(3):
+            for side_step in range(3):
+                window = every_pad[:, down_step : down_step + height, side_step : side_step + breadth]
+                blocks.append(
+                    lax.dot_general(
+                        window.reshape(-1, width_in),
+                        every_grad,
+                        (((0,), (0,)), ((), ())),
+                        preferred_element_type=jnp.float32,
+                    )
+                )
+        total_in = jnp.concatenate(blocks, axis=0)
+    else:
+        grad_w_in = lax.dot_general(
+            unfolded_in,
+            grad_one.reshape(-1, width_out),
+            (((0,), (0,)), ((), ())),
+            preferred_element_type=jnp.float32,
+        )
+        size_in = grad_w_in.shape[0]
+        total = lax.psum(jnp.concatenate([grad_w_in, grad_w_out], axis=0), ("face", "tile"))
+        total_in = total[:size_in]
+        total_out = total[size_in:]
+    squares = jnp.sum(total_in * total_in) + jnp.sum(total_out * total_out)
+    factor = lax.rsqrt(squares / (total_in.size + total_out.size) + epsilon)
+    update_in = (total_in * factor).astype(jnp.bfloat16)
+    update_out = (total_out * factor).astype(jnp.bfloat16)
     update_in = update_in.reshape(3, 3, width_in, width_out)
     update_out = update_out.reshape(3, 3, width_out, width_out)
     return (grad_one[None, None], update_in, update_out)

time: 321 us -> 348 us (1.084)
  waiting for transfers between devices: 175 us -> 132 us
  blocking collectives: 76.2 us -> 118 us
  local copies, waits for them, and re-layouts: 10.5 us -> 25.2 us
  matrix products: 10.7 us -> 19.8 us
  starting transfers between devices: 0.04 us -> 7.05 us
    psum x1, waiting for transfers between devices: 175 us -> 104 us  [body(): total_out = lax.psum(grad_w_out, ('face', 'tile'))]
    all_gather x0 -> x2, blocking collectives: none -> 33.5 us  [gather_all(): local = lax.all_gather(block, 'tile', axis=0, tiled=True)]
    ppermute x0 -> x6, waiting for transfers between devices: none -> 27.7 us  [gather_all(): parts.append(lax.ppermute(local, 'face', pairs))]
    all_gather x2, blocking collectives: 18.2 us -> 27.3 us  [padded_tile(): edge_set = lax.all_gather(edges, 'face', axis=0, tiled=True)]
    dot_general x1 -> x9, matrix products: 0.53 us -> 9.52 us  [body(): lax.dot_general(window.reshape(-1, width_in), every_grad, (((0,), (0,)),...]
    slice x0 -> x1, local copies, waits for them, and re-layouts: none -> 8.93 us  [body(): every_pad[:, down_step:down_step + height, side_step:side_step + breadth]]
    ppermute x0 -> x6, starting transfers between devices: none -> 7.02 us  [gather_all(): parts.append(lax.ppermute(local, 'face', pairs))]
    ppermute x0 -> x3, local copies, waits for them, and re-layouts: none -> 3.89 us  [gather_all(): parts.append(lax.ppermute(local, 'face', pairs))]
  transfers between devices with their start and end apart: 1 -> 7, of which waited for: 1 -> 4; matrix products, arithmetic and copies ran while one was open for 0% -> 13% of each run, Pallas kernels for 0% -> 0%
where the time goes in v6:
time: 348 us; the launch traced here: 347 us
  waiting for transfers between devices  132 us (38%)
  blocking collectives  118 us (34%)
  other arithmetic  29.4 us (8%)
  local copies, waits for them, and re-layouts  25.2 us (7%)
  matrix products  19.8 us (6%)
  between operations  16 us (5%)
  starting transfers between devices  7.05 us (2%)
    psum x1, waiting for transfers between devices, body(): total_out = lax.psum(grad_w_out, ('face', 'tile'))  104 us
    all_gather x2, blocking collectives, gather_all(): local = lax.all_gather(block, 'tile', axis=0, tiled=True)  33.5 us
    all_gather x2, blocking collectives, padded_tile(): rims = lax.all_gather(rim_of(cells), 'tile', axis=0, tiled=True)  30.1 us
    ppermute x6, waiting for transfers between devices, gather_all(): parts.append(lax.ppermute(local, 'face', pairs))  27.7 us
    all_gather x2, blocking collectives, padded_tile(): edge_set = lax.all_gather(edges, 'face', axis=0, tiled=True)  27.3 us
    all_gather x1, blocking collectives, return_border(): borders = lax.all_gather(border, 'tile', axis=0, tiled=True)  15 us
    all_gather x1, blocking collectives, return_border(): seam_set = lax.all_gather(seam_sum, 'face', axis=0, tiled=True)  11.7 us
    dot_general x9, matrix products, body(): lax.dot_general(window.reshape(-1, width_in), every_grad, (((0,), (0,)),...  9.52 us
  transfers between devices with their start and end apart: 7, of which 4 were waited for; matrix products, arithmetic and copies ran while one was open for 13% of the time, Pallas kernels for 0%

profile of v6, /device:TPU:0, one launch (start us, length us, event | category | flops | bytes accessed | tf_op | source)
XLA Modules:
  0.0 347.1 jit_solution(12968216557379542346)
XLA Ops:
  7.2 0.9 slice_bitcast_fusion.9
  8.1 0.8 fusion.72
  8.9 15.9 %all_gather.24 = bf16[384,192]{1,0:T(8,128)(2,1)S(1)} all-gather(bf16[48,192]{1,0:T(8,128)(2,1)S(1)} %pad_maximum_fusion.10), channel_id=1, replica_groups=mesh['face'=4,'tile'=8] {'tile'}, dimensions={0}, use_global_device_ids=true | all-gather | bytes 165888 | tf_op jit(solution)/shard_map/all_gather | solution.py:96
  25.0 0.9 convolution_convert_fusion.1
  25.9 8.7 %all_gather.25 = bf16[512,192]{0,1:T(8,128)(2,1)S(1)} all-gather(bf16[128,192]{0,1:T(8,128)(2,1)S(1)} %convolution_convert_fusion.1), channel_id=1, replica_groups=mesh['face'=4,'tile'=8] {'face'}, dimensions={0}, use_global_device_ids=true | all-gather | bytes 245760 | tf_op jit(solution)/shard_map/all_gather | solution.py:102
  34.6 0.7 constant_dynamic-slice_fusion.1
  35.3 0.7 fusion.74
  36.0 0.7 fusion.73
  36.7 5.8 %compare_select_fusion = s32[52]{0:T(128)S(1)} fusion(s32[8,52]{1,0:T(8,128)} %constant.142.clone, s32[]{:T(128)S(6)} %select_n.218, s32[8,52]{1,0:T(8,128)} %constant.143.clone, s32[]{:T(128)} %bitcast.13, s32[]{:T(128)} %bitcast.12, s32[]{:T(128)} %bitcast.11, s32[]{:T(128)} %bitcast.10, s32[]{:T(128)} %bitcast.9, s32[]{:T(128)} %bitcast.8, s32[]{:T(128)} %bitcast.7, ...), kind=kLoop, calls=%fused_computation.111 | loop fusion | flops 1820 | bytes 660 | tf_op jit(solution)/shard_map/jit(_where)/select_n | solution.py:107
  42.8 0.9 pad_maximum_fusion.3
  43.7 16.8 %all-gather = bf16[80,18,192]{2,1,0:T(8,128)(2,1)S(1)} all-gather(bf16[10,18,192]{2,1,0:T(8,128)(2,1)S(1)} %pad_maximum_fusion.3), channel_id=2, replica_groups=mesh['face'=4,'tile'=8] {'tile'}, dimensions={0}, use_global_device_ids=true | all-gather | bytes 622080 | tf_op jit(solution)/shard_map/all_gather | solution.py:161
  60.5 0.9 copy-done.3
  61.4 1.1 copy.60
  62.5 1.5 collective-permute-start.2
  64.0 1.5 collective-permute-start.1
  65.5 0.6 collective-permute-start
  66.2 0.7 fusion.67
  66.9 1.1 concatenate.79
  68.0 2.4 multiply_convert_fusion.2
  70.5 14.3 %all_gather.26 = bf16[384,384]{1,0:T(8,128)(2,1)S(1)} all-gather(bf16[48,384]{1,0:T(8,128)(2,1)S(1)} %pad_maximum_fusion.9), channel_id=1, replica_groups=mesh['face'=4,'tile'=8] {'tile'}, dimensions={0}, use_global_device_ids=true | all-gather | bytes 331776 | tf_op jit(solution)/shard_map/all_gather | solution.py:96
  85.1 18.6 %all_gather.27 = bf16[512,384]{1,0:T(8,128)(2,1)S(1)} all-gather(bf16[128,384]{1,0:T(8,128)(2,1)S(1)} %convolution_convert_fusion), channel_id=1, replica_groups=mesh['face'=4,'tile'=8] {'face'}, dimensions={0}, use_global_device_ids=true | all-gather | bytes 491520 | tf_op jit(solution)/shard_map/all_gather | solution.py:102
  104.5 0.6 fusion.75
  105.2 0.9 fusion.21
  106.6 15.0 %all-gather.1 = f32[8,52,384]{2,1,0:T(8,128)S(1)} all-gather(f32[1,52,384]{2,1,0:T(8,128)S(1)} %maximum_bitcast_fusion), channel_id=1, replica_groups=mesh['face'=4,'tile'=8] {'tile'}, dimensions={0}, use_global_device_ids=true | all-gather | bytes 718848 | tf_op jit(solution)/shard_map/all_gather | solution.py:127
  121.7 0.4 fusion.6
  122.2 11.7 %all_gather.29 = f32[512,384]{1,0:T(8,128)S(1)} all-gather(f32[128,384]{1,0:T(8,128)S(1)} %fusion.6), channel_id=1, replica_groups=mesh['face'=4,'tile'=8] {'face'}, dimensions={0}, use_global_device_ids=true | all-gather | bytes 983040 | tf_op jit(solution)/shard_map/all_gather | solution.py:133
  133.9 5.8 %bitcast_select_fusion = s32[48]{0:T(128)S(1)} fusion(s32[8,48]{1,0:T(8,128)} %constant.146.clone, s32[]{:T(128)S(6)} %select_n.218, s32[]{:T(128)} %bitcast.13, s32[]{:T(128)} %bitcast.12, s32[]{:T(128)} %bitcast.11, s32[]{:T(128)} %bitcast.10, s32[]{:T(128)} %bitcast.9, s32[]{:T(128)} %bitcast.8, s32[]{:T(128)} %bitcast.7, s32[]{:T(128)} %bitcast.6), kind=kLoop, calls=%fused_computation.114 | loop fusion | flops 1536 | bytes 420 | tf_op jit(solution)/shard_map/jit(_where)/select_n | solution.py:140
  139.6 0.4 fusion.38
  140.0 0.4 convolution_add_fusion
  140.7 16.7 %all_gather.31 = bf16[8,128,384]{2,1,0:T(8,128)(2,1)} all-gather(bf16[1,128,384]{2,1,0:T(8,128)(2,1)S(1)} %bitcast.226), channel_id=1, replica_groups=mesh['face'=4,'tile'=8] {'tile'}, dimensions={0}, use_global_device_ids=true | all-gather | bytes 884736 | tf_op jit(solution)/shard_map/all_gather | solution.py:161
  157.3 1.5 collective-permute-start.5
  158.8 1.2 collective-permute-start.4
  160.1 3.3 fusion.19
  163.4 0.8 collective-permute-start.3
  164.2 1.3 copy.65
  165.5 1.3 copy.64
  166.8 1.3 copy.63
  168.2 0.9 pad_maximum_fusion
  169.1 8.9 %fusion.62 = (bf16[32,8,16,192]{3,2,1,0:T(8,128)(2,1)S(1)}, bf16[32,8,16,192]{3,2,1,0:T(8,128)(2,1)}, bf16[32,8,16,192]{3,2,1,0:T(8,128)(2,1)}, bf16[32,8,16,192...) fusion(bf16[32,10,18,192]{3,2,1,0:T(8,128)(2,1)S(1)} %pad_maxim, ...), kind=kLoop, calls=%fused_computation.162 | loop fusion | bytes 28311552 | tf_op jit(solution)/shard_map/slice | solution.py:223
  178.0 6.6 %collective-permute-done.5 = bf16[8,128,384]{2,1,0:T(8,128)(2,1)} collective-permute-done((bf16[8,128,384]{2,1,0:T(8,128)(2,1)}, bf16[8,128,384]{2,1,0:T(8,128)(2,1)}, u32[]{:S(2)}, u32[]{:S(2)}) %collective-permute-start.5) | collective-permute-done | bytes 786464 | tf_op jit(solution)/shard_map/ppermute | solution.py:165
  184.7 13.9 %collective-permute-done.4 = bf16[8,128,384]{2,1,0:T(8,128)(2,1)} collective-permute-done((bf16[8,128,384]{2,1,0:T(8,128)(2,1)}, bf16[8,128,384]{2,1,0:T(8,128)(2,1)}, u32[]{:S(2)}, u32[]{:S(2)}) %collective-permute-start.4) | collective-permute-done | bytes 786464 | tf_op jit(solution)/shard_map/ppermute | solution.py:165
  198.5 7.1 %collective-permute-done.3 = bf16[8,128,384]{2,1,0:T(8,128)(2,1)S(1)} collective-permute-done((bf16[8,128,384]{2,1,0:T(8,128)(2,1)}, bf16[8,128,384]{2,1,0:T(8,128)(2,1)S(1)}, u32[]{:S(2)}, u32[]{:S(2)}) %collective-permute-start.3) | collective-permute-done | bytes 786464 | tf_op jit(solution)/shard_map/ppermute | solution.py:165
  205.7 1.8 pad_maximum_fusion.1
  207.6 1.0 convolution_dynamic-update-slice_fusion.8
  208.6 0.7 copy-done.11
  209.3 1.1 convolution_dynamic-update-slice_fusion.7
  210.3 0.6 copy-done.10
  210.9 1.1 convolution_dynamic-update-slice_fusion.6
  211.9 0.6 copy-done.9
  212.5 1.1 convolution_dynamic-update-slice_fusion.5
  213.6 0.5 copy-done.8
  214.1 1.1 convolution_dynamic-update-slice_fusion.4
  215.2 0.5 copy-done.7
  215.7 1.1 convolution_dynamic-update-slice_fusion.3
  216.8 0.5 copy-done.6
  217.3 1.1 convolution_dynamic-update-slice_fusion.2
  218.4 0.5 copy-done.5
  218.9 1.1 convolution_dynamic-update-slice_fusion.1
  220.0 1.1 convolution_dynamic-update-slice_fusion
  221.1 1.4 multiply_reduce_fusion.1
  222.5 104.5 %all-reduce.15.cloned.1.call-done = f32[3456,384]{1,0:T(8,128)} async-done(((f32[3456,384]{1,0:T(8,128)}), f32[3456,384]{1,0:T(8,128)}) %all-reduce.15.cloned.1.call-update) | async-done | bytes 5308432 | tf_op jit(solution)/shard_map/psum | solution.py:216
  326.9 4.5 %multiply_reduce_fusion = f32[]{:T(128)} fusion(f32[3456,384]{1,0:T(8,128)} %all-reduce.15.cloned.1.call-done), kind=kLoop, calls=%fused_computation.1 | loop fusion | flops 2654207 | bytes 5308420 | tf_op jit(solution)/shard_map/reduce_sum | solution.py:244
  332.7 3.2 multiply_convert_fusion.1
  335.8 4.4 %multiply_convert_fusion = bf16[3456,384]{1,0:T(8,128)(2,1)} fusion(f32[3456,384]{1,0:T(8,128)} %all-reduce.15.cloned.1.call-done, f32[]{:T(128)S(6)} %rsqrt.3), kind=kLoop, calls=%fused_computation | loop fusion | flops 2654208 | bytes 7962628 | tf_op jit(solution)/shard_map/convert_element_type | solution.py:247
  (92 shorter events, 2.5 us)
Async XLA Ops:
  7.2 97.3 %copy-start = (bf16[3,3,384,384]{3,2,1,0:T(8,128)(2,1)S(1)}, bf16[3,3,384,384]{3,2,1,0:T(8,128)(2,1)}, u32[]{:S(2)}) copy-start(bf16[3,3,384,384]{3,2,1,0:T(8,128)(2,1)} %param.15) | copy-start | bytes 7962628
  7.2 58.9 %copy-start.15 = (bf16[1,1,8,16,192]{4,3,2,1,0:T(8,128)(2,1)S(1)}, bf16[1,1,8,16,192]{4,3,2,1,0:T(8,128)(2,1)}, u32[]{:S(2)}) copy-start(bf16[1,1,8,16,192]{4,3,2,1,0:T(8,128)(2,1)} %param.12) | copy-start | bytes 147460
  7.2 319.7 %all-reduce.15.cloned.1.call-start = ((), (), s32[]{:S(2)}) async-start(), calls=%async_computation | async-start | bytes 10616832 | tf_op jit(solution)/shard_map/psum | solution.py:216
  60.5 0.9 copy-start.3
  62.5 22.3 %copy-start.22 = (s32[128]{0:T(128)S(1)}, s32[128]{0:T(128)}, u32[]{:S(2)}) copy-start(s32[128]{0:T(128)} %constant.141.clone) | copy-start | bytes 1540
  62.5 100.9 %collective-permute-start.2 = (bf16[8,10,18,192]{3,0,2,1:T(8,128)(2,1)}, bf16[8,10,18,192]{3,0,2,1:T(8,128)(2,1)}, u32[]{:S(2)}, u32[]{:S(2)}) collective-permute-start(bf16[8,10,18,192]{3,0,2,1:T(8,128)(2,1)} %copy.60), channel_id=1, source_target_pairs={{0,24},{8,0},{16,8},{24,16},{1,25},{9,1},{17,9},{25,17},{2,26},{10... | collective-permute-start | bytes 1658888 | tf_op jit(solution)/shard_map/ppermute | solution.py:165
  64.0 101.5 %collective-permute-start.1 = (bf16[8,10,18,192]{3,0,2,1:T(8,128)(2,1)}, bf16[8,10,18,192]{3,0,2,1:T(8,128)(2,1)}, u32[]{:S(2)}, u32[]{:S(2)}) collective-permute-start(bf16[8,10,18,192]{3,0,2,1:T(8,128)(2,1)} %copy.60), channel_id=1, source_target_pairs={{0,16},{8,24},{16,0},{24,8},{1,17},{9,25},{17,1},{25,9},{2,18},{10... | collective-permute-start | bytes 1658888 | tf_op jit(solution)/shard_map/ppermute | solution.py:165
  65.5 101.4 %collective-permute-start = (bf16[8,10,18,192]{3,0,2,1:T(8,128)(2,1)}, bf16[8,10,18,192]{3,0,2,1:T(8,128)(2,1)}, u32[]{:S(2)}, u32[]{:S(2)}) collective-permute-start(bf16[8,10,18,192]{3,0,2,1:T(8,128)(2,1)} %copy.60), channel_id=1, source_target_pairs={{0,8},{8,16},{16,24},{24,0},{1,9},{9,17},{17,25},{25,1},{2,10},{10... | collective-permute-start | bytes 1658888 | tf_op jit(solution)/shard_map/ppermute | solution.py:165
  104.3 0.9 copy-start.17
  105.1 1.1 copy-start.13
  106.2 15.5 %copy-start.21 = (s32[416]{0:T(512)S(1)}, s32[416]{0:T(512)}, u32[]{:S(2)}) copy-start(s32[416]{0:T(512)} %constant.144.clone) | copy-start | bytes 4996
  106.5 33.1 %copy-start.20 = (s32[416]{0:T(512)S(1)}, s32[416]{0:T(512)}, u32[]{:S(2)}) copy-start(s32[416]{0:T(512)} %constant.145.clone) | copy-start | bytes 4996
  121.6 18.9 %copy-start.16 = (f32[128,384]{1,0:T(8,128)S(1)}, f32[128,384]{1,0:T(8,128)}, u32[]{:S(2)}) copy-start(f32[128,384]{1,0:T(8,128)} %get-tuple-element.74) | copy-start | bytes 589828
  121.7 38.4 %copy-start.14 = (f32[128,384]{1,0:T(8,128)S(1)}, f32[128,384]{1,0:T(8,128)}, u32[]{:S(2)}) copy-start(f32[128,384]{1,0:T(8,128)} %copy-done.13) | copy-start | bytes 589828
  121.7 38.4 %copy-start.18 = (bf16[1,1,8,16,384]{4,3,2,1,0:T(8,128)(2,1)S(1)}, bf16[1,1,8,16,384]{4,3,2,1,0:T(8,128)(2,1)}, u32[]{:S(2)}) copy-start(bf16[1,1,8,16,384]{4,3,2,1,0:T(8,128)(2,1)} %param.13) | copy-start | bytes 294916
  140.7 22.7 %copy-start.19 = (bf16[8,16,384]{2,1,0:T(8,128)(2,1)}, bf16[8,16,384]{2,1,0:T(8,128)(2,1)S(1)}, u32[]{:S(2)}) copy-start(bf16[8,16,384]{2,1,0:T(8,128)(2,1)S(1)} %fusion.18) | copy-start | bytes 294916
  157.3 27.3 %collective-permute-start.5 = (bf16[8,128,384]{2,1,0:T(8,128)(2,1)}, bf16[8,128,384]{2,1,0:T(8,128)(2,1)}, u32[]{:S(2)}, u32[]{:S(2)}) collective-permute-start(bf16[8,128,384]{2,1,0:T(8,128)(2,1)} %all_gather.31), channel_id=1, source_target_pairs={{0,24},{8,0},{16,8},{24,16},{1,25},{9,1},{17,9},{25,17},{2,26},{10... | collective-permute-start | bytes 2359304 | tf_op jit(solution)/shard_map/ppermute | solution.py:165
  158.8 39.7 %collective-permute-start.4 = (bf16[8,128,384]{2,1,0:T(8,128)(2,1)}, bf16[8,128,384]{2,1,0:T(8,128)(2,1)}, u32[]{:S(2)}, u32[]{:S(2)}) collective-permute-start(bf16[8,128,384]{2,1,0:T(8,128)(2,1)} %all_gather.31), channel_id=1, source_target_pairs={{0,16},{8,24},{16,0},{24,8},{1,17},{9,25},{17,1},{25,9},{2,18},{10... | collective-permute-start | bytes 2359304 | tf_op jit(solution)/shard_map/ppermute | solution.py:165
  163.4 4.7 %copy-start.4 = (bf16[80,18,192]{2,1,0:T(8,128)(2,1)S(1)}, bf16[80,18,192]{2,1,0:T(8,128)(2,1)}, u32[]{:S(2)}) copy-start(bf16[80,18,192]{2,1,0:T(8,128)(2,1)} %copy-done.3) | copy-start | bytes 1658884
  163.4 42.3 %collective-permute-start.3 = (bf16[8,128,384]{2,1,0:T(8,128)(2,1)}, bf16[8,128,384]{2,1,0:T(8,128)(2,1)S(1)}, u32[]{:S(2)}, u32[]{:S(2)}) collective-permute-start(bf16[8,128,384]{2,1,0:T(8,128)(2,1)} %all_gather.31), channel_id=1, source_target_pairs={{0,8},{8,16},{16,24},{24,0},{1,9},{9,17},{17,25},{25,1},{2,10},{10... | collective-permute-start | bytes 2359304 | tf_op jit(solution)/shard_map/ppermute | solution.py:165
  178.0 29.5 %copy-start.12 = (bf16[32,8,16,192]{3,2,1,0:T(8,128)(2,1)S(1)}, bf16[32,8,16,192]{3,2,1,0:T(8,128)(2,1)}, u32[]{:S(2)}) copy-start(bf16[32,8,16,192]{3,2,1,0:T(8,128)(2,1)} %get-tuple-element.11) | copy-start | bytes 4718596
  207.5 1.7 copy-start.11
  209.2 1.6 copy-start.10
  210.9 1.7 copy-start.9
  212.5 1.6 copy-start.8
  214.1 1.6 copy-start.7
  215.7 1.6 copy-start.6
  217.3 1.6 copy-start.5
  221.1 110.3 %copy-start.2 = (f32[1728,384]{1,0:T(8,128)}, f32[1728,384]{1,0:T(8,128)S(1)}, u32[]{:S(2)}) copy-start(f32[1728,384]{1,0:T(8,128)S(1)} %convolution_dynamic-update-slice_fusion) | copy-start | bytes 7962628
  332.7 7.6 %copy-start.1 = (bf16[3,3,384,384]{3,2,1,0:T(8,128)(2,1)S(1)}, bf16[3,3,384,384]{3,2,1,0:T(8,128)(2,1)}, u32[]{:S(2)}) copy-start(bf16[3,3,384,384]{3,2,1,0:T(8,128)(2,1)} %param.15) | copy-start | bytes 7962628
Sparse Core Ops, SparseCore 0:
  163.5 163.3 all-reduce.14

commit v7 on v6

--- a/solution.py
+++ b/solution.py
@@ -157,6 +157,10 @@
     return jnp.concatenate(windows, axis=1)
 
 
+def grad_one_size(frame):
+    return (frame.shape[0] - 2) * (frame.shape[1] - 2) * frame.shape[2]
+
+
 def gather_all(block, faces):
     local = lax.all_gather(block, "tile", axis=0, tiled=True)
     parts = [local]
@@ -203,34 +207,47 @@
             frame = frame + jnp.pad(
                 piece, ((down_step, 2 - down_step), (side_step, 2 - side_step), (0, 0))
             )
-    own_rim = return_border(border_of(frame), maps, place, link_row, turn_row)
-    _, rim_back = jax.vjp(rim_of, jnp.zeros((height, breadth, width_out), jnp.float32))
-    (rim_add,) = rim_back(own_rim)
-    grad_act = frame[1:-1, 1:-1] + rim_add
-    grad_one = (grad_act * gelu_slope(pre_one.reshape(height, breadth, width_out))).astype(
-        jnp.bfloat16
-    )
+    def grad_hidden_of(frame):
+        own_rim = return_border(border_of(frame), maps, place, link_row, turn_row)
+        _, rim_back = jax.vjp(rim_of, jnp.zeros((height, breadth, width_out), jnp.float32))
+        (rim_add,) = rim_back(own_rim)
+        grad_act = frame[1:-1, 1:-1] + rim_add
+        slope = gelu_slope(pre_one.reshape(height, breadth, width_out))
+        return (grad_act * slope).astype(jnp.bfloat16)
+
     faces = lax.axis_size("face")
-    gathered = faces * tiles * (padded_tile_in.size + grad_one.size) * 2
+    gathered = faces * tiles * (padded_tile_in.size + grad_one_size(frame)) * 2
     if gathered <= factor_budget:
         total_out = lax.psum(grad_w_out, ("face", "tile"))
-        every_pad = gather_all(padded_tile_in[None], faces)
-        every_grad = gather_all(grad_one.reshape(1, -1, width_out), faces)
-        every_grad = every_grad.reshape(-1, width_out)
-        blocks = []
-        for down_step in range(3):
-            for side_step in range(3):
-                window = every_pad[:, down_step : down_step + height, side_step : side_step + breadth]
-                blocks.append(
-                    lax.dot_general(
-                        window.reshape(-1, width_in),
-                        every_grad,
-                        (((0,), (0,)), ((), ())),
-                        preferred_element_type=jnp.float32,
+
+        def rest(frame):
+            grad_one = grad_hidden_of(frame)
+            every_pad = gather_all(padded_tile_in[None], faces)
+            every_grad = gather_all(grad_one.reshape(1, -1, width_out), faces)
+            every_grad = every_grad.reshape(-1, width_out)
+            blocks = []
+            for down_step in range(3):
+                for side_step in range(3):
+                    window = every_pad[:, down_step : down_step + height, side_step : side_step + breadth]
+                    blocks.append(
+                        lax.dot_general(
+                            window.reshape(-1, width_in),
+                            every_grad,
+                            (((0,), (0,)), ((), ())),
+                            preferred_element_type=jnp.float32,
+                        )
                     )
-                )
-        total_in = jnp.concatenate(blocks, axis=0)
+            return grad_one, jnp.concatenate(blocks, axis=0)
+
+        def skipped(frame):
+            return (
+                jnp.zeros((height, breadth, width_out), jnp.bfloat16),
+                jnp.zeros((9 * width_in, width_out), jnp.float32),
+            )
+
+        grad_one, total_in = lax.cond(place < tiles, rest, skipped, frame)
     else:
+        grad_one = grad_hidden_of(frame)
         grad_w_in = lax.dot_general(
             unfolded_in,
             grad_one.reshape(-1, width_out),

time: 348 us -> 287 us (0.82)
  waiting for transfers between devices: 132 us -> 39.1 us
  matrix products: 19.8 us -> 31.2 us
  local copies, waits for them, and re-layouts: 25.2 us -> 36 us
  blocking collectives: 118 us -> 124 us
    psum x1, waiting for transfers between devices: 104 us -> 21.4 us  [body(): total_out = lax.psum(grad_w_out, ('face', 'tile'))]
    ppermute x6, waiting for transfers between devices: 27.7 us -> 17.7 us  [gather_all(): parts.append(lax.ppermute(local, 'face', pairs))]
    all_gather x2, blocking collectives: 27.3 us -> 18.2 us  [padded_tile(): edge_set = lax.all_gather(edges, 'face', axis=0, tiled=True)]
    slice x1 -> x10, local copies, waits for them, and re-layouts: 8.93 us -> 16.1 us  [rest(): every_pad[:, down_step:down_step + height, side_step:side_step + breadth]]
    cond x0 -> x15, local copies, waits for them, and re-layouts: none -> 6.67 us
    all_gather x2, blocking collectives: 33.5 us -> 40 us  [gather_all(): local = lax.all_gather(block, 'tile', axis=0, tiled=True)]
    dot_general x9, matrix products: 9.52 us -> 15.8 us  [rest(): lax.dot_general(window.reshape(-1, width_in), every_grad, (((0,), (0,)),...]
    all_gather x1, blocking collectives: 11.7 us -> 17.4 us  [return_border(): seam_set = lax.all_gather(seam_sum, 'face', axis=0, tiled=True)]
  transfers between devices with their start and end apart: 7 -> 7, of which waited for: 4 -> 3; matrix products, arithmetic and copies ran while one was open for 13% -> 22% of each run, Pallas kernels for 0% -> 0%
where the time goes in v7:
time: 287 us; the launch traced here: 285 us
  blocking collectives  124 us (43%)
  waiting for transfers between devices  39.1 us (14%)
  local copies, waits for them, and re-layouts  36 us (13%)
  other arithmetic  31.8 us (11%)
  matrix products  31.2 us (11%)
  between operations  15.1 us (5%)
  starting transfers between devices  7.12 us (2%)
    all_gather x2, blocking collectives, gather_all(): local = lax.all_gather(block, 'tile', axis=0, tiled=True)  40 us
    all_gather x2, blocking collectives, padded_tile(): rims = lax.all_gather(rim_of(cells), 'tile', axis=0, tiled=True)  30.2 us
    psum x1, waiting for transfers between devices, body(): total_out = lax.psum(grad_w_out, ('face', 'tile'))  21.4 us
    all_gather x1, blocking collectives, return_border(): borders = lax.all_gather(border, 'tile', axis=0, tiled=True)  18.4 us
    all_gather x2, blocking collectives, padded_tile(): edge_set = lax.all_gather(edges, 'face', axis=0, tiled=True)  18.2 us
    ppermute x6, waiting for transfers between devices, gather_all(): parts.append(lax.ppermute(local, 'face', pairs))  17.7 us
    all_gather x1, blocking collectives, return_border(): seam_set = lax.all_gather(seam_sum, 'face', axis=0, tiled=True)  17.4 us
    slice x10, local copies, waits for them, and re-layouts, rest(): every_pad[:, down_step:down_step + height, side_step:side_step + breadth]  16.1 us
  transfers between devices with their start and end apart: 7, of which 3 were waited for; matrix products, arithmetic and copies ran while one was open for 22% of the time, Pallas kernels for 0%

profile of v7, /device:TPU:0, one launch (start us, length us, event | category | flops | bytes accessed | tf_op | source)
XLA Modules:
  0.0 285.3 jit_solution(8133159285122954245)
XLA Ops:
  7.2 0.9 slice_bitcast_fusion.9
  8.1 0.9 copy.133
  9.0 0.7 constant_dynamic-slice_fusion
  11.0 15.9 %all_gather.24 = bf16[384,192]{1,0:T(8,128)(2,1)S(1)} all-gather(bf16[48,192]{1,0:T(8,128)(2,1)S(1)} %pad_maximum_fusion.9), channel_id=1, replica_groups=mesh['face'=4,'tile'=8] {'tile'}, dimensions={0}, use_global_device_ids=true | all-gather | bytes 165888 | tf_op jit(solution)/shard_map/all_gather | solution.py:96
  27.0 0.9 convolution_convert_fusion.1
  28.0 8.7 %all_gather.25 = bf16[512,192]{0,1:T(8,128)(2,1)S(1)} all-gather(bf16[128,192]{0,1:T(8,128)(2,1)S(1)} %convolution_convert_fusion.1), channel_id=1, replica_groups=mesh['face'=4,'tile'=8] {'face'}, dimensions={0}, use_global_device_ids=true | all-gather | bytes 245760 | tf_op jit(solution)/shard_map/all_gather | solution.py:102
  36.7 5.7 %compare_select_fusion.9 = s32[52]{0:T(128)S(1)} fusion(s32[8,52]{1,0:T(8,128)} %constant.173.clone, s32[]{:T(128)S(6)} %select_n.220, s32[8,52]{1,0:T(8,128)} %constant.174.clone, s32[]{:T(128)} %bitcast.52, s32[]{:T(128)} %bitcast.51, s32[]{:T(128)} %bitcast.50, s32[]{:T(128)} %bitcast.49, s32[]{:T(128)} %bitcast.48, s32[]{:T(128)} %bitcast.47, ...), kind=kLoop, calls=%fused_computation.131 | loop fusion | flops 1820 | bytes 660 | tf_op jit(solution)/shard_map/jit(_where)/select_n | solution.py:107
  46.0 1.1 concatenate.80
  47.1 1.7 multiply_convert_fusion.2
  49.0 14.3 %all_gather.26 = bf16[384,384]{1,0:T(8,128)(2,1)S(1)} all-gather(bf16[48,384]{1,0:T(8,128)(2,1)S(1)} %pad_maximum_fusion.8), channel_id=1, replica_groups=mesh['face'=4,'tile'=8] {'tile'}, dimensions={0}, use_global_device_ids=true | all-gather | bytes 331776 | tf_op jit(solution)/shard_map/all_gather | solution.py:96
  63.3 0.9 convolution_convert_fusion
  64.2 9.5 %all_gather.27 = bf16[512,384]{1,0:T(8,128)(2,1)S(1)} all-gather(bf16[128,384]{1,0:T(8,128)(2,1)S(1)} %convolution_convert_fusion), channel_id=1, replica_groups=mesh['face'=4,'tile'=8] {'face'}, dimensions={0}, use_global_device_ids=true | all-gather | bytes 491520 | tf_op jit(solution)/shard_map/all_gather | solution.py:102
  73.7 0.9 convolution_convert_fusion.2
  76.0 3.3 %fusion.28 = f32[3456,384]{1,0:T(8,128)} fusion(bf16[128,3456]{1,0:T(8,128)(2,1)S(1)} %constant_dynamic-update-slice_fusion.4, f32[128,384]{1,0:T(8,128)S(1)} %fusion.76, bf16[128,384]{1,0:T(8,128)(2,1)S(1)} %bitcast.222), kind=kOutput, calls=%fused_computation.78 | convolution fusion | flops 340279296 | bytes 6488064 | tf_op jit(solution)/shard_map/dot_general | solution.py:196
  80.0 2.1 fusion.30
  82.1 162.2 %conditional.1 = (f32[1728,384]{1,0:T(8,128)}, bf16[1,1,8,16,384]{4,3,2,1,0:T(8,128)(2,1)}, f32[]{:T(128)}) conditional(s32[]{:T(128)} %convert_element_type.61, () %tuple.20, (bf16[10,18,192]{2,0,1:T(8,128)(2,1)S(1)}, f32[128,3456]{1,0:T(8,128)}, s32[]{:T(128)}, (), (), /*index=5*/s32[1,4]{1,0:T(1,128)}, s32[1,4]{1,0:T(1,128)}, (), ...), branch_computations={%region_0.1_spmd, %region_1.3_spmd} | conditional | flops 5893907968 | bytes 165965888 | solution.py:248
  82.2 22.9 %all-gather = bf16[80,18,192]{2,1,0:T(8,128)(2,1)S(1)} all-gather(bf16[10,18,192]{2,1,0:T(8,128)(2,1)S(1)} %copy.122), channel_id=2, replica_groups=mesh['face'=4,'tile'=8] {'tile'}, dimensions={0}, use_global_device_ids=true | all-gather | bytes 622080 | tf_op jit(solution)/shard_map/cond/branch_1_fun/all_gather | solution.py:165
  105.0 1.1 constant_dynamic-update-slice_fusion.3
  106.4 1.5 collective-permute-start
  107.9 1.4 collective-permute-start.2
  111.4 0.7 copy_bitcast_fusion
  112.1 0.8 maximum_bitcast_fusion
  112.9 18.4 %all-gather.1 = f32[8,52,384]{2,1,0:T(8,128)} all-gather(f32[1,52,384]{2,1,0:T(8,128)S(1)} %maximum_bitcast_fusion), channel_id=1, replica_groups=mesh['face'=4,'tile'=8] {'tile'}, dimensions={0}, use_global_device_ids=true | all-gather | bytes 718848 | tf_op jit(solution)/shard_map/cond/branch_1_fun/all_gather | solution.py:127
  131.3 2.0 reshape.328
  133.3 1.5 fusion
  134.9 17.4 %all_gather.18 = f32[512,384]{1,0:T(8,128)} all-gather(f32[128,384]{1,0:T(8,128)S(1)} %fusion), channel_id=1, replica_groups=mesh['face'=4,'tile'=8] {'face'}, dimensions={0}, use_global_device_ids=true | all-gather | bytes 983040 | tf_op jit(solution)/shard_map/cond/branch_1_fun/all_gather | solution.py:133
  152.3 1.5 fusion.66
  153.8 1.5 fusion.8
  155.2 5.9 %bitcast_select_fusion = s32[48]{0:T(128)S(1)} fusion(s32[8,48]{1,0:T(8,128)} %constant.177.clone.1, s32[]{:T(128)S(6)} %select_n.192, s32[]{:T(128)} %bitcast.25, s32[]{:T(128)} %bitcast.24, s32[]{:T(128)} %bitcast.23, s32[]{:T(128)} %bitcast.22, s32[]{:T(128)} %bitcast.21, s32[]{:T(128)} %bitcast.20, s32[]{:T(128)} %bitcast.19, s32[]{:T(128)} %bitcast.18), kind=kLoop, calls=%fused_computation.43 | loop fusion | flops 1536 | bytes 420 | tf_op jit(solution)/shard_map/cond/branch_1_fun/jit(_where)/select_n | solution.py:140
  161.2 1.5 convolution_add_fusion
  162.8 0.8 fusion.6
  163.5 17.1 %all_gather.19 = bf16[8,128,384]{2,1,0:T(8,128)(2,1)} all-gather(bf16[1,128,384]{2,1,0:T(8,128)(2,1)} %bitcast.29), channel_id=1, replica_groups=mesh['face'=4,'tile'=8] {'tile'}, dimensions={0}, use_global_device_ids=true | all-gather | bytes 884736 | tf_op jit(solution)/shard_map/cond/branch_1_fun/all_gather | solution.py:165
  180.6 1.4 collective-permute-start.5
  182.1 2.0 collective-permute-start.4
  184.6 1.2 constant_dynamic-update-slice_fusion.2
  185.8 1.2 constant_dynamic-update-slice_fusion.1
  187.1 1.2 constant_dynamic-update-slice_fusion
  188.3 3.6 %fusion.62 = (bf16[32,8,16,192]{3,0,2,1:T(8,128)(2,1)}, bf16[32,8,16,192]{3,0,2,1:T(8,128)(2,1)}, bf16[32,8,16,192]{3,0,2,1:T(8,128)(2,1)}, bf16[32,8,16,192]{3,...) fusion(bf16[32,10,18,192]{3,0,2,1:T(8,128)(2,1)S(1)} %constant_, ...), kind=kLoop, calls=%fused_computation.165 | loop fusion | bytes 28311552 | tf_op jit(solution)/shard_map/cond/branch_1_fun/slice | solution.py:231
  191.9 2.9 %copy.101 = bf16[32,8,16,192]{3,2,1,0:T(8,128)(2,1)S(1)} copy(bf16[32,8,16,192]{3,0,2,1:T(8,128)(2,1)} %get-tuple-element.136) | data formatting | bytes 3145728 | tf_op jit(solution)/shard_map/cond/branch_1_fun/slice | solution.py:231
  194.8 1.2 copy.100
  196.4 1.2 copy.99
  197.6 1.2 copy.98
  198.8 1.2 copy.97
  200.0 1.2 copy.96
  201.2 1.2 copy.95
  202.4 1.2 copy.94
  203.6 1.2 copy.93
  204.8 15.4 %collective-permute-done.4 = bf16[8,128,384]{2,1,0:T(8,128)(2,1)} collective-permute-done((bf16[8,128,384]{2,1,0:T(8,128)(2,1)}, bf16[8,128,384]{2,1,0:T(8,128)(2,1)}, u32[]{:S(2)}, u32[]{:S(2)}) %collective-permute-start.4) | collective-permute-done | bytes 786464 | tf_op jit(solution)/shard_map/cond/branch_1_fun/ppermute | solution.py:169
  220.2 2.3 collective-permute-done.3
  222.5 2.3 pad_maximum_fusion
  224.9 1.8 convolution_dynamic-update-slice_fusion.8
  226.6 1.8 convolution_dynamic-update-slice_fusion.7
  228.4 1.8 convolution_dynamic-update-slice_fusion.6
  230.1 1.8 convolution_dynamic-update-slice_fusion.5
  231.9 1.8 convolution_dynamic-update-slice_fusion.4
  233.6 1.8 convolution_dynamic-update-slice_fusion.3
  235.4 1.8 convolution_dynamic-update-slice_fusion.2
  237.1 1.8 convolution_dynamic-update-slice_fusion.1
  238.9 1.8 convolution_dynamic-update-slice_fusion
  240.6 3.1 %multiply_reduce_fusion = f32[]{:T(128)} fusion(f32[1728,384]{1,0:T(8,128)} %convolution_dynamic-update-slice_fusion), kind=kLoop, calls=%fused_computation.1 | loop fusion | flops 1327103 | bytes 2654212 | tf_op jit(solution)/shard_map/reduce_sum | solution.py:261
  244.4 21.4 %all-reduce.15.cloned.1.call-done = f32[3456,384]{1,0:T(8,128)} async-done(((f32[3456,384]{1,0:T(8,128)}), f32[3456,384]{1,0:T(8,128)}) %all-reduce.15.cloned.1.call-update) | async-done | bytes 5308432 | tf_op jit(solution)/shard_map/psum | solution.py:221
  265.7 4.5 %multiply_reduce_fusion.1 = f32[]{:T(128)} fusion(f32[3456,384]{1,0:T(8,128)} %all-reduce.15.cloned.1.call-done), kind=kLoop, calls=%fused_computation.58 | loop fusion | flops 2654207 | bytes 5308420 | tf_op jit(solution)/shard_map/reduce_sum | solution.py:261
  270.9 3.2 %multiply_convert_fusion.1 = bf16[1728,384]{1,0:T(8,128)(2,1)} fusion(f32[1728,384]{1,0:T(8,128)} %get-tuple-element.90, f32[]{:T(128)S(6)} %rsqrt.3), kind=kLoop, calls=%fused_computation.59 | loop fusion | flops 1327104 | bytes 3981316 | tf_op jit(solution)/shard_map/convert_element_type | solution.py:263
  274.1 4.4 %multiply_convert_fusion = bf16[3456,384]{1,0:T(8,128)(2,1)} fusion(f32[3456,384]{1,0:T(8,128)} %all-reduce.15.cloned.1.call-done, f32[]{:T(128)S(6)} %rsqrt.3), kind=kLoop, calls=%fused_computation.57 | loop fusion | flops 2654208 | bytes 7962628 | tf_op jit(solution)/shard_map/convert_element_type | solution.py:264
  (96 shorter events, 10.2 us)
Async XLA Ops:
  7.2 68.1 %copy-start = (bf16[3,3,384,384]{3,2,1,0:T(8,128)(2,1)S(1)}, bf16[3,3,384,384]{3,2,1,0:T(8,128)(2,1)}, u32[]{:S(2)}) copy-start(bf16[3,3,384,384]{3,2,1,0:T(8,128)(2,1)} %param.17) | copy-start | bytes 7962628
  7.2 38.8 %copy-start.6 = (bf16[1,1,8,16,192]{4,3,2,1,0:T(8,128)(2,1)S(1)}, bf16[1,1,8,16,192]{4,3,2,1,0:T(8,128)(2,1)}, u32[]{:S(2)}) copy-start(bf16[1,1,8,16,192]{4,3,2,1,0:T(8,128)(2,1)} %param.14) | copy-start | bytes 147460
  7.2 258.5 %all-reduce.15.cloned.1.call-start = ((), (), s32[]{:S(2)}) async-start(), calls=%async_computation | async-start | bytes 10616832 | tf_op jit(solution)/shard_map/psum | solution.py:221
  9.7 1.3 copy-start.11
  9.7 1.3 copy-start.13
  42.5 0.6 copy-start.15
  42.8 0.6 copy-start.7
  42.8 0.6 copy-start.9
  75.1 0.9 copy-start.5
  79.3 0.7 copy-start.8
  79.3 0.7 copy-start.10
  82.1 27.2 %copy-start.4 = (f32[128,3456]{1,0:T(8,128)S(1)}, f32[128,3456]{1,0:T(8,128)}, u32[]{:S(2)}) copy-start(f32[128,3456]{1,0:T(8,128)} %get-tuple-element.75) | copy-start | bytes 5308420 | tf_op jit(solution)/shard_map/cond
  106.2 79.7 %collective-permute-start.1 = (bf16[8,10,18,192]{3,0,2,1:T(8,128)(2,1)}, bf16[8,10,18,192]{3,0,2,1:T(8,128)(2,1)}, u32[]{:S(2)}, u32[]{:S(2)}) collective-permute-start(bf16[8,10,18,192]{3,0,2,1:T(8,128)(2,1)} %get-tuple-element.135), channel_id=1, source_target_pairs={{0,16},{8,24},{16,0},{24,8},{1,17},{9,25},{17,1},{25,9},{2,18},{10... | collective-permute-start | bytes 1658888 | tf_op jit(solution)/shard_map/cond/branch_1_fun/ppermute | solution.py:169
  106.4 77.7 %collective-permute-start = (bf16[8,10,18,192]{3,0,2,1:T(8,128)(2,1)}, bf16[8,10,18,192]{3,0,2,1:T(8,128)(2,1)}, u32[]{:S(2)}, u32[]{:S(2)}) collective-permute-start(bf16[8,10,18,192]{3,0,2,1:T(8,128)(2,1)} %get-tuple-element.135), channel_id=1, source_target_pairs={{0,8},{8,16},{16,24},{24,0},{1,9},{9,17},{17,25},{25,1},{2,10},{10... | collective-permute-start | bytes 1658888 | tf_op jit(solution)/shard_map/cond/branch_1_fun/ppermute | solution.py:169
  107.9 79.2 %collective-permute-start.2 = (bf16[8,10,18,192]{3,0,2,1:T(8,128)(2,1)}, bf16[8,10,18,192]{3,0,2,1:T(8,128)(2,1)}, u32[]{:S(2)}, u32[]{:S(2)}) collective-permute-start(bf16[8,10,18,192]{3,0,2,1:T(8,128)(2,1)} %get-tuple-element.135), channel_id=1, source_target_pairs={{0,24},{8,0},{16,8},{24,16},{1,25},{9,1},{17,9},{25,17},{2,26},{10... | collective-permute-start | bytes 1658888 | tf_op jit(solution)/shard_map/cond/branch_1_fun/ppermute | solution.py:169
  109.6 42.6 %copy-start.12 = (s32[1,4]{1,0:T(1,128)S(1)}, s32[1,4]{1,0:T(1,128)}, u32[]{:S(2)}) copy-start(s32[1,4]{1,0:T(1,128)} %get-tuple-element.80) | copy-start | bytes 52 | tf_op jit(solution)/shard_map/cond
  112.9 40.8 %copy-start.14 = (s32[48]{0:T(128)S(1)}, s32[48]{0:T(128)}, u32[]{:S(2)}) copy-start(s32[48]{0:T(128)} %iota_add_fusion) | copy-start | bytes 580 | tf_op jit(solution)/shard_map/cond
  180.6 24.1 %collective-permute-start.5 = (bf16[8,128,384]{2,1,0:T(8,128)(2,1)}, bf16[8,128,384]{2,1,0:T(8,128)(2,1)}, u32[]{:S(2)}, u32[]{:S(2)}) collective-permute-start(bf16[8,128,384]{2,1,0:T(8,128)(2,1)} %all_gather.19), channel_id=1, source_target_pairs={{0,24},{8,0},{16,8},{24,16},{1,25},{9,1},{17,9},{25,17},{2,26},{10... | collective-permute-start | bytes 2359304 | tf_op jit(solution)/shard_map/cond/branch_1_fun/ppermute | solution.py:169
  182.1 38.1 %collective-permute-start.4 = (bf16[8,128,384]{2,1,0:T(8,128)(2,1)}, bf16[8,128,384]{2,1,0:T(8,128)(2,1)}, u32[]{:S(2)}, u32[]{:S(2)}) collective-permute-start(bf16[8,128,384]{2,1,0:T(8,128)(2,1)} %all_gather.19), channel_id=1, source_target_pairs={{0,16},{8,24},{16,0},{24,8},{1,17},{9,25},{17,1},{25,9},{2,18},{10... | collective-permute-start | bytes 2359304 | tf_op jit(solution)/shard_map/cond/branch_1_fun/ppermute | solution.py:169
  184.1 38.4 %collective-permute-start.3 = (bf16[8,128,384]{2,1,0:T(8,128)(2,1)}, bf16[8,128,384]{2,1,0:T(8,128)(2,1)}, u32[]{:S(2)}, u32[]{:S(2)}) collective-permute-start(bf16[8,128,384]{2,1,0:T(8,128)(2,1)} %all_gather.19), channel_id=1, source_target_pairs={{0,8},{8,16},{16,24},{24,0},{1,9},{9,17},{17,25},{25,1},{2,10},{10... | collective-permute-start | bytes 2359304 | tf_op jit(solution)/shard_map/cond/branch_1_fun/ppermute | solution.py:169
  191.9 2.9 %copy-start.3 = (bf16[32,8,16,192]{3,0,2,1:T(8,128)(2,1)S(1)}, bf16[32,8,16,192]{3,0,2,1:T(8,128)(2,1)}, u32[]{:S(2)}) copy-start(bf16[32,8,16,192]{3,0,2,1:T(8,128)(2,1)} %get-tuple-element.137) | copy-start | bytes 4718596 | tf_op jit(solution)/shard_map/cond
  194.8 1.6 copy-start.2
  270.9 7.6 %copy-start.1 = (bf16[3,3,384,384]{3,2,1,0:T(8,128)(2,1)S(1)}, bf16[3,3,384,384]{3,2,1,0:T(8,128)(2,1)}, u32[]{:S(2)}) copy-start(bf16[3,3,384,384]{3,2,1,0:T(8,128)(2,1)} %param.17) | copy-start | bytes 7962628
Sparse Core Ops, SparseCore 0:
  79.4 186.2 all-reduce.14

commit v8 on v7

--- a/solution.py
+++ b/solution.py
@@ -68,7 +68,11 @@
     edge = ((ei // height) * across + ej // breadth) * rim_len + k
     edge_of_rim = np.full((tiles, rim_len), -1)
     edge_of_rim[edge // rim_len, edge % rim_len] = np.arange(4 * side)
-    maps = (intra, seam_cell, edge, edge_of_rim)
+    rim_side = np.where(edge_of_rim >= 0, edge_of_rim // side, -1)
+    rim_pos = np.where(edge_of_rim >= 0, edge_of_rim % side, 0)
+    frame_side = np.where(seam, s, -1)
+    frame_pos = np.where(seam, p, 0)
+    maps = (intra, seam_cell, edge, frame_side, frame_pos, rim_side, rim_pos)
     return tuple(m.astype(np.int32) for m in maps)
 
 
@@ -76,20 +80,30 @@
     return (rows[:, None] == cols[None, :]).astype(dtype)
 
 
-def seam_source(cell, link_row, turn_row, side):
-    which = cell // side
-    pos = cell % side
-    link = jnp.zeros_like(cell)
-    turn = jnp.zeros_like(cell)
+def seam_source(which, pos, link_row, turn_row, side):
+    link = jnp.full_like(which, -1)
+    turn = jnp.zeros_like(which)
     for k in range(4):
         link = jnp.where(which == k, link_row[k], link)
         turn = jnp.where(which == k, turn_row[k], turn)
-    return link * side + jnp.where(turn == 1, side - 1 - pos, pos)
-
-
-def padded_tile(cells, maps, place, link_row, turn_row):
+    glued = link * side + jnp.where(turn == 1, side - 1 - pos, pos)
+    return jnp.where(which >= 0, glued, -1)
+
+
+def halo_source(maps, place, link_row, turn_row):
+    intra, _, edge, frame_side, frame_pos, _, _ = maps
+    tiles, frame_len = intra.shape
+    rim_len = frame_len - 4
+    side = edge.shape[0] // 4
+    pick = lambda table: lax.dynamic_index_in_dim(jnp.asarray(table), place, 0, False)
+    glued = seam_source(pick(frame_side), pick(frame_pos), link_row, turn_row, side)
+    own_intra = pick(intra)
+    return jnp.where(own_intra >= 0, own_intra, jnp.where(glued >= 0, tiles * rim_len + glued, -1))
+
+
+def padded_tile(cells, maps, source):
     height, breadth, depth = cells.shape
-    intra, seam_cell, edge, _ = maps
+    intra, seam_cell, edge = maps[:3]
     rim_len = 2 * (height + breadth)
     tiles = intra.shape[0]
     side = edge.shape[0] // 4
@@ -100,11 +114,7 @@
         preferred_element_type=jnp.float32,
     ).astype(cells.dtype)
     edge_set = lax.all_gather(edges, "face", axis=0, tiled=True)
-    own_intra = lax.dynamic_index_in_dim(jnp.asarray(intra), place, 0, False)
-    own_seam = lax.dynamic_index_in_dim(jnp.asarray(seam_cell), place, 0, False)
     pool = jnp.concatenate([rims, edge_set], axis=0)
-    glued = tiles * rim_len + seam_source(jnp.maximum(own_seam, 0), link_row, turn_row, side)
-    source = jnp.where(own_intra >= 0, own_intra, jnp.where(own_seam >= 0, glued, -1))
     halo = jnp.dot(
         one_hot(source, jnp.arange(pool.shape[0]), cells.dtype),
         pool,
@@ -119,7 +129,7 @@
 
 
 def return_border(border, maps, place, link_row, turn_row):
-    intra, seam_cell, edge, edge_of_rim = maps
+    intra, seam_cell, edge, _, _, rim_side, rim_pos = maps
     tiles, frame_len = intra.shape
     rim_len = frame_len - 4
     side = edge.shape[0] // 4
@@ -135,9 +145,8 @@
     from_tiles = jnp.dot(
         one_hot(own_cells, jnp.asarray(intra.reshape(-1)), jnp.float32), borders, precision=exact
     )
-    own_edge = lax.dynamic_index_in_dim(jnp.asarray(edge_of_rim), place, 0, False)
-    glued = seam_source(jnp.maximum(own_edge, 0), link_row, turn_row, side)
-    glued = jnp.where(own_edge >= 0, glued, -1)
+    pick = lambda table: lax.dynamic_index_in_dim(jnp.asarray(table), place, 0, False)
+    glued = seam_source(pick(rim_side), pick(rim_pos), link_row, turn_row, side)
     from_seams = jnp.dot(
         one_hot(glued, jnp.arange(seam_set.shape[0]), jnp.float32), seam_set, precision=exact
     )
@@ -180,15 +189,14 @@
     link_row = lax.dynamic_index_in_dim(seam_link, face_pos, 0, False)
     turn_row = lax.dynamic_index_in_dim(seam_turn, face_pos, 0, False)
     maps = face_maps(tiles, height, breadth)
-    padded_tile_in = padded_tile(cells, maps, place, link_row, turn_row)
+    source = halo_source(maps, place, link_row, turn_row)
+    padded_tile_in = padded_tile(cells, maps, source)
     unfolded_in = unfold(padded_tile_in, height, breadth)
     pre_one = jnp.dot(
         unfolded_in, weight_in.reshape(-1, width_out), preferred_element_type=jnp.float32
     )
     act = gelu_value(pre_one).astype(jnp.bfloat16)
-    padded_act = padded_tile(
-        act.reshape(height, breadth, width_out), maps, place, link_row, turn_row
-    )
+    padded_act = padded_tile(act.reshape(height, breadth, width_out), maps, source)
     unfolded_act = unfold(padded_act, height, breadth)
     kernel_out = weight_out.reshape(-1, width_out)
     pre_two = jnp.dot(unfolded_act, kernel_out, preferred_element_type=jnp.float32)

time: 287 us -> 287 us (level)
  no operation moved by 1% of the time
where the time goes in v8:
time: 287 us; the launch traced here: 286 us
  blocking collectives  124 us (43%)
  waiting for transfers between devices  39.4 us (14%)
  local copies, waits for them, and re-layouts  36 us (13%)
  other arithmetic  31.8 us (11%)
  matrix products  31.2 us (11%)
  between operations  15.1 us (5%)
  starting transfers between devices  7.17 us (2%)
    all_gather x2, blocking collectives, gather_all(): local = lax.all_gather(block, 'tile', axis=0, tiled=True)  40 us
    all_gather x2, blocking collectives, padded_tile(): rims = lax.all_gather(rim_of(cells), 'tile', axis=0, tiled=True)  30.2 us
    psum x1, waiting for transfers between devices, body(): total_out = lax.psum(grad_w_out, ('face', 'tile'))  21.7 us
    all_gather x2, blocking collectives, padded_tile(): edge_set = lax.all_gather(edges, 'face', axis=0, tiled=True)  18.2 us
    all_gather x1, blocking collectives, return_border(): borders = lax.all_gather(border, 'tile', axis=0, tiled=True)  18 us
    all_gather x1, blocking collectives, return_border(): seam_set = lax.all_gather(seam_sum, 'face', axis=0, tiled=True)  17.8 us
    ppermute x6, waiting for transfers between devices, gather_all(): parts.append(lax.ppermute(local, 'face', pairs))  17.7 us
    slice x10, local copies, waits for them, and re-layouts, rest(): every_pad[:, down_step:down_step + height, side_step:side_step + breadth]  16.1 us
  transfers between devices with their start and end apart: 7, of which 3 were waited for; matrix products, arithmetic and copies ran while one was open for 22% of the time, Pallas kernels for 0%

profile of v8, /device:TPU:0, one launch (start us, length us, event | category | flops | bytes accessed | tf_op | source)
XLA Modules:
  0.0 285.8 jit_solution(18189232685469076121)
XLA Ops:
  7.2 0.9 slice_bitcast_fusion.9
  8.1 0.9 copy.136
  9.0 0.7 constant_dynamic-slice_fusion.1
  11.0 15.9 %all_gather.24 = bf16[384,192]{1,0:T(8,128)(2,1)S(1)} all-gather(bf16[48,192]{1,0:T(8,128)(2,1)S(1)} %pad_maximum_fusion.9), channel_id=1, replica_groups=mesh['face'=4,'tile'=8] {'tile'}, dimensions={0}, use_global_device_ids=true | all-gather | bytes 165888 | tf_op jit(solution)/shard_map/all_gather | solution.py:110
  27.0 0.9 convolution_convert_fusion.1
  28.0 8.7 %all_gather.25 = bf16[512,192]{0,1:T(8,128)(2,1)S(1)} all-gather(bf16[128,192]{0,1:T(8,128)(2,1)S(1)} %convolution_convert_fusion.1), channel_id=1, replica_groups=mesh['face'=4,'tile'=8] {'face'}, dimensions={0}, use_global_device_ids=true | all-gather | bytes 245760 | tf_op jit(solution)/shard_map/all_gather | solution.py:116
  36.7 5.7 %compare_select_fusion.8 = s32[52]{0:T(128)S(1)} fusion(s32[8,52]{1,0:T(8,128)} %constant.123.clone, s32[]{:T(128)S(6)} %select_n.196, s32[8,52]{1,0:T(8,128)} %constant.122.clone, s32[8,52]{1,0:T(8,128)} %constant.121.clone, s32[]{:T(128)} %bitcast.47, s32[]{:T(128)} %bitcast.42, s32[]{:T(128)} %bitcast.50, s32[]{:T(128)} %bitcast.49, s32[]{:T(128)} %bitcast.48, ...), kind=kLoop, calls=%fused_computation.129 | loop fusion | flops 1248 | bytes 868 | tf_op jit(solution)/shard_map/jit(_where)/select_n | solution.py:101
  46.0 1.1 concatenate.80
  47.1 1.7 multiply_convert_fusion.2
  49.0 14.3 %all_gather.26 = bf16[384,384]{1,0:T(8,128)(2,1)S(1)} all-gather(bf16[48,384]{1,0:T(8,128)(2,1)S(1)} %pad_maximum_fusion.8), channel_id=1, replica_groups=mesh['face'=4,'tile'=8] {'tile'}, dimensions={0}, use_global_device_ids=true | all-gather | bytes 331776 | tf_op jit(solution)/shard_map/all_gather | solution.py:110
  63.3 0.9 convolution_convert_fusion
  64.2 9.5 %all_gather.27 = bf16[512,384]{1,0:T(8,128)(2,1)S(1)} all-gather(bf16[128,384]{1,0:T(8,128)(2,1)S(1)} %convolution_convert_fusion), channel_id=1, replica_groups=mesh['face'=4,'tile'=8] {'face'}, dimensions={0}, use_global_device_ids=true | all-gather | bytes 491520 | tf_op jit(solution)/shard_map/all_gather | solution.py:116
  73.7 0.9 convolution_convert_fusion.2
  76.0 3.3 %fusion.28 = f32[3456,384]{1,0:T(8,128)} fusion(bf16[128,3456]{1,0:T(8,128)(2,1)S(1)} %constant_dynamic-update-slice_fusion.4, f32[128,384]{1,0:T(8,128)S(1)} %fusion.77, bf16[128,384]{1,0:T(8,128)(2,1)S(1)} %bitcast.222), kind=kOutput, calls=%fused_computation.76 | convolution fusion | flops 340279296 | bytes 6488064 | tf_op jit(solution)/shard_map/dot_general | solution.py:204
  80.0 2.1 fusion.30
  82.1 162.3 %conditional.1 = (f32[1728,384]{1,0:T(8,128)}, bf16[1,1,8,16,384]{4,3,2,1,0:T(8,128)(2,1)}, f32[]{:T(128)}) conditional(s32[]{:T(128)} %convert_element_type.61, () %tuple.20, (bf16[10,18,192]{2,0,1:T(8,128)(2,1)S(1)}, f32[128,3456]{1,0:T(8,128)}, s32[]{:T(128)}, (), (), /*index=5*/s32[1,4]{1,0:T(1,128)}, s32[1,4]{1,0:T(1,128)}, (), (), ...), branch_computations={%region_0.1_spmd, %region_1.3_spmd} | conditional | flops 5893907456 | bytes 165966080 | solution.py:256
  82.2 22.9 %all-gather = bf16[80,18,192]{2,1,0:T(8,128)(2,1)S(1)} all-gather(bf16[10,18,192]{2,1,0:T(8,128)(2,1)S(1)} %copy.125), channel_id=2, replica_groups=mesh['face'=4,'tile'=8] {'tile'}, dimensions={0}, use_global_device_ids=true | all-gather | bytes 622080 | tf_op jit(solution)/shard_map/cond/branch_1_fun/all_gather | solution.py:174
  105.1 1.1 constant_dynamic-update-slice_fusion.3
  106.4 1.5 collective-permute-start
  107.8 1.4 collective-permute-start.2
  111.4 0.7 copy_bitcast_fusion
  112.1 0.8 maximum_bitcast_fusion
  112.9 18.0 %all-gather.1 = f32[8,52,384]{2,1,0:T(8,128)} all-gather(f32[1,52,384]{2,1,0:T(8,128)S(1)} %maximum_bitcast_fusion), channel_id=1, replica_groups=mesh['face'=4,'tile'=8] {'tile'}, dimensions={0}, use_global_device_ids=true | all-gather | bytes 718848 | tf_op jit(solution)/shard_map/cond/branch_1_fun/all_gather | solution.py:137
  130.9 2.0 reshape.374
  133.0 1.5 fusion
  134.5 17.8 %all_gather.18 = f32[512,384]{1,0:T(8,128)} all-gather(f32[128,384]{1,0:T(8,128)S(1)} %fusion), channel_id=1, replica_groups=mesh['face'=4,'tile'=8] {'face'}, dimensions={0}, use_global_device_ids=true | all-gather | bytes 983040 | tf_op jit(solution)/shard_map/cond/branch_1_fun/all_gather | solution.py:143
  152.3 1.5 fusion.67
  153.8 1.5 fusion.8
  155.3 5.9 %bitcast_select_fusion.1 = s32[48]{0:T(128)S(1)} fusion(s32[8,48]{1,0:T(8,128)} %constant.128.clone.1, s32[]{:T(128)S(6)} %select_n.167, s32[8,48]{1,0:T(8,128)} %constant.127.clone.1, s32[]{:T(128)} %bitcast.20, s32[]{:T(128)} %bitcast.15, s32[]{:T(128)} %bitcast.23, s32[]{:T(128)} %bitcast.22, s32[]{:T(128)} %bitcast.21, s32[]{:T(128)} %bitcast.18, ...), kind=kLoop, calls=%fused_computation.42 | loop fusion | flops 912 | bytes 612 | tf_op jit(solution)/shard_map/cond/branch_1_fun/jit(_where)/select_n | solution.py:90
  161.2 1.5 convolution_add_fusion
  162.8 0.8 fusion.6
  163.6 17.1 %all_gather.19 = bf16[8,128,384]{2,1,0:T(8,128)(2,1)} all-gather(bf16[1,128,384]{2,1,0:T(8,128)(2,1)} %bitcast.29), channel_id=1, replica_groups=mesh['face'=4,'tile'=8] {'tile'}, dimensions={0}, use_global_device_ids=true | all-gather | bytes 884736 | tf_op jit(solution)/shard_map/cond/branch_1_fun/all_gather | solution.py:174
  180.6 1.2 collective-permute-start.5
  181.9 2.3 collective-permute-start.4
  184.7 1.2 constant_dynamic-update-slice_fusion.2
  185.9 1.2 constant_dynamic-update-slice_fusion.1
  187.1 1.2 constant_dynamic-update-slice_fusion
  188.4 3.6 %fusion.63 = (bf16[32,8,16,192]{3,0,2,1:T(8,128)(2,1)}, bf16[32,8,16,192]{3,0,2,1:T(8,128)(2,1)}, bf16[32,8,16,192]{3,0,2,1:T(8,128)(2,1)}, bf16[32,8,16,192]{3,...) fusion(bf16[32,10,18,192]{3,0,2,1:T(8,128)(2,1)S(1)} %constant_, ...), kind=kLoop, calls=%fused_computation.163 | loop fusion | bytes 28311552 | tf_op jit(solution)/shard_map/cond/branch_1_fun/slice | solution.py:239
  192.0 2.9 %copy.104 = bf16[32,8,16,192]{3,2,1,0:T(8,128)(2,1)S(1)} copy(bf16[32,8,16,192]{3,0,2,1:T(8,128)(2,1)} %get-tuple-element.145) | data formatting | bytes 3145728 | tf_op jit(solution)/shard_map/cond/branch_1_fun/slice | solution.py:239
  194.9 1.2 copy.103
  196.5 1.2 copy.102
  197.7 1.2 copy.101
  198.9 1.2 copy.100
  200.1 1.2 copy.99
  201.3 1.2 copy.98
  202.5 1.2 copy.97
  203.7 1.2 copy.96
  204.9 15.3 %collective-permute-done.4 = bf16[8,128,384]{2,1,0:T(8,128)(2,1)} collective-permute-done((bf16[8,128,384]{2,1,0:T(8,128)(2,1)}, bf16[8,128,384]{2,1,0:T(8,128)(2,1)}, u32[]{:S(2)}, u32[]{:S(2)}) %collective-permute-start.4) | collective-permute-done | bytes 786464 | tf_op jit(solution)/shard_map/cond/branch_1_fun/ppermute | solution.py:178
  220.2 2.4 collective-permute-done.3
  222.6 2.3 pad_maximum_fusion
  224.9 1.8 convolution_dynamic-update-slice_fusion.8
  226.7 1.8 convolution_dynamic-update-slice_fusion.7
  228.4 1.8 convolution_dynamic-update-slice_fusion.6
  230.2 1.8 convolution_dynamic-update-slice_fusion.5
  231.9 1.8 convolution_dynamic-update-slice_fusion.4
  233.7 1.8 convolution_dynamic-update-slice_fusion.3
  235.4 1.8 convolution_dynamic-update-slice_fusion.2
  237.2 1.8 convolution_dynamic-update-slice_fusion.1
  238.9 1.8 convolution_dynamic-update-slice_fusion
  240.7 3.1 %multiply_reduce_fusion = f32[]{:T(128)} fusion(f32[1728,384]{1,0:T(8,128)} %convolution_dynamic-update-slice_fusion), kind=kLoop, calls=%fused_computation.1 | loop fusion | flops 1327103 | bytes 2654212 | tf_op jit(solution)/shard_map/reduce_sum | solution.py:269
  244.5 21.7 %all-reduce.15.cloned.1.call-done = f32[3456,384]{1,0:T(8,128)} async-done(((f32[3456,384]{1,0:T(8,128)}), f32[3456,384]{1,0:T(8,128)}) %all-reduce.15.cloned.1.call-update) | async-done | bytes 5308432 | tf_op jit(solution)/shard_map/psum | solution.py:229
  266.2 4.5 %multiply_reduce_fusion.1 = f32[]{:T(128)} fusion(f32[3456,384]{1,0:T(8,128)} %all-reduce.15.cloned.1.call-done), kind=kLoop, calls=%fused_computation.56 | loop fusion | flops 2654207 | bytes 5308420 | tf_op jit(solution)/shard_map/reduce_sum | solution.py:269
  271.3 3.2 %multiply_convert_fusion.1 = bf16[1728,384]{1,0:T(8,128)(2,1)} fusion(f32[1728,384]{1,0:T(8,128)} %get-tuple-element.93, f32[]{:T(128)S(6)} %rsqrt.3), kind=kLoop, calls=%fused_computation.57 | loop fusion | flops 1327104 | bytes 3981316 | tf_op jit(solution)/shard_map/convert_element_type | solution.py:271
  274.5 4.4 %multiply_convert_fusion = bf16[3456,384]{1,0:T(8,128)(2,1)} fusion(f32[3456,384]{1,0:T(8,128)} %all-reduce.15.cloned.1.call-done, f32[]{:T(128)S(6)} %rsqrt.3), kind=kLoop, calls=%fused_computation.55 | loop fusion | flops 2654208 | bytes 7962628 | tf_op jit(solution)/shard_map/convert_element_type | solution.py:272
  (96 shorter events, 10.1 us)
Async XLA Ops:
  7.2 68.1 %copy-start = (bf16[3,3,384,384]{3,2,1,0:T(8,128)(2,1)S(1)}, bf16[3,3,384,384]{3,2,1,0:T(8,128)(2,1)}, u32[]{:S(2)}) copy-start(bf16[3,3,384,384]{3,2,1,0:T(8,128)(2,1)} %param.19) | copy-start | bytes 7962628
  7.2 38.8 %copy-start.6 = (bf16[1,1,8,16,192]{4,3,2,1,0:T(8,128)(2,1)S(1)}, bf16[1,1,8,16,192]{4,3,2,1,0:T(8,128)(2,1)}, u32[]{:S(2)}) copy-start(bf16[1,1,8,16,192]{4,3,2,1,0:T(8,128)(2,1)} %param.16) | copy-start | bytes 147460
  7.2 259.0 %all-reduce.15.cloned.1.call-start = ((), (), s32[]{:S(2)}) async-start(), calls=%async_computation | async-start | bytes 10616832 | tf_op jit(solution)/shard_map/psum | solution.py:229
  9.7 1.3 copy-start.11
  9.7 1.3 copy-start.13
  42.5 0.6 copy-start.15
  42.8 0.6 copy-start.7
  42.8 0.6 copy-start.9
  75.1 0.9 copy-start.5
  79.3 0.7 copy-start.8
  79.3 0.7 copy-start.10
  82.1 27.1 %copy-start.4 = (f32[128,3456]{1,0:T(8,128)S(1)}, f32[128,3456]{1,0:T(8,128)}, u32[]{:S(2)}) copy-start(f32[128,3456]{1,0:T(8,128)} %get-tuple-element.77) | copy-start | bytes 5308420 | tf_op jit(solution)/shard_map/cond
  106.2 79.7 %collective-permute-start.1 = (bf16[8,10,18,192]{3,0,2,1:T(8,128)(2,1)}, bf16[8,10,18,192]{3,0,2,1:T(8,128)(2,1)}, u32[]{:S(2)}, u32[]{:S(2)}) collective-permute-start(bf16[8,10,18,192]{3,0,2,1:T(8,128)(2,1)} %get-tuple-element.144), channel_id=1, source_target_pairs={{0,16},{8,24},{16,0},{24,8},{1,17},{9,25},{17,1},{25,9},{2,18},{10... | collective-permute-start | bytes 1658888 | tf_op jit(solution)/shard_map/cond/branch_1_fun/ppermute | solution.py:178
  106.4 77.8 %collective-permute-start = (bf16[8,10,18,192]{3,0,2,1:T(8,128)(2,1)}, bf16[8,10,18,192]{3,0,2,1:T(8,128)(2,1)}, u32[]{:S(2)}, u32[]{:S(2)}) collective-permute-start(bf16[8,10,18,192]{3,0,2,1:T(8,128)(2,1)} %get-tuple-element.144), channel_id=1, source_target_pairs={{0,8},{8,16},{16,24},{24,0},{1,9},{9,17},{17,25},{25,1},{2,10},{10... | collective-permute-start | bytes 1658888 | tf_op jit(solution)/shard_map/cond/branch_1_fun/ppermute | solution.py:178
  107.8 79.3 %collective-permute-start.2 = (bf16[8,10,18,192]{3,0,2,1:T(8,128)(2,1)}, bf16[8,10,18,192]{3,0,2,1:T(8,128)(2,1)}, u32[]{:S(2)}, u32[]{:S(2)}) collective-permute-start(bf16[8,10,18,192]{3,0,2,1:T(8,128)(2,1)} %get-tuple-element.144), channel_id=1, source_target_pairs={{0,24},{8,0},{16,8},{24,16},{1,25},{9,1},{17,9},{25,17},{2,26},{10... | collective-permute-start | bytes 1658888 | tf_op jit(solution)/shard_map/cond/branch_1_fun/ppermute | solution.py:178
  109.6 42.7 %copy-start.12 = (s32[1,4]{1,0:T(1,128)S(1)}, s32[1,4]{1,0:T(1,128)}, u32[]{:S(2)}) copy-start(s32[1,4]{1,0:T(1,128)} %get-tuple-element.82) | copy-start | bytes 52 | tf_op jit(solution)/shard_map/cond
  112.9 40.9 %copy-start.14 = (s32[48]{0:T(128)S(1)}, s32[48]{0:T(128)}, u32[]{:S(2)}) copy-start(s32[48]{0:T(128)} %iota_add_fusion) | copy-start | bytes 580 | tf_op jit(solution)/shard_map/cond
  180.6 24.2 %collective-permute-start.5 = (bf16[8,128,384]{2,1,0:T(8,128)(2,1)}, bf16[8,128,384]{2,1,0:T(8,128)(2,1)}, u32[]{:S(2)}, u32[]{:S(2)}) collective-permute-start(bf16[8,128,384]{2,1,0:T(8,128)(2,1)} %all_gather.19), channel_id=1, source_target_pairs={{0,24},{8,0},{16,8},{24,16},{1,25},{9,1},{17,9},{25,17},{2,26},{10... | collective-permute-start | bytes 2359304 | tf_op jit(solution)/shard_map/cond/branch_1_fun/ppermute | solution.py:178
  181.9 38.3 %collective-permute-start.4 = (bf16[8,128,384]{2,1,0:T(8,128)(2,1)}, bf16[8,128,384]{2,1,0:T(8,128)(2,1)}, u32[]{:S(2)}, u32[]{:S(2)}) collective-permute-start(bf16[8,128,384]{2,1,0:T(8,128)(2,1)} %all_gather.19), channel_id=1, source_target_pairs={{0,16},{8,24},{16,0},{24,8},{1,17},{9,25},{17,1},{25,9},{2,18},{10... | collective-permute-start | bytes 2359304 | tf_op jit(solution)/shard_map/cond/branch_1_fun/ppermute | solution.py:178
  184.1 38.4 %collective-permute-start.3 = (bf16[8,128,384]{2,1,0:T(8,128)(2,1)}, bf16[8,128,384]{2,1,0:T(8,128)(2,1)}, u32[]{:S(2)}, u32[]{:S(2)}) collective-permute-start(bf16[8,128,384]{2,1,0:T(8,128)(2,1)} %all_gather.19), channel_id=1, source_target_pairs={{0,8},{8,16},{16,24},{24,0},{1,9},{9,17},{17,25},{25,1},{2,10},{10... | collective-permute-start | bytes 2359304 | tf_op jit(solution)/shard_map/cond/branch_1_fun/ppermute | solution.py:178
  192.0 2.9 %copy-start.3 = (bf16[32,8,16,192]{3,0,2,1:T(8,128)(2,1)S(1)}, bf16[32,8,16,192]{3,0,2,1:T(8,128)(2,1)}, u32[]{:S(2)}) copy-start(bf16[32,8,16,192]{3,0,2,1:T(8,128)(2,1)} %get-tuple-element.146) | copy-start | bytes 4718596 | tf_op jit(solution)/shard_map/cond
  194.9 1.6 copy-start.2
  271.3 7.6 %copy-start.1 = (bf16[3,3,384,384]{3,2,1,0:T(8,128)(2,1)S(1)}, bf16[3,3,384,384]{3,2,1,0:T(8,128)(2,1)}, u32[]{:S(2)}) copy-start(bf16[3,3,384,384]{3,2,1,0:T(8,128)(2,1)} %param.19) | copy-start | bytes 7962628
Sparse Core Ops, SparseCore 0:
  79.4 186.7 all-reduce.14

commit v9 on v8

--- a/solution.py
+++ b/solution.py
@@ -233,19 +233,23 @@
             every_pad = gather_all(padded_tile_in[None], faces)
             every_grad = gather_all(grad_one.reshape(1, -1, width_out), faces)
             every_grad = every_grad.reshape(-1, width_out)
-            blocks = []
-            for down_step in range(3):
-                for side_step in range(3):
-                    window = every_pad[:, down_step : down_step + height, side_step : side_step + breadth]
-                    blocks.append(
-                        lax.dot_general(
-                            window.reshape(-1, width_in),
-                            every_grad,
-                            (((0,), (0,)), ((), ())),
-                            preferred_element_type=jnp.float32,
-                        )
-                    )
-            return grad_one, jnp.concatenate(blocks, axis=0)
+            def one_offset(step, blocks):
+                window = lax.dynamic_slice(
+                    every_pad,
+                    (0, step // 3, step % 3, 0),
+                    (every_pad.shape[0], height, breadth, width_in),
+                )
+                block = lax.dot_general(
+                    window.reshape(-1, width_in),
+                    every_grad,
+                    (((0,), (0,)), ((), ())),
+                    preferred_element_type=jnp.float32,
+                )
+                return lax.dynamic_update_index_in_dim(blocks, block, step, 0)
+
+            blocks = jnp.zeros((9, width_in, width_out), jnp.float32)
+            blocks = lax.fori_loop(0, 9, one_offset, blocks)
+            return grad_one, blocks.reshape(9 * width_in, width_out)
 
         def skipped(frame):
             return (

time: 287 us -> 294 us (1.024)
  local copies, waits for them, and re-layouts: 36 us -> 45.4 us
  waiting for transfers between devices: 39.4 us -> 32.2 us
  blocking collectives: 124 us -> 129 us
  other arithmetic: 31.8 us -> 35.5 us
    dynamic_slice x0 -> x18, local copies, waits for them, and re-layouts: none -> 26.7 us  [one_offset(): lax.dynamic_slice(every_pad, (0, step // 3, step % 3, 0), (every_pad.shap...]
    psum x1, waiting for transfers between devices: 21.7 us -> 0.02 us  [body(): total_out = lax.psum(grad_w_out, ('face', 'tile'))]
    slice x10 -> x0, local copies, waits for them, and re-layouts: 16.1 us -> none  [rest(): every_pad[:, down_step:down_step + height, side_step:side_step + breadth]]
    ppermute x6, waiting for transfers between devices: 17.7 us -> 32.1 us  [gather_all(): parts.append(lax.ppermute(local, 'face', pairs))]
    while x0 -> x18, local copies, waits for them, and re-layouts: none -> 6.79 us
    cond x15 -> x10, local copies, waits for them, and re-layouts: 6.68 us -> 1.88 us
    all_gather x1, blocking collectives: 17.8 us -> 22.3 us  [return_border(): seam_set = lax.all_gather(seam_sum, 'face', axis=0, tiled=True)]
    concatenate x1 -> x2, other arithmetic: 2.34 us -> 6.46 us  [gather_all(): return jnp.concatenate(parts, axis=0)]
  transfers between devices with their start and end apart: 7 -> 7, of which waited for: 3 -> 2; matrix products, arithmetic and copies ran while one was open for 22% -> 23% of each run, Pallas kernels for 0% -> 0%
where the time goes in v9:
time: 294 us; the launch traced here: 292 us
  blocking collectives  129 us (44%)
  local copies, waits for them, and re-layouts  45.4 us (15%)
  other arithmetic  35.5 us (12%)
  waiting for transfers between devices  32.2 us (11%)
  matrix products  28.5 us (10%)
  between operations  15.1 us (5%)
  starting transfers between devices  5.74 us (2%)
    all_gather x2, blocking collectives, gather_all(): local = lax.all_gather(block, 'tile', axis=0, tiled=True)  39.1 us
    ppermute x6, waiting for transfers between devices, gather_all(): parts.append(lax.ppermute(local, 'face', pairs))  32.1 us
    all_gather x2, blocking collectives, padded_tile(): rims = lax.all_gather(rim_of(cells), 'tile', axis=0, tiled=True)  30.2 us
    dynamic_slice x18, local copies, waits for them, and re-layouts, one_offset(): lax.dynamic_slice(every_pad, (0, step // 3, step % 3, 0), (every_pad.shap...  26.7 us
    all_gather x1, blocking collectives, return_border(): seam_set = lax.all_gather(seam_sum, 'face', axis=0, tiled=True)  22.3 us
    all_gather x1, blocking collectives, return_border(): borders = lax.all_gather(border, 'tile', axis=0, tiled=True)  18.9 us
    all_gather x2, blocking collectives, padded_tile(): edge_set = lax.all_gather(edges, 'face', axis=0, tiled=True)  18.2 us
    dot_general x9, matrix products, one_offset(): lax.dot_general(window.reshape(-1, width_in), every_grad, (((0,), (0,)),...  15.9 us
  transfers between devices with their start and end apart: 7, of which 2 were waited for; matrix products, arithmetic and copies ran while one was open for 23% of the time, Pallas kernels for 0%

profile of v9, /device:TPU:0, one launch (start us, length us, event | category | flops | bytes accessed | tf_op | source)
XLA Modules:
  0.0 292.1 jit_solution(5633782938913435334)
XLA Ops:
  7.2 0.9 slice_bitcast_fusion.9
  8.1 0.9 copy.103
  11.0 15.9 %all_gather.24 = bf16[384,192]{1,0:T(8,128)(2,1)S(1)} all-gather(bf16[48,192]{1,0:T(8,128)(2,1)S(1)} %pad_maximum_fusion.10), channel_id=1, replica_groups=mesh['face'=4,'tile'=8] {'tile'}, dimensions={0}, use_global_device_ids=true | all-gather | bytes 165888 | tf_op jit(solution)/shard_map/all_gather | solution.py:110
  27.0 0.9 convolution_convert_fusion.1
  28.0 8.7 %all_gather.25 = bf16[512,192]{0,1:T(8,128)(2,1)S(1)} all-gather(bf16[128,192]{0,1:T(8,128)(2,1)S(1)} %convolution_convert_fusion.1), channel_id=1, replica_groups=mesh['face'=4,'tile'=8] {'face'}, dimensions={0}, use_global_device_ids=true | all-gather | bytes 245760 | tf_op jit(solution)/shard_map/all_gather | solution.py:116
  36.7 5.9 %compare_select_fusion.8 = s32[52]{0:T(128)S(1)} fusion(s32[8,52]{1,0:T(8,128)} %constant.206.clone, s32[]{:T(128)S(6)} %select_n.257, s32[8,52]{1,0:T(8,128)} %constant.205.clone, s32[8,52]{1,0:T(8,128)} %constant.204.clone, s32[]{:T(128)} %bitcast.41, s32[]{:T(128)} %bitcast.36, s32[]{:T(128)} %bitcast.44, s32[]{:T(128)} %bitcast.43, s32[]{:T(128)} %bitcast.42, ...), kind=kLoop, calls=%fused_computation.120 | loop fusion | flops 1248 | bytes 868 | tf_op jit(solution)/shard_map/jit(_where)/select_n | solution.py:101
  45.8 1.1 concatenate.77
  46.9 1.7 multiply_convert_fusion.2
  48.7 14.3 %all_gather.26 = bf16[384,384]{1,0:T(8,128)(2,1)S(1)} all-gather(bf16[48,384]{1,0:T(8,128)(2,1)S(1)} %pad_maximum_fusion.9), channel_id=1, replica_groups=mesh['face'=4,'tile'=8] {'tile'}, dimensions={0}, use_global_device_ids=true | all-gather | bytes 331776 | tf_op jit(solution)/shard_map/all_gather | solution.py:110
  63.1 0.9 convolution_convert_fusion
  64.0 9.5 %all_gather.27 = bf16[512,384]{1,0:T(8,128)(2,1)S(1)} all-gather(bf16[128,384]{1,0:T(8,128)(2,1)S(1)} %convolution_convert_fusion), channel_id=1, replica_groups=mesh['face'=4,'tile'=8] {'face'}, dimensions={0}, use_global_device_ids=true | all-gather | bytes 491520 | tf_op jit(solution)/shard_map/all_gather | solution.py:116
  75.1 3.3 %fusion.29 = f32[3456,384]{1,0:T(8,128)} fusion(bf16[128,3456]{1,0:T(8,128)(2,1)S(1)} %constant_dynamic-update-slice_fusion, f32[128,384]{1,0:T(8,128)S(1)} %fusion.77, bf16[128,384]{1,0:T(8,128)(2,1)S(1)} %bitcast.195), kind=kOutput, calls=%fused_computation.67 | convolution fusion | flops 340279296 | bytes 6488064 | tf_op jit(solution)/shard_map/dot_general | solution.py:204
  78.5 2.1 fusion.31
  80.7 192.0 %conditional.1 = (f32[1728,384]{1,0:T(8,128)}, bf16[1,1,8,16,384]{4,3,2,1,0:T(8,128)(2,1)}, f32[]{:T(128)}) conditional(s32[]{:T(128)} %convert_element_type.61, () %tuple.42, (bf16[10,18,192]{2,0,1:T(8,128)(2,1)S(1)}, f32[128,3456]{1,0:T(8,128)}, s32[]{:T(128)}, (), (), /*index=5*/s32[1,4]{1,0:T(1,128)S(1)}, s32[1,4]{1,0:T(1,128)S(1)}, (), (), ...), branch_computations={%region_0.1_spmd, %region_1.5_spmd} | conditional | flops 1070916544 | bytes 76460856 | solution.py:260
  80.7 22.6 %all-gather = bf16[80,18,192]{2,1,0:T(8,128)(2,1)S(1)} all-gather(bf16[10,18,192]{2,1,0:T(8,128)(2,1)S(1)} %copy.92), channel_id=2, replica_groups=mesh['face'=4,'tile'=8] {'tile'}, dimensions={0}, use_global_device_ids=true | all-gather | bytes 622080 | tf_op jit(solution)/shard_map/cond/branch_1_fun/all_gather | solution.py:174
  103.3 1.1 copy.70
  104.4 1.4 collective-permute-start.2
  108.1 18.9 %all-gather.1 = f32[8,52,384]{2,1,0:T(8,128)} all-gather(f32[1,52,384]{2,1,0:T(8,128)S(1)} %maximum_bitcast_fusion), channel_id=1, replica_groups=mesh['face'=4,'tile'=8] {'tile'}, dimensions={0}, use_global_device_ids=true | all-gather | bytes 718848 | tf_op jit(solution)/shard_map/cond/branch_1_fun/all_gather | solution.py:137
  127.0 1.2 reshape.360
  128.6 22.3 %all_gather.18 = f32[512,384]{1,0:T(8,128)} all-gather(f32[128,384]{1,0:T(8,128)S(1)} %fusion.1), channel_id=1, replica_groups=mesh['face'=4,'tile'=8] {'face'}, dimensions={0}, use_global_device_ids=true | all-gather | bytes 983040 | tf_op jit(solution)/shard_map/cond/branch_1_fun/all_gather | solution.py:143
  151.9 5.9 %bitcast_select_fusion.1 = s32[48]{0:T(128)S(1)} fusion(s32[8,48]{1,0:T(8,128)} %constant.211.clone.1, s32[]{:T(128)S(6)} %select_n.228, s32[8,48]{1,0:T(8,128)} %constant.210.clone.1, s32[]{:T(128)} %bitcast.21, s32[]{:T(128)} %bitcast.16, s32[]{:T(128)} %bitcast.24, s32[]{:T(128)} %bitcast.23, s32[]{:T(128)} %bitcast.22, s32[]{:T(128)} %bitcast.19, ...), kind=kLoop, calls=%fused_computation.33 | loop fusion | flops 912 | bytes 612 | tf_op jit(solution)/shard_map/cond/branch_1_fun/jit(_where)/select_n | solution.py:90
  157.8 1.5 convolution_add_fusion
  159.4 1.7 fusion.7
  161.1 16.5 %all_gather.19 = bf16[8,128,384]{2,1,0:T(8,128)(2,1)S(1)} all-gather(bf16[1,128,384]{2,1,0:T(8,128)(2,1)} %bitcast.30), channel_id=1, replica_groups=mesh['face'=4,'tile'=8] {'tile'}, dimensions={0}, use_global_device_ids=true | all-gather | bytes 884736 | tf_op jit(solution)/shard_map/cond/branch_1_fun/all_gather | solution.py:174
  177.7 1.4 collective-permute-start.5
  179.0 1.2 collective-permute-start.4
  180.9 3.2 %pad_maximum_fusion.1 = bf16[32,10,18,192]{3,0,2,1:T(8,128)(2,1)} fusion(bf16[8,10,18,192]{3,0,2,1:T(8,128)(2,1)} %collective-permute-done.2, bf16[8,10,18,192]{3,0,2,1:T(8,128)(2,1)} %collective-permute-done.1, bf16[8,10,18,192]{3,0,2,1:T(8,128)(2,1)} %collective-permute-done, bf16[8,10,18,192]{3,0,2,1:T(8,128)(2,1)} %copy.70), kind=kLoop, calls=%fused_computation.4 | loop fusion | flops 8847360 | bytes 4423680 | tf_op jit(solution)/shard_map/cond/branch_1_fun/concatenate | solution.py:179
  184.1 14.3 %collective-permute-done.5 = bf16[8,128,384]{2,1,0:T(8,128)(2,1)} collective-permute-done((bf16[8,128,384]{2,1,0:T(8,128)(2,1)S(1)}, bf16[8,128,384]{2,1,0:T(8,128)(2,1)}, u32[]{:S(2)}, u32[]{:S(2)}) %collective-permute-start.5) | collective-permute-done | bytes 786464 | tf_op jit(solution)/shard_map/cond/branch_1_fun/ppermute | solution.py:178
  198.4 17.8 %collective-permute-done.4 = bf16[8,128,384]{2,1,0:T(8,128)(2,1)} collective-permute-done((bf16[8,128,384]{2,1,0:T(8,128)(2,1)S(1)}, bf16[8,128,384]{2,1,0:T(8,128)(2,1)}, u32[]{:S(2)}, u32[]{:S(2)}) %collective-permute-start.4) | collective-permute-done | bytes 786464 | tf_op jit(solution)/shard_map/cond/branch_1_fun/ppermute | solution.py:178
  216.2 3.2 %pad_maximum_fusion = bf16[32,128,384]{2,1,0:T(8,128)(2,1)} fusion(bf16[8,128,384]{2,1,0:T(8,128)(2,1)} %collective-permute-done.5, bf16[8,128,384]{2,1,0:T(8,128)(2,1)} %collective-permute-done.4, bf16[8,128,384]{2,1,0:T(8,128)(2,1)} %collective-permute-done.3, bf16[8,128,384]{2,1,0:T(8,128)(2,1)S(1)} %all_gather.19), kind=kLoop, calls=%fused_computation.3 | loop fusion | flops 4718592 | bytes 6291456 | tf_op jit(solution)/shard_map/cond/branch_1_fun/concatenate | solution.py:179
  219.4 49.5 %while.14 = (s32[]{:T(128)}, f32[9,192,384]{2,1,0:T(8,128)}, bf16[32,10,18,192]{3,0,2,1:T(8,128)(2,1)}, bf16[4096,384]{1,0:T(8,128)(2,1)}, s32[]{:T(128)}, /*ind...) while((s32[]{:T(128)}, f32[9,192,384]{2,1,0:T(8,128)}, bf16[32,10,18,192]{3,0,2,1:T(8,128)(2,1)}, ...), condition=%wide.region_3.3_spmd, body=%wide.region_2.2_spmd.sunk | while | flops 603979776 | bytes 23888204 | solution.py:251
  219.4 1.8 constant_dynamic-slice_fusion.7
  221.2 1.2 copy.107
  223.1 1.8 fusion.96
  224.9 1.8 constant_dynamic-slice_fusion.7
  226.7 1.2 copy.107
  228.5 1.8 fusion.96
  230.3 1.8 constant_dynamic-slice_fusion.7
  232.1 1.2 copy.107
  233.3 1.0 copy-done.2
  234.3 1.8 fusion.96
  236.1 1.8 constant_dynamic-slice_fusion.7
  237.8 1.2 copy.107
  239.0 0.8 copy-done.2
  239.8 1.8 fusion.96
  241.6 1.8 constant_dynamic-slice_fusion.7
  243.4 1.2 copy.107
  245.3 1.8 fusion.96
  247.1 1.8 constant_dynamic-slice_fusion.7
  248.9 1.2 copy.107
  250.8 1.8 fusion.96
  252.6 1.8 constant_dynamic-slice_fusion.7
  254.4 1.2 copy.107
  256.3 1.8 fusion.96
  258.1 1.8 constant_dynamic-slice_fusion.7
  259.9 1.2 copy.107
  261.8 1.8 fusion.96
  263.5 1.8 constant_dynamic-slice_fusion.7
  265.3 1.2 copy.107
  267.2 1.8 fusion.96
  268.9 3.0 %multiply_reduce_fusion = f32[]{:T(128)} fusion(f32[9,192,384]{2,1,0:T(8,128)} %get-tuple-element.198), kind=kLoop, calls=%fused_computation.5 | loop fusion | flops 1327103 | bytes 2654212 | tf_op jit(solution)/shard_map/reduce_sum | solution.py:273
  272.7 4.5 %multiply_reduce_fusion.1 = f32[]{:T(128)} fusion(f32[3456,384]{1,0:T(8,128)} %all-reduce.15.cloned.1.call-done), kind=kLoop, calls=%fused_computation.47 | loop fusion | flops 2654207 | bytes 5308420 | tf_op jit(solution)/shard_map/reduce_sum | solution.py:273
  277.8 3.0 %multiply_convert_fusion.1 = bf16[1728,384]{1,0:T(8,128)(2,1)} fusion(f32[1728,384]{1,0:T(8,128)} %get-tuple-element.206, f32[]{:T(128)S(6)} %rsqrt.3), kind=kLoop, calls=%fused_computation.48 | loop fusion | flops 1327104 | bytes 3981316 | tf_op jit(solution)/shard_map/convert_element_type | solution.py:275
  280.9 4.4 %multiply_convert_fusion = bf16[3456,384]{1,0:T(8,128)(2,1)} fusion(f32[3456,384]{1,0:T(8,128)} %all-reduce.15.cloned.1.call-done, f32[]{:T(128)S(6)} %rsqrt.3), kind=kLoop, calls=%fused_computation.46 | loop fusion | flops 2654208 | bytes 7962628 | tf_op jit(solution)/shard_map/convert_element_type | solution.py:276
  (116 shorter events, 16.2 us)
Async XLA Ops:
  7.2 67.2 %copy-start = (bf16[3,3,384,384]{3,2,1,0:T(8,128)(2,1)S(1)}, bf16[3,3,384,384]{3,2,1,0:T(8,128)(2,1)}, u32[]{:S(2)}) copy-start(bf16[3,3,384,384]{3,2,1,0:T(8,128)(2,1)} %param.21) | copy-start | bytes 7962628
  7.2 38.6 %copy-start.5 = (bf16[1,1,8,16,192]{4,3,2,1,0:T(8,128)(2,1)S(1)}, bf16[1,1,8,16,192]{4,3,2,1,0:T(8,128)(2,1)}, u32[]{:S(2)}) copy-start(bf16[1,1,8,16,192]{4,3,2,1,0:T(8,128)(2,1)} %param.18) | copy-start | bytes 147460
  7.2 265.5 %all-reduce.15.cloned.1.call-start = ((), (), s32[]{:S(2)}) async-start(), calls=%async_computation | async-start | bytes 10616832 | tf_op jit(solution)/shard_map/psum | solution.py:229
  9.7 1.3 copy-start.6
  9.7 1.3 copy-start.8
  42.6 3.2 %copy-start.12 = (s32[52]{0:T(128)}, s32[52]{0:T(128)S(1)}, u32[]{:S(2)}) copy-start(s32[52]{0:T(128)S(1)} %compare_select_fusion.8) | copy-start | bytes 628
  46.9 26.6 %copy-start.13 = (s32[52]{0:T(128)S(1)}, s32[52]{0:T(128)}, u32[]{:S(2)}) copy-start(s32[52]{0:T(128)} %copy-done.12) | copy-start | bytes 628
  74.2 0.9 copy-start.4
  78.4 2.2 copy-start.7
  78.4 2.2 copy-start.9
  80.7 26.3 %copy-start.1 = (f32[128,3456]{1,0:T(8,128)S(1)}, f32[128,3456]{1,0:T(8,128)}, u32[]{:S(2)}) copy-start(f32[128,3456]{1,0:T(8,128)} %get-tuple-element.189) | copy-start | bytes 5308420 | tf_op jit(solution)/shard_map/cond
  104.4 75.8 %collective-permute-start.2 = (bf16[8,10,18,192]{3,0,2,1:T(8,128)(2,1)}, bf16[8,10,18,192]{3,0,2,1:T(8,128)(2,1)}, u32[]{:S(2)}, u32[]{:S(2)}) collective-permute-start(bf16[8,10,18,192]{3,0,2,1:T(8,128)(2,1)} %copy.70), channel_id=1, source_target_pairs={{0,24},{8,0},{16,8},{24,16},{1,25},{9,1},{17,9},{25,17},{2,26},{10... | collective-permute-start | bytes 1658888 | tf_op jit(solution)/shard_map/cond/branch_1_fun/ppermute | solution.py:178
  105.8 75.0 %collective-permute-start.1 = (bf16[8,10,18,192]{3,0,2,1:T(8,128)(2,1)}, bf16[8,10,18,192]{3,0,2,1:T(8,128)(2,1)}, u32[]{:S(2)}, u32[]{:S(2)}) collective-permute-start(bf16[8,10,18,192]{3,0,2,1:T(8,128)(2,1)} %copy.70), channel_id=1, source_target_pairs={{0,16},{8,24},{16,0},{24,8},{1,17},{9,25},{17,1},{25,9},{2,18},{10... | collective-permute-start | bytes 1658888 | tf_op jit(solution)/shard_map/cond/branch_1_fun/ppermute | solution.py:178
  106.3 74.5 %collective-permute-start = (bf16[8,10,18,192]{3,0,2,1:T(8,128)(2,1)}, bf16[8,10,18,192]{3,0,2,1:T(8,128)(2,1)}, u32[]{:S(2)}, u32[]{:S(2)}) collective-permute-start(bf16[8,10,18,192]{3,0,2,1:T(8,128)(2,1)} %copy.70), channel_id=1, source_target_pairs={{0,8},{8,16},{16,24},{24,0},{1,9},{9,17},{17,25},{25,1},{2,10},{10... | collective-permute-start | bytes 1658888 | tf_op jit(solution)/shard_map/cond/branch_1_fun/ppermute | solution.py:178
  107.1 21.1 %copy-start.11 = (s32[416]{0:T(512)S(1)}, s32[416]{0:T(512)}, u32[]{:S(2)}) copy-start(s32[416]{0:T(512)} %constant.208.clone.1) | copy-start | bytes 4996 | tf_op jit(solution)/shard_map/cond
  107.3 0.7 copy-start.3
  107.3 44.3 %copy-start.10 = (s32[416]{0:T(512)S(1)}, s32[416]{0:T(512)}, u32[]{:S(2)}) copy-start(s32[416]{0:T(512)} %constant.209.clone.1) | copy-start | bytes 4996 | tf_op jit(solution)/shard_map/cond
  177.7 20.7 %collective-permute-start.5 = (bf16[8,128,384]{2,1,0:T(8,128)(2,1)S(1)}, bf16[8,128,384]{2,1,0:T(8,128)(2,1)}, u32[]{:S(2)}, u32[]{:S(2)}) collective-permute-start(bf16[8,128,384]{2,1,0:T(8,128)(2,1)S(1)} %all_gather.19), channel_id=1, source_target_pairs={{0,24},{8,0},{16,8},{24,16},{1,25},{9,1},{17,9},{25,17},{2,26},{10... | collective-permute-start | bytes 2359304 | tf_op jit(solution)/shard_map/cond/branch_1_fun/ppermute | solution.py:178
  179.0 37.2 %collective-permute-start.4 = (bf16[8,128,384]{2,1,0:T(8,128)(2,1)S(1)}, bf16[8,128,384]{2,1,0:T(8,128)(2,1)}, u32[]{:S(2)}, u32[]{:S(2)}) collective-permute-start(bf16[8,128,384]{2,1,0:T(8,128)(2,1)S(1)} %all_gather.19), channel_id=1, source_target_pairs={{0,16},{8,24},{16,0},{24,8},{1,17},{9,25},{17,1},{25,9},{2,18},{10... | collective-permute-start | bytes 2359304 | tf_op jit(solution)/shard_map/cond/branch_1_fun/ppermute | solution.py:178
  180.2 36.0 %collective-permute-start.3 = (bf16[8,128,384]{2,1,0:T(8,128)(2,1)S(1)}, bf16[8,128,384]{2,1,0:T(8,128)(2,1)}, u32[]{:S(2)}, u32[]{:S(2)}) collective-permute-start(bf16[8,128,384]{2,1,0:T(8,128)(2,1)S(1)} %all_gather.19), channel_id=1, source_target_pairs={{0,8},{8,16},{16,24},{24,0},{1,9},{9,17},{17,25},{25,1},{2,10},{10... | collective-permute-start | bytes 2359304 | tf_op jit(solution)/shard_map/cond/branch_1_fun/ppermute | solution.py:178
  221.2 1.9 copy-start.2
  226.6 1.9 copy-start.2
  232.1 2.2 copy-start.2
  237.8 2.0 copy-start.2
  243.4 1.9 copy-start.2
  248.9 1.9 copy-start.2
  254.4 1.9 copy-start.2
  259.9 1.9 copy-start.2
  265.3 1.9 copy-start.2
Sparse Core Ops, SparseCore 0:
  78.5 184.5 all-reduce.14

commit v10 on v8

--- a/solution.py
+++ b/solution.py
@@ -233,19 +233,20 @@
             every_pad = gather_all(padded_tile_in[None], faces)
             every_grad = gather_all(grad_one.reshape(1, -1, width_out), faces)
             every_grad = every_grad.reshape(-1, width_out)
-            blocks = []
-            for down_step in range(3):
-                for side_step in range(3):
-                    window = every_pad[:, down_step : down_step + height, side_step : side_step + breadth]
-                    blocks.append(
-                        lax.dot_general(
-                            window.reshape(-1, width_in),
-                            every_grad,
-                            (((0,), (0,)), ((), ())),
-                            preferred_element_type=jnp.float32,
-                        )
+            windows = jnp.concatenate(
+                [
+                    every_pad[:, down_step : down_step + height, side_step : side_step + breadth].reshape(
+                        -1, width_in
                     )
-            return grad_one, jnp.concatenate(blocks, axis=0)
+                    for down_step in range(3)
+                    for side_step in range(3)
+                ],
+                axis=1,
+            )
+            total_in = lax.dot_general(
+                windows, every_grad, (((0,), (0,)), ((), ())), preferred_element_type=jnp.float32
+            )
+            return grad_one, total_in
 
         def skipped(frame):
             return (

time: 287 us -> 288 us (level)
  local copies, waits for them, and re-layouts: 36 us -> 67.5 us
  waiting for transfers between devices: 39.4 us -> 10.4 us
  other arithmetic: 31.8 us -> 27.3 us
  blocking collectives: 124 us -> 128 us
    concatenate x0 -> x1, local copies, waits for them, and re-layouts: none -> 24 us  [rest(): jnp.concatenate([every_pad[:, down_step:down_step + height, side_step:sid...]
    ppermute x6, waiting for transfers between devices: 17.7 us -> 0.02 us  [gather_all(): parts.append(lax.ppermute(local, 'face', pairs))]
    psum x1, waiting for transfers between devices: 21.7 us -> 10.4 us  [body(): total_out = lax.psum(grad_w_out, ('face', 'tile'))]
    slice x10, local copies, waits for them, and re-layouts: 16.1 us -> 26.8 us  [rest(): every_pad[:, down_step:down_step + height, side_step:side_step + breadth]]
    reduce_sum x2 -> x1, other arithmetic: 7.61 us -> 4.54 us  [body(): squares = jnp.sum(total_in * total_in) + jnp.sum(total_out * total_out)]
    all_gather x1, blocking collectives: 17.8 us -> 20.8 us  [return_border(): seam_set = lax.all_gather(seam_sum, 'face', axis=0, tiled=True)]
    dot_general x9 -> x1, matrix products: 15.8 us -> 13.3 us  [rest(): lax.dot_general(windows, every_grad, (((0,), (0,)), ((), ())), preferred_...]
    cond x15 -> x19, local copies, waits for them, and re-layouts: 6.68 us -> 5.58 us
  transfers between devices with their start and end apart: 7 -> 7, of which waited for: 3 -> 1; matrix products, arithmetic and copies ran while one was open for 22% -> 31% of each run, Pallas kernels for 0% -> 0%
where the time goes in v10:
time: 288 us; the launch traced here: 285 us
  blocking collectives  128 us (44%)
  local copies, waits for them, and re-layouts  67.5 us (23%)
  matrix products  29.3 us (10%)
  other arithmetic  27.3 us (9%)
  between operations  15.1 us (5%)
  waiting for transfers between devices  10.4 us (4%)
  starting transfers between devices  6.61 us (2%)
    all_gather x2, blocking collectives, gather_all(): local = lax.all_gather(block, 'tile', axis=0, tiled=True)  39.8 us
    all_gather x2, blocking collectives, padded_tile(): rims = lax.all_gather(rim_of(cells), 'tile', axis=0, tiled=True)  30.2 us
    slice x10, local copies, waits for them, and re-layouts, rest(): every_pad[:, down_step:down_step + height, side_step:side_step + breadth]  26.8 us
    concatenate x1, local copies, waits for them, and re-layouts, rest(): jnp.concatenate([every_pad[:, down_step:down_step + height, side_step:sid...  24 us
    all_gather x1, blocking collectives, return_border(): seam_set = lax.all_gather(seam_sum, 'face', axis=0, tiled=True)  20.8 us
    all_gather x1, blocking collectives, return_border(): borders = lax.all_gather(border, 'tile', axis=0, tiled=True)  19 us
    all_gather x2, blocking collectives, padded_tile(): edge_set = lax.all_gather(edges, 'face', axis=0, tiled=True)  18.2 us
    dot_general x1, matrix products, rest(): lax.dot_general(windows, every_grad, (((0,), (0,)), ((), ())), preferred_...  13.3 us
  transfers between devices with their start and end apart: 7, of which 1 were waited for; matrix products, arithmetic and copies ran while one was open for 31% of the time, Pallas kernels for 0%

profile of v10, /device:TPU:0, one launch (start us, length us, event | category | flops | bytes accessed | tf_op | source)
XLA Modules:
  0.0 285.2 jit_solution(13460865406078141810)
XLA Ops:
  7.2 1.0 copy.136
  8.3 0.7 slice_bitcast_fusion.9
  9.0 15.9 %all_gather.24 = bf16[384,192]{1,0:T(8,128)(2,1)S(1)} all-gather(bf16[48,192]{1,0:T(8,128)(2,1)S(1)} %pad_maximum_fusion.9), channel_id=1, replica_groups=mesh['face'=4,'tile'=8] {'tile'}, dimensions={0}, use_global_device_ids=true | all-gather | bytes 165888 | tf_op jit(solution)/shard_map/all_gather | solution.py:110
  25.0 0.9 convolution_convert_fusion.1
  26.0 8.7 %all_gather.25 = bf16[512,192]{0,1:T(8,128)(2,1)S(1)} all-gather(bf16[128,192]{0,1:T(8,128)(2,1)S(1)} %convolution_convert_fusion.1), channel_id=1, replica_groups=mesh['face'=4,'tile'=8] {'face'}, dimensions={0}, use_global_device_ids=true | all-gather | bytes 245760 | tf_op jit(solution)/shard_map/all_gather | solution.py:116
  34.7 0.7 constant_dynamic-slice_fusion.1
  35.4 0.6 fusion.76
  36.0 0.7 fusion.75
  36.7 5.8 %compare_select_fusion.8 = s32[52]{0:T(128)S(1)} fusion(s32[8,52]{1,0:T(8,128)} %constant.123.clone, s32[]{:T(128)S(6)} %select_n.196, s32[8,52]{1,0:T(8,128)} %constant.122.clone, s32[8,52]{1,0:T(8,128)} %constant.121.clone, s32[]{:T(128)} %bitcast.47, s32[]{:T(128)} %bitcast.42, s32[]{:T(128)} %bitcast.50, s32[]{:T(128)} %bitcast.49, s32[]{:T(128)} %bitcast.48, ...), kind=kLoop, calls=%fused_computation.120 | loop fusion | flops 1248 | bytes 868 | tf_op jit(solution)/shard_map/jit(_where)/select_n | solution.py:101
  42.5 0.3 convolution_convert_fusion.3
  42.8 0.2 copy-done.17
  43.3 0.6 copy.114
  44.0 0.6 copy.116
  44.6 0.6 copy.117
  45.2 0.6 copy.118
  45.9 1.1 concatenate.80
  47.1 1.7 multiply_convert_fusion.2
  48.9 14.3 %all_gather.26 = bf16[384,384]{1,0:T(8,128)(2,1)S(1)} all-gather(bf16[48,384]{1,0:T(8,128)(2,1)S(1)} %pad_maximum_fusion.8), channel_id=1, replica_groups=mesh['face'=4,'tile'=8] {'tile'}, dimensions={0}, use_global_device_ids=true | all-gather | bytes 331776 | tf_op jit(solution)/shard_map/all_gather | solution.py:110
  63.2 0.9 convolution_convert_fusion
  64.2 9.5 %all_gather.27 = bf16[512,384]{1,0:T(8,128)(2,1)S(1)} all-gather(bf16[128,384]{1,0:T(8,128)(2,1)S(1)} %convolution_convert_fusion), channel_id=1, replica_groups=mesh['face'=4,'tile'=8] {'face'}, dimensions={0}, use_global_device_ids=true | all-gather | bytes 491520 | tf_op jit(solution)/shard_map/all_gather | solution.py:116
  73.6 0.9 convolution_convert_fusion.2
  75.2 0.6 fusion.77
  75.9 3.2 %fusion.28 = f32[3456,384]{1,0:T(8,128)} fusion(bf16[128,3456]{1,0:T(8,128)(2,1)S(1)} %constant_dynamic-update-slice_fusion.4, f32[128,384]{1,0:T(8,128)S(1)} %fusion.77, bf16[128,384]{1,0:T(8,128)(2,1)S(1)} %bitcast.198), kind=kOutput, calls=%fused_computation.67 | convolution fusion | flops 340279296 | bytes 6488064 | tf_op jit(solution)/shard_map/dot_general | solution.py:204
  79.2 0.6 copy-done.8
  79.9 2.2 fusion.30
  82.1 173.1 %conditional.1 = (f32[1728,384]{1,0:T(8,128)}, bf16[1,1,8,16,384]{4,3,2,1,0:T(8,128)(2,1)}, f32[]{:T(128)}) conditional(s32[]{:T(128)} %convert_element_type.61, () %tuple.20, (bf16[10,18,192]{2,0,1:T(8,128)(2,1)S(1)}, f32[128,3456]{1,0:T(8,128)}, s32[]{:T(128)}, (), (), /*index=5*/s32[1,4]{1,0:T(1,128)}, s32[1,4]{1,0:T(1,128)}, (), (), ...), branch_computations={%region_0.1_spmd, %region_1.3_spmd} | conditional | flops 5893907456 | bytes 166470240 | solution.py:257
  82.1 22.9 %all-gather = bf16[80,18,192]{2,1,0:T(8,128)(2,1)S(1)} all-gather(bf16[10,18,192]{2,1,0:T(8,128)(2,1)S(1)} %copy.125), channel_id=2, replica_groups=mesh['face'=4,'tile'=8] {'tile'}, dimensions={0}, use_global_device_ids=true | all-gather | bytes 622080 | tf_op jit(solution)/shard_map/cond/branch_1_fun/all_gather | solution.py:174
  105.0 1.1 constant_dynamic-update-slice_fusion.3
  106.1 0.2 collective-permute-start
  106.3 1.4 collective-permute-start.1
  107.8 1.5 collective-permute-start.2
  109.7 19.0 %all-gather.1 = f32[8,52,384]{2,1,0:T(8,128)} all-gather(f32[1,52,384]{2,1,0:T(8,128)S(1)} %maximum_bitcast_fusion), channel_id=1, replica_groups=mesh['face'=4,'tile'=8] {'tile'}, dimensions={0}, use_global_device_ids=true | all-gather | bytes 718848 | tf_op jit(solution)/shard_map/cond/branch_1_fun/all_gather | solution.py:137
  128.7 2.0 reshape.374
  130.8 1.5 fusion
  132.3 20.8 %all_gather.18 = f32[512,384]{1,0:T(8,128)} all-gather(f32[128,384]{1,0:T(8,128)S(1)} %fusion), channel_id=1, replica_groups=mesh['face'=4,'tile'=8] {'face'}, dimensions={0}, use_global_device_ids=true | all-gather | bytes 983040 | tf_op jit(solution)/shard_map/cond/branch_1_fun/all_gather | solution.py:143
  153.1 2.1 fusion.8
  155.2 0.7 fusion.67
  155.9 5.9 %bitcast_select_fusion.1 = s32[48]{0:T(128)S(1)} fusion(s32[8,48]{1,0:T(8,128)} %constant.128.clone.1, s32[]{:T(128)S(6)} %select_n.167, s32[8,48]{1,0:T(8,128)} %constant.127.clone.1, s32[]{:T(128)} %bitcast.28, s32[]{:T(128)} %bitcast.23, s32[]{:T(128)} %bitcast.31, s32[]{:T(128)} %bitcast.30, s32[]{:T(128)} %bitcast.29, s32[]{:T(128)} %bitcast.26, ...), kind=kLoop, calls=%fused_computation.33 | loop fusion | flops 912 | bytes 612 | tf_op jit(solution)/shard_map/cond/branch_1_fun/jit(_where)/select_n | solution.py:90
  161.8 1.5 convolution_add_fusion
  163.4 0.8 fusion.6
  164.1 16.9 %all_gather.19 = bf16[8,128,384]{2,1,0:T(8,128)(2,1)} all-gather(bf16[1,128,384]{2,1,0:T(8,128)(2,1)} %bitcast.37), channel_id=1, replica_groups=mesh['face'=4,'tile'=8] {'tile'}, dimensions={0}, use_global_device_ids=true | all-gather | bytes 884736 | tf_op jit(solution)/shard_map/cond/branch_1_fun/all_gather | solution.py:174
  181.0 1.5 collective-permute-start.5
  182.5 1.4 collective-permute-start.4
  183.9 0.6 collective-permute-start.3
  184.5 1.2 constant_dynamic-update-slice_fusion.2
  185.7 1.2 constant_dynamic-update-slice_fusion.1
  186.9 1.2 constant_dynamic-update-slice_fusion
  188.2 3.6 %fusion.63 = (bf16[32,8,16,192]{3,0,2,1:T(8,128)(2,1)S(1)}, bf16[32,8,16,192]{3,0,2,1:T(8,128)(2,1)S(1)}, bf16[32,8,16,192]{3,0,2,1:T(8,128)(2,1)S(1)}, bf16[32,...) fusion(bf16[32,10,18,192]{3,0,2,1:T(8,128)(2,1)S(1)} %constant_, ...), kind=kLoop, calls=%fused_computation.154 | loop fusion | bytes 28311552 | tf_op jit(solution)/shard_map/cond/branch_1_fun/slice | solution.py:238
  191.8 2.9 %copy.96 = bf16[32,8,16,192]{3,2,1,0:T(8,128)(2,1)S(1)} copy(bf16[32,8,16,192]{3,0,2,1:T(8,128)(2,1)} %get-tuple-element.153) | data formatting | bytes 3145728 | tf_op jit(solution)/shard_map/cond/branch_1_fun/slice | solution.py:238
  194.7 2.5 copy.97
  197.2 2.5 copy.98
  199.7 2.6 copy.99
  202.3 2.5 copy.100
  204.8 2.5 copy.101
  207.3 2.5 copy.102
  209.9 2.6 copy.103
  212.4 2.5 copy.104
  214.9 24.0 %concatenate.52 = bf16[4096,1728]{1,0:T(8,128)(2,1)} concatenate(bf16[4096,192]{1,0:T(8,128)(2,1)S(1)} %bitcast.167, bf16[4096,192]{1,0:T(8,128)(2,1)} %bitcast.168, bf16[4096,192]{1,0:T(8,128)(2,1)} %bitcast.169, bf16[4096,192]{1,0:T(8,128)(2,1)} %bitcast.170, bf16[4096,192]{1,0:T(8,128)(2,1)} %bitcast.171, bf16[4096,192]{1,0:T(8,128)(2,1)} %bitcast.172, ...), dimensions={1} | concatenate | bytes 28311552 | tf_op jit(solution)/shard_map/cond/branch_1_fun/concatenate | solution.py:236
  239.0 2.2 pad_maximum_fusion
  241.2 13.3 %multiply_reduce_fusion = (f32[]{:T(128)}, f32[1728,384]{1,0:T(8,128)}) fusion(bf16[4096,1728]{1,0:T(8,128)(2,1)} %concatenate.52, bf16[4096,384]{1,0:T(8,128)(2,1)S(1)} %bitcast.177), kind=kOutput, calls=%fused_computation.1 | convolution fusion | flops 5437145088 | bytes 19955716 | tf_op jit(solution)/shard_map/cond/branch_1_fun/dot_general | solution.py:246
  255.2 10.4 %all-reduce.15.cloned.1.call-done = f32[3456,384]{1,0:T(8,128)} async-done(((f32[3456,384]{1,0:T(8,128)}), f32[3456,384]{1,0:T(8,128)}) %all-reduce.15.cloned.1.call-update) | async-done | bytes 5308432 | tf_op jit(solution)/shard_map/psum | solution.py:229
  265.6 4.5 %multiply_reduce_fusion.1 = f32[]{:T(128)} fusion(f32[3456,384]{1,0:T(8,128)} %all-reduce.15.cloned.1.call-done), kind=kLoop, calls=%fused_computation.47 | loop fusion | flops 2654207 | bytes 5308420 | tf_op jit(solution)/shard_map/reduce_sum | solution.py:270
  270.8 3.2 %multiply_convert_fusion.1 = bf16[1728,384]{1,0:T(8,128)(2,1)} fusion(f32[1728,384]{1,0:T(8,128)} %get-tuple-element.93, f32[]{:T(128)S(6)} %rsqrt.3), kind=kLoop, calls=%fused_computation.48 | loop fusion | flops 1327104 | bytes 3981316 | tf_op jit(solution)/shard_map/convert_element_type | solution.py:272
  274.0 4.4 %multiply_convert_fusion = bf16[3456,384]{1,0:T(8,128)(2,1)} fusion(f32[3456,384]{1,0:T(8,128)} %all-reduce.15.cloned.1.call-done, f32[]{:T(128)S(6)} %rsqrt.3), kind=kLoop, calls=%fused_computation.46 | loop fusion | flops 2654208 | bytes 7962628 | tf_op jit(solution)/shard_map/convert_element_type | solution.py:273
  (92 shorter events, 1.7 us)
Async XLA Ops:
  7.2 68.0 %copy-start = (bf16[3,3,384,384]{3,2,1,0:T(8,128)(2,1)S(1)}, bf16[3,3,384,384]{3,2,1,0:T(8,128)(2,1)}, u32[]{:S(2)}) copy-start(bf16[3,3,384,384]{3,2,1,0:T(8,128)(2,1)} %param.19) | copy-start | bytes 7962628
  7.2 38.7 %copy-start.6 = (bf16[1,1,8,16,192]{4,3,2,1,0:T(8,128)(2,1)S(1)}, bf16[1,1,8,16,192]{4,3,2,1,0:T(8,128)(2,1)}, u32[]{:S(2)}) copy-start(bf16[1,1,8,16,192]{4,3,2,1,0:T(8,128)(2,1)} %param.16) | copy-start | bytes 147460
  7.2 258.4 %all-reduce.15.cloned.1.call-start = ((), (), s32[]{:S(2)}) async-start(), calls=%async_computation | async-start | bytes 10616832 | tf_op jit(solution)/shard_map/psum | solution.py:229
  35.4 7.7 %copy-start.11 = (s32[1,4]{1,0:T(1,128)}, s32[1,4]{1,0:T(1,128)S(1)}, u32[]{:S(2)}) copy-start(s32[1,4]{1,0:T(1,128)S(1)} %get-tuple-element.233) | copy-start | bytes 52
  35.4 7.7 %copy-start.13 = (s32[1,4]{1,0:T(1,128)}, s32[1,4]{1,0:T(1,128)S(1)}, u32[]{:S(2)}) copy-start(s32[1,4]{1,0:T(1,128)S(1)} %get-tuple-element.234) | copy-start | bytes 52
  42.5 0.6 copy-start.17
  42.8 3.1 %copy-start.7 = (bf16[8,1,192]{2,0,1:T(8,128)(2,1)}, bf16[8,1,192]{2,0,1:T(8,128)(2,1)S(1)}, u32[]{:S(2)}) copy-start(bf16[8,1,192]{2,0,1:T(8,128)(2,1)S(1)} %get-tuple-element.221) | copy-start | bytes 9220
  42.8 3.1 %copy-start.9 = (bf16[8,1,192]{2,0,1:T(8,128)(2,1)}, bf16[8,1,192]{2,0,1:T(8,128)(2,1)S(1)}, u32[]{:S(2)}) copy-start(bf16[8,1,192]{2,0,1:T(8,128)(2,1)S(1)} %get-tuple-element.222) | copy-start | bytes 9220
  75.0 0.9 copy-start.5
  79.1 0.7 copy-start.8
  79.1 0.7 copy-start.10
  82.1 27.2 %copy-start.4 = (f32[128,3456]{1,0:T(8,128)S(1)}, f32[128,3456]{1,0:T(8,128)}, u32[]{:S(2)}) copy-start(f32[128,3456]{1,0:T(8,128)} %get-tuple-element.77) | copy-start | bytes 5308420 | tf_op jit(solution)/shard_map/cond
  106.1 77.8 %collective-permute-start = (bf16[8,10,18,192]{3,0,2,1:T(8,128)(2,1)}, bf16[8,10,18,192]{3,0,2,1:T(8,128)(2,1)}, u32[]{:S(2)}, u32[]{:S(2)}) collective-permute-start(bf16[8,10,18,192]{3,0,2,1:T(8,128)(2,1)} %get-tuple-element.144), channel_id=1, source_target_pairs={{0,8},{8,16},{16,24},{24,0},{1,9},{9,17},{17,25},{25,1},{2,10},{10... | collective-permute-start | bytes 1658888 | tf_op jit(solution)/shard_map/cond/branch_1_fun/ppermute | solution.py:178
  106.3 79.4 %collective-permute-start.1 = (bf16[8,10,18,192]{3,0,2,1:T(8,128)(2,1)}, bf16[8,10,18,192]{3,0,2,1:T(8,128)(2,1)}, u32[]{:S(2)}, u32[]{:S(2)}) collective-permute-start(bf16[8,10,18,192]{3,0,2,1:T(8,128)(2,1)} %get-tuple-element.144), channel_id=1, source_target_pairs={{0,16},{8,24},{16,0},{24,8},{1,17},{9,25},{17,1},{25,9},{2,18},{10... | collective-permute-start | bytes 1658888 | tf_op jit(solution)/shard_map/cond/branch_1_fun/ppermute | solution.py:178
  107.8 79.2 %collective-permute-start.2 = (bf16[8,10,18,192]{3,0,2,1:T(8,128)(2,1)}, bf16[8,10,18,192]{3,0,2,1:T(8,128)(2,1)}, u32[]{:S(2)}, u32[]{:S(2)}) collective-permute-start(bf16[8,10,18,192]{3,0,2,1:T(8,128)(2,1)} %get-tuple-element.144), channel_id=1, source_target_pairs={{0,24},{8,0},{16,8},{24,16},{1,25},{9,1},{17,9},{25,17},{2,26},{10... | collective-permute-start | bytes 1658888 | tf_op jit(solution)/shard_map/cond/branch_1_fun/ppermute | solution.py:178
  109.4 21.4 %copy-start.16 = (s32[416]{0:T(512)S(1)}, s32[416]{0:T(512)}, u32[]{:S(2)}) copy-start(s32[416]{0:T(512)} %constant.125.clone.1) | copy-start | bytes 4996 | tf_op jit(solution)/shard_map/cond
  109.6 43.5 %copy-start.15 = (s32[416]{0:T(512)S(1)}, s32[416]{0:T(512)}, u32[]{:S(2)}) copy-start(s32[416]{0:T(512)} %constant.126.clone.1) | copy-start | bytes 4996 | tf_op jit(solution)/shard_map/cond
  109.6 45.6 %copy-start.12 = (s32[1,4]{1,0:T(1,128)S(1)}, s32[1,4]{1,0:T(1,128)}, u32[]{:S(2)}) copy-start(s32[1,4]{1,0:T(1,128)} %get-tuple-element.82) | copy-start | bytes 52 | tf_op jit(solution)/shard_map/cond
  109.6 45.6 %copy-start.14 = (s32[1,4]{1,0:T(1,128)S(1)}, s32[1,4]{1,0:T(1,128)}, u32[]{:S(2)}) copy-start(s32[1,4]{1,0:T(1,128)} %get-tuple-element.81) | copy-start | bytes 52 | tf_op jit(solution)/shard_map/cond
  181.0 57.9 %collective-permute-start.5 = (bf16[8,128,384]{2,1,0:T(8,128)(2,1)}, bf16[8,128,384]{2,1,0:T(8,128)(2,1)}, u32[]{:S(2)}, u32[]{:S(2)}) collective-permute-start(bf16[8,128,384]{2,1,0:T(8,128)(2,1)} %all_gather.19), channel_id=1, source_target_pairs={{0,24},{8,0},{16,8},{24,16},{1,25},{9,1},{17,9},{25,17},{2,26},{10... | collective-permute-start | bytes 2359304 | tf_op jit(solution)/shard_map/cond/branch_1_fun/ppermute | solution.py:178
  182.5 56.4 %collective-permute-start.4 = (bf16[8,128,384]{2,1,0:T(8,128)(2,1)}, bf16[8,128,384]{2,1,0:T(8,128)(2,1)}, u32[]{:S(2)}, u32[]{:S(2)}) collective-permute-start(bf16[8,128,384]{2,1,0:T(8,128)(2,1)} %all_gather.19), channel_id=1, source_target_pairs={{0,16},{8,24},{16,0},{24,8},{1,17},{9,25},{17,1},{25,9},{2,18},{10... | collective-permute-start | bytes 2359304 | tf_op jit(solution)/shard_map/cond/branch_1_fun/ppermute | solution.py:178
  183.9 55.1 %collective-permute-start.3 = (bf16[8,128,384]{2,1,0:T(8,128)(2,1)}, bf16[8,128,384]{2,1,0:T(8,128)(2,1)}, u32[]{:S(2)}, u32[]{:S(2)}) collective-permute-start(bf16[8,128,384]{2,1,0:T(8,128)(2,1)} %all_gather.19), channel_id=1, source_target_pairs={{0,8},{8,16},{16,24},{24,0},{1,9},{9,17},{17,25},{25,1},{2,10},{10... | collective-permute-start | bytes 2359304 | tf_op jit(solution)/shard_map/cond/branch_1_fun/ppermute | solution.py:178
  191.8 2.9 %copy-start.3 = (bf16[32,8,16,192]{3,0,2,1:T(8,128)(2,1)S(1)}, bf16[32,8,16,192]{3,0,2,1:T(8,128)(2,1)}, u32[]{:S(2)}) copy-start(bf16[32,8,16,192]{3,0,2,1:T(8,128)(2,1)} %get-tuple-element.152) | copy-start | bytes 4718596 | tf_op jit(solution)/shard_map/cond
  194.7 2.5 copy-start.2
  270.8 7.6 %copy-start.1 = (bf16[3,3,384,384]{3,2,1,0:T(8,128)(2,1)S(1)}, bf16[3,3,384,384]{3,2,1,0:T(8,128)(2,1)}, u32[]{:S(2)}) copy-start(bf16[3,3,384,384]{3,2,1,0:T(8,128)(2,1)} %param.19) | copy-start | bytes 7962628
Sparse Core Ops, SparseCore 0:
  79.3 186.2 all-reduce.14

commit v11 on v8

--- a/solution.py
+++ b/solution.py
@@ -81,11 +81,9 @@
 
 
 def seam_source(which, pos, link_row, turn_row, side):
-    link = jnp.full_like(which, -1)
-    turn = jnp.zeros_like(which)
-    for k in range(4):
-        link = jnp.where(which == k, link_row[k], link)
-        turn = jnp.where(which == k, turn_row[k], turn)
+    hit = which[:, None] == jnp.arange(4, dtype=which.dtype)[None, :]
+    link = jnp.sum(jnp.where(hit, link_row[None, :], 0), axis=1)
+    turn = jnp.sum(jnp.where(hit, turn_row[None, :], 0), axis=1)
     glued = link * side + jnp.where(turn == 1, side - 1 - pos, pos)
     return jnp.where(which >= 0, glued, -1)
 

time: 287 us -> 278 us (0.969)
  other arithmetic: 31.8 us -> 22.3 us
    select_n x1, other arithmetic: 5.93 us -> 0.71 us  [seam_source(): return jnp.where(which >= 0, glued, -1)]
    select_n x1, other arithmetic: 5.75 us -> 0.73 us  [halo_source(): jnp.where(own_intra >= 0, own_intra, jnp.where(glued >= 0, tiles * rim_le...]
  transfers between devices with their start and end apart: 7 -> 7, of which waited for: 3 -> 2; matrix products, arithmetic and copies ran while one was open for 22% -> 21% of each run, Pallas kernels for 0% -> 0%
where the time goes in v11:
time: 278 us; the launch traced here: 277 us
  blocking collectives  125 us (45%)
  waiting for transfers between devices  41.2 us (15%)
  local copies, waits for them, and re-layouts  35.1 us (13%)
  matrix products  31.1 us (11%)
  other arithmetic  22.3 us (8%)
  between operations  15 us (5%)
  starting transfers between devices  6.88 us (2%)
    all_gather x2, blocking collectives, gather_all(): local = lax.all_gather(block, 'tile', axis=0, tiled=True)  40.5 us
    all_gather x2, blocking collectives, padded_tile(): rims = lax.all_gather(rim_of(cells), 'tile', axis=0, tiled=True)  30.2 us
    psum x1, waiting for transfers between devices, body(): total_out = lax.psum(grad_w_out, ('face', 'tile'))  23.7 us
    all_gather x2, blocking collectives, padded_tile(): edge_set = lax.all_gather(edges, 'face', axis=0, tiled=True)  18.2 us
    all_gather x1, blocking collectives, return_border(): borders = lax.all_gather(border, 'tile', axis=0, tiled=True)  18 us
    all_gather x1, blocking collectives, return_border(): seam_set = lax.all_gather(seam_sum, 'face', axis=0, tiled=True)  17.8 us
    ppermute x6, waiting for transfers between devices, gather_all(): parts.append(lax.ppermute(local, 'face', pairs))  17.5 us
    slice x10, local copies, waits for them, and re-layouts, rest(): every_pad[:, down_step:down_step + height, side_step:side_step + breadth]  16.1 us
  transfers between devices with their start and end apart: 7, of which 2 were waited for; matrix products, arithmetic and copies ran while one was open for 21% of the time, Pallas kernels for 0%

profile of v11, /device:TPU:0, one launch (start us, length us, event | category | flops | bytes accessed | tf_op | source)
XLA Modules:
  0.0 277.3 jit_solution(16830142217500167839)
XLA Ops:
  7.2 0.9 slice_bitcast_fusion.9
  8.1 0.9 copy.170
  9.0 15.9 %all_gather.24 = bf16[384,192]{1,0:T(8,128)(2,1)S(1)} all-gather(bf16[48,192]{1,0:T(8,128)(2,1)S(1)} %pad_maximum_fusion.9), channel_id=1, replica_groups=mesh['face'=4,'tile'=8] {'tile'}, dimensions={0}, use_global_device_ids=true | all-gather | bytes 165888 | tf_op jit(solution)/shard_map/all_gather | solution.py:108
  25.0 0.9 convolution_convert_fusion.1
  26.0 8.7 %all_gather.25 = bf16[512,192]{0,1:T(8,128)(2,1)S(1)} all-gather(bf16[128,192]{0,1:T(8,128)(2,1)S(1)} %convolution_convert_fusion.1), channel_id=1, replica_groups=mesh['face'=4,'tile'=8] {'face'}, dimensions={0}, use_global_device_ids=true | all-gather | bytes 245760 | tf_op jit(solution)/shard_map/all_gather | solution.py:114
  34.7 0.7 fusion.45
  35.4 0.7 fusion.46
  36.7 0.7 compare_select_fusion.2
  40.9 1.1 concatenate.80
  42.1 1.7 multiply_convert_fusion.2
  43.9 14.3 %all_gather.26 = bf16[384,384]{1,0:T(8,128)(2,1)S(1)} all-gather(bf16[48,384]{1,0:T(8,128)(2,1)S(1)} %pad_maximum_fusion.8), channel_id=1, replica_groups=mesh['face'=4,'tile'=8] {'tile'}, dimensions={0}, use_global_device_ids=true | all-gather | bytes 331776 | tf_op jit(solution)/shard_map/all_gather | solution.py:108
  58.3 0.9 convolution_convert_fusion
  59.2 9.5 %all_gather.27 = bf16[512,384]{1,0:T(8,128)(2,1)S(1)} all-gather(bf16[128,384]{1,0:T(8,128)(2,1)S(1)} %convolution_convert_fusion), channel_id=1, replica_groups=mesh['face'=4,'tile'=8] {'face'}, dimensions={0}, use_global_device_ids=true | all-gather | bytes 491520 | tf_op jit(solution)/shard_map/all_gather | solution.py:114
  68.7 0.9 convolution_convert_fusion.2
  70.9 3.3 %fusion.26 = f32[3456,384]{1,0:T(8,128)} fusion(bf16[128,3456]{1,0:T(8,128)(2,1)S(1)} %constant_dynamic-update-slice_fusion.4, f32[128,384]{1,0:T(8,128)S(1)} %fusion.72, bf16[128,384]{1,0:T(8,128)(2,1)S(1)} %bitcast.192), kind=kOutput, calls=%fused_computation.70 | convolution fusion | flops 340279296 | bytes 6488064 | tf_op jit(solution)/shard_map/dot_general | solution.py:202
  74.9 2.1 fusion.28
  77.1 157.0 %conditional.1 = (f32[1728,384]{1,0:T(8,128)}, bf16[1,1,8,16,384]{4,3,2,1,0:T(8,128)(2,1)}, f32[]{:T(128)}) conditional(s32[]{:T(128)} %convert_element_type.61, () %tuple.20, (bf16[10,18,192]{2,0,1:T(8,128)(2,1)S(1)}, f32[128,3456]{1,0:T(8,128)}, s32[]{:T(128)}, (), (), /*index=5*/s32[4]{0:T(128)}, s32[4]{0:T(128)}, (), (), ...), branch_computations={%region_2.3_spmd, %region_3.7_spmd} | conditional | flops 5893907456 | bytes 165967360 | solution.py:254
  77.1 22.9 %all-gather = bf16[80,18,192]{2,1,0:T(8,128)(2,1)S(1)} all-gather(bf16[10,18,192]{2,1,0:T(8,128)(2,1)S(1)} %copy.159), channel_id=2, replica_groups=mesh['face'=4,'tile'=8] {'tile'}, dimensions={0}, use_global_device_ids=true | all-gather | bytes 622080 | tf_op jit(solution)/shard_map/cond/branch_1_fun/all_gather | solution.py:172
  100.0 1.1 constant_dynamic-update-slice_fusion.3
  101.3 1.4 collective-permute-start
  102.7 1.5 collective-permute-start.2
  106.3 0.7 copy_bitcast_fusion
  107.1 0.8 maximum_bitcast_fusion
  107.9 18.0 %all-gather.1 = f32[8,52,384]{2,1,0:T(8,128)} all-gather(f32[1,52,384]{2,1,0:T(8,128)S(1)} %maximum_bitcast_fusion), channel_id=1, replica_groups=mesh['face'=4,'tile'=8] {'tile'}, dimensions={0}, use_global_device_ids=true | all-gather | bytes 718848 | tf_op jit(solution)/shard_map/cond/branch_1_fun/all_gather | solution.py:135
  125.9 2.0 reshape.244
  127.9 1.5 fusion
  129.4 17.8 %all_gather.18 = f32[512,384]{1,0:T(8,128)} all-gather(f32[128,384]{1,0:T(8,128)S(1)} %fusion), channel_id=1, replica_groups=mesh['face'=4,'tile'=8] {'face'}, dimensions={0}, use_global_device_ids=true | all-gather | bytes 983040 | tf_op jit(solution)/shard_map/cond/branch_1_fun/all_gather | solution.py:141
  147.9 1.5 fusion.8
  150.1 0.7 compare_select_fusion.1
  150.8 1.5 convolution_add_fusion
  152.4 0.8 fusion.6
  153.2 17.6 %all_gather.19 = bf16[8,128,384]{2,1,0:T(8,128)(2,1)} all-gather(bf16[1,128,384]{2,1,0:T(8,128)(2,1)} %bitcast.19), channel_id=1, replica_groups=mesh['face'=4,'tile'=8] {'tile'}, dimensions={0}, use_global_device_ids=true | all-gather | bytes 884736 | tf_op jit(solution)/shard_map/cond/branch_1_fun/all_gather | solution.py:172
  170.8 1.7 collective-permute-start.5
  172.5 1.3 collective-permute-start.4
  173.8 0.8 collective-permute-start.3
  174.6 1.2 constant_dynamic-update-slice_fusion.2
  175.8 1.2 constant_dynamic-update-slice_fusion.1
  177.0 1.2 constant_dynamic-update-slice_fusion
  178.2 3.7 %fusion.62 = (bf16[32,8,16,192]{3,0,2,1:T(8,128)(2,1)}, bf16[32,8,16,192]{3,0,2,1:T(8,128)(2,1)}, bf16[32,8,16,192]{3,0,2,1:T(8,128)(2,1)}, bf16[32,8,16,192]{3,...) fusion(bf16[32,10,18,192]{3,0,2,1:T(8,128)(2,1)S(1)} %constant_, ...), kind=kLoop, calls=%fused_computation.153 | loop fusion | bytes 28311552 | tf_op jit(solution)/shard_map/cond/branch_1_fun/slice | solution.py:237
  181.9 2.9 %copy.138 = bf16[32,8,16,192]{3,2,1,0:T(8,128)(2,1)S(1)} copy(bf16[32,8,16,192]{3,0,2,1:T(8,128)(2,1)} %get-tuple-element.157) | data formatting | bytes 3145728 | tf_op jit(solution)/shard_map/cond/branch_1_fun/slice | solution.py:237
  184.8 1.2 copy.137
  186.4 1.2 copy.136
  187.6 1.2 copy.135
  188.8 1.2 copy.134
  190.0 1.2 copy.133
  191.2 1.2 copy.132
  192.4 1.2 copy.131
  193.6 1.2 copy.130
  194.8 17.5 %collective-permute-done.4 = bf16[8,128,384]{2,1,0:T(8,128)(2,1)} collective-permute-done((bf16[8,128,384]{2,1,0:T(8,128)(2,1)}, bf16[8,128,384]{2,1,0:T(8,128)(2,1)}, u32[]{:S(2)}, u32[]{:S(2)}) %collective-permute-start.4) | collective-permute-done | bytes 786464 | tf_op jit(solution)/shard_map/cond/branch_1_fun/ppermute | solution.py:176
  212.3 2.3 pad_maximum_fusion
  214.6 1.8 convolution_dynamic-update-slice_fusion.8
  216.4 1.8 convolution_dynamic-update-slice_fusion.7
  218.1 1.8 convolution_dynamic-update-slice_fusion.6
  219.9 1.8 convolution_dynamic-update-slice_fusion.5
  221.6 1.8 convolution_dynamic-update-slice_fusion.4
  223.4 1.8 convolution_dynamic-update-slice_fusion.3
  225.1 1.8 convolution_dynamic-update-slice_fusion.2
  226.9 1.8 convolution_dynamic-update-slice_fusion.1
  228.6 1.8 convolution_dynamic-update-slice_fusion
  230.4 3.1 %multiply_reduce_fusion = f32[]{:T(128)} fusion(f32[1728,384]{1,0:T(8,128)} %convolution_dynamic-update-slice_fusion), kind=kLoop, calls=%fused_computation.1 | loop fusion | flops 1327103 | bytes 2654212 | tf_op jit(solution)/shard_map/reduce_sum | solution.py:267
  234.1 23.7 %all-reduce.15.cloned.1.call-done = f32[3456,384]{1,0:T(8,128)} async-done(((f32[3456,384]{1,0:T(8,128)}), f32[3456,384]{1,0:T(8,128)}) %all-reduce.15.cloned.1.call-update) | async-done | bytes 5308432 | tf_op jit(solution)/shard_map/psum | solution.py:227
  257.8 4.5 %multiply_reduce_fusion.1 = f32[]{:T(128)} fusion(f32[3456,384]{1,0:T(8,128)} %all-reduce.15.cloned.1.call-done), kind=kLoop, calls=%fused_computation.50 | loop fusion | flops 2654207 | bytes 5308420 | tf_op jit(solution)/shard_map/reduce_sum | solution.py:267
  262.9 3.2 %multiply_convert_fusion.1 = bf16[1728,384]{1,0:T(8,128)(2,1)} fusion(f32[1728,384]{1,0:T(8,128)} %get-tuple-element.91, f32[]{:T(128)S(6)} %rsqrt.3), kind=kLoop, calls=%fused_computation.51 | loop fusion | flops 1327104 | bytes 3981316 | tf_op jit(solution)/shard_map/convert_element_type | solution.py:269
  266.1 4.4 %multiply_convert_fusion = bf16[3456,384]{1,0:T(8,128)(2,1)} fusion(f32[3456,384]{1,0:T(8,128)} %all-reduce.15.cloned.1.call-done, f32[]{:T(128)S(6)} %rsqrt.3), kind=kLoop, calls=%fused_computation.49 | loop fusion | flops 2654208 | bytes 7962628 | tf_op jit(solution)/shard_map/convert_element_type | solution.py:270
  (97 shorter events, 10.3 us)
Async XLA Ops:
  7.2 63.0 %copy-start = (bf16[3,3,384,384]{3,2,1,0:T(8,128)(2,1)S(1)}, bf16[3,3,384,384]{3,2,1,0:T(8,128)(2,1)}, u32[]{:S(2)}) copy-start(bf16[3,3,384,384]{3,2,1,0:T(8,128)(2,1)} %param.19) | copy-start | bytes 7962628
  7.2 33.8 %copy-start.6 = (bf16[1,1,8,16,192]{4,3,2,1,0:T(8,128)(2,1)S(1)}, bf16[1,1,8,16,192]{4,3,2,1,0:T(8,128)(2,1)}, u32[]{:S(2)}) copy-start(bf16[1,1,8,16,192]{4,3,2,1,0:T(8,128)(2,1)} %param.16) | copy-start | bytes 147460
  7.2 250.6 %all-reduce.15.cloned.1.call-start = ((), (), s32[]{:S(2)}) async-start(), calls=%async_computation | async-start | bytes 10616832 | tf_op jit(solution)/shard_map/psum | solution.py:227
  36.1 0.6 copy-start.11
  36.1 0.6 copy-start.13
  37.4 0.5 copy-start.15
  37.7 0.6 copy-start.7
  37.7 0.6 copy-start.9
  70.0 0.9 copy-start.5
  74.2 0.7 copy-start.8
  74.2 0.7 copy-start.10
  77.1 27.2 %copy-start.4 = (f32[128,3456]{1,0:T(8,128)S(1)}, f32[128,3456]{1,0:T(8,128)}, u32[]{:S(2)}) copy-start(f32[128,3456]{1,0:T(8,128)} %get-tuple-element.75) | copy-start | bytes 5308420 | tf_op jit(solution)/shard_map/cond
  101.1 74.7 %collective-permute-start.1 = (bf16[8,10,18,192]{3,0,2,1:T(8,128)(2,1)}, bf16[8,10,18,192]{3,0,2,1:T(8,128)(2,1)}, u32[]{:S(2)}, u32[]{:S(2)}) collective-permute-start(bf16[8,10,18,192]{3,0,2,1:T(8,128)(2,1)} %get-tuple-element.156), channel_id=1, source_target_pairs={{0,16},{8,24},{16,0},{24,8},{1,17},{9,25},{17,1},{25,9},{2,18},{10... | collective-permute-start | bytes 1658888 | tf_op jit(solution)/shard_map/cond/branch_1_fun/ppermute | solution.py:176
  101.3 72.5 %collective-permute-start = (bf16[8,10,18,192]{3,0,2,1:T(8,128)(2,1)}, bf16[8,10,18,192]{3,0,2,1:T(8,128)(2,1)}, u32[]{:S(2)}, u32[]{:S(2)}) collective-permute-start(bf16[8,10,18,192]{3,0,2,1:T(8,128)(2,1)} %get-tuple-element.156), channel_id=1, source_target_pairs={{0,8},{8,16},{16,24},{24,0},{1,9},{9,17},{17,25},{25,1},{2,10},{10... | collective-permute-start | bytes 1658888 | tf_op jit(solution)/shard_map/cond/branch_1_fun/ppermute | solution.py:176
  102.7 74.3 %collective-permute-start.2 = (bf16[8,10,18,192]{3,0,2,1:T(8,128)(2,1)}, bf16[8,10,18,192]{3,0,2,1:T(8,128)(2,1)}, u32[]{:S(2)}, u32[]{:S(2)}) collective-permute-start(bf16[8,10,18,192]{3,0,2,1:T(8,128)(2,1)} %get-tuple-element.156), channel_id=1, source_target_pairs={{0,24},{8,0},{16,8},{24,16},{1,25},{9,1},{17,9},{25,17},{2,26},{10... | collective-permute-start | bytes 1658888 | tf_op jit(solution)/shard_map/cond/branch_1_fun/ppermute | solution.py:176
  104.6 44.8 %copy-start.12 = (s32[4]{0:T(128)S(1)}, s32[4]{0:T(128)}, u32[]{:S(2)}) copy-start(s32[4]{0:T(128)} %get-tuple-element.79) | copy-start | bytes 52 | tf_op jit(solution)/shard_map/cond
  107.9 40.1 %copy-start.14 = (s32[48]{0:T(128)S(1)}, s32[48]{0:T(128)}, u32[]{:S(2)}) copy-start(s32[48]{0:T(128)} %iota_add_fusion) | copy-start | bytes 580 | tf_op jit(solution)/shard_map/cond
  170.8 24.0 %collective-permute-start.5 = (bf16[8,128,384]{2,1,0:T(8,128)(2,1)}, bf16[8,128,384]{2,1,0:T(8,128)(2,1)}, u32[]{:S(2)}, u32[]{:S(2)}) collective-permute-start(bf16[8,128,384]{2,1,0:T(8,128)(2,1)} %all_gather.19), channel_id=1, source_target_pairs={{0,24},{8,0},{16,8},{24,16},{1,25},{9,1},{17,9},{25,17},{2,26},{10... | collective-permute-start | bytes 2359304 | tf_op jit(solution)/shard_map/cond/branch_1_fun/ppermute | solution.py:176
  172.5 39.7 %collective-permute-start.4 = (bf16[8,128,384]{2,1,0:T(8,128)(2,1)}, bf16[8,128,384]{2,1,0:T(8,128)(2,1)}, u32[]{:S(2)}, u32[]{:S(2)}) collective-permute-start(bf16[8,128,384]{2,1,0:T(8,128)(2,1)} %all_gather.19), channel_id=1, source_target_pairs={{0,16},{8,24},{16,0},{24,8},{1,17},{9,25},{17,1},{25,9},{2,18},{10... | collective-permute-start | bytes 2359304 | tf_op jit(solution)/shard_map/cond/branch_1_fun/ppermute | solution.py:176
  173.8 38.5 %collective-permute-start.3 = (bf16[8,128,384]{2,1,0:T(8,128)(2,1)}, bf16[8,128,384]{2,1,0:T(8,128)(2,1)}, u32[]{:S(2)}, u32[]{:S(2)}) collective-permute-start(bf16[8,128,384]{2,1,0:T(8,128)(2,1)} %all_gather.19), channel_id=1, source_target_pairs={{0,8},{8,16},{16,24},{24,0},{1,9},{9,17},{17,25},{25,1},{2,10},{10... | collective-permute-start | bytes 2359304 | tf_op jit(solution)/shard_map/cond/branch_1_fun/ppermute | solution.py:176
  181.9 2.9 %copy-start.3 = (bf16[32,8,16,192]{3,0,2,1:T(8,128)(2,1)S(1)}, bf16[32,8,16,192]{3,0,2,1:T(8,128)(2,1)}, u32[]{:S(2)}) copy-start(bf16[32,8,16,192]{3,0,2,1:T(8,128)(2,1)} %get-tuple-element.158) | copy-start | bytes 4718596 | tf_op jit(solution)/shard_map/cond
  184.8 1.6 copy-start.2
  262.9 7.6 %copy-start.1 = (bf16[3,3,384,384]{3,2,1,0:T(8,128)(2,1)S(1)}, bf16[3,3,384,384]{3,2,1,0:T(8,128)(2,1)}, u32[]{:S(2)}) copy-start(bf16[3,3,384,384]{3,2,1,0:T(8,128)(2,1)} %param.19) | copy-start | bytes 7962628
Sparse Core Ops, SparseCore 0:
  74.3 183.4 all-reduce.14

commit v12 on v11

--- a/solution.py
+++ b/solution.py
@@ -111,8 +111,12 @@
         rims,
         preferred_element_type=jnp.float32,
     ).astype(cells.dtype)
-    edge_set = lax.all_gather(edges, "face", axis=0, tiled=True)
-    pool = jnp.concatenate([rims, edge_set], axis=0)
+    faces = lax.axis_size("face")
+    parts = [edges]
+    for shift in range(1, faces):
+        pairs = [(i, (i + shift) % faces) for i in range(faces)]
+        parts.append(lax.ppermute(edges, "face", pairs))
+    pool = jnp.concatenate([rims] + parts, axis=0)
     halo = jnp.dot(
         one_hot(source, jnp.arange(pool.shape[0]), cells.dtype),
         pool,
@@ -187,7 +191,9 @@
     link_row = lax.dynamic_index_in_dim(seam_link, face_pos, 0, False)
     turn_row = lax.dynamic_index_in_dim(seam_turn, face_pos, 0, False)
     maps = face_maps(tiles, height, breadth)
-    source = halo_source(maps, place, link_row, turn_row)
+    faces = lax.axis_size("face")
+    offset_row = ((face_pos - link_row // 4) % faces) * 4 + link_row % 4
+    source = halo_source(maps, place, offset_row, turn_row)
     padded_tile_in = padded_tile(cells, maps, source)
     unfolded_in = unfold(padded_tile_in, height, breadth)
     pre_one = jnp.dot(

time: 278 us -> 279 us (level)
  blocking collectives: 125 us -> 107 us
  starting transfers between devices: 6.88 us -> 16.1 us
  waiting for transfers between devices: 41.2 us -> 45.1 us
  local copies, waits for them, and re-layouts: 35.1 us -> 38.2 us
    all_gather x2 -> x0, blocking collectives: 18.2 us -> none  [padded_tile(): edge_set = lax.all_gather(edges, 'face', axis=0, tiled=True)]
    ppermute x0 -> x6, starting transfers between devices: none -> 7.6 us  [padded_tile(): parts.append(lax.ppermute(edges, 'face', pairs))]
    ppermute x0 -> x6, waiting for transfers between devices: none -> 4.09 us  [padded_tile(): parts.append(lax.ppermute(edges, 'face', pairs))]
  transfers between devices with their start and end apart: 7 -> 13, of which waited for: 2 -> 4; matrix products, arithmetic and copies ran while one was open for 21% -> 23% of each run, Pallas kernels for 0% -> 0%
where the time goes in v12:
time: 279 us; the launch traced here: 278 us
  blocking collectives  107 us (38%)
  waiting for transfers between devices  45.1 us (16%)
  local copies, waits for them, and re-layouts  38.2 us (14%)
  matrix products  31.5 us (11%)
  other arithmetic  23.8 us (9%)
  starting transfers between devices  16.1 us (6%)
  between operations  15.1 us (5%)
    all_gather x2, blocking collectives, gather_all(): local = lax.all_gather(block, 'tile', axis=0, tiled=True)  40.4 us
    all_gather x2, blocking collectives, padded_tile(): rims = lax.all_gather(rim_of(cells), 'tile', axis=0, tiled=True)  30.2 us
    psum x1, waiting for transfers between devices, body(): total_out = lax.psum(grad_w_out, ('face', 'tile'))  23.9 us
    all_gather x1, blocking collectives, return_border(): seam_set = lax.all_gather(seam_sum, 'face', axis=0, tiled=True)  18.9 us
    all_gather x1, blocking collectives, return_border(): borders = lax.all_gather(border, 'tile', axis=0, tiled=True)  17.8 us
    ppermute x6, waiting for transfers between devices, gather_all(): parts.append(lax.ppermute(local, 'face', pairs))  17.2 us
    slice x10, local copies, waits for them, and re-layouts, rest(): every_pad[:, down_step:down_step + height, side_step:side_step + breadth]  16.1 us
    dot_general x9, matrix products, rest(): lax.dot_general(window.reshape(-1, width_in), every_grad, (((0,), (0,)),...  15.8 us
  transfers between devices with their start and end apart: 13, of which 4 were waited for; matrix products, arithmetic and copies ran while one was open for 23% of the time, Pallas kernels for 0%

profile of v12, /device:TPU:0, one launch (start us, length us, event | category | flops | bytes accessed | tf_op | source)
XLA Modules:
  0.0 278.0 jit_solution(13983565943325639530)
XLA Ops:
  7.2 0.9 slice_bitcast_fusion.9
  8.1 0.9 copy.187
  9.0 15.9 %all_gather.18 = bf16[384,192]{1,0:T(8,128)(2,1)S(1)} all-gather(bf16[48,192]{1,0:T(8,128)(2,1)S(1)} %pad_maximum_fusion.9), channel_id=1, replica_groups=mesh['face'=4,'tile'=8] {'tile'}, dimensions={0}, use_global_device_ids=true | all-gather | bytes 165888 | tf_op jit(solution)/shard_map/all_gather | solution.py:108
  24.9 0.9 convolution_convert_fusion.1
  25.8 2.5 collective-permute-start.8
  30.9 1.3 fusion.46
  36.6 1.3 convolution_convert_fusion.3
  41.1 1.1 concatenate.80
  42.2 1.7 multiply_convert_fusion.2
  44.1 14.3 %all_gather.19 = bf16[384,384]{1,0:T(8,128)(2,1)S(1)} all-gather(bf16[48,384]{1,0:T(8,128)(2,1)S(1)} %pad_maximum_fusion.8), channel_id=1, replica_groups=mesh['face'=4,'tile'=8] {'tile'}, dimensions={0}, use_global_device_ids=true | all-gather | bytes 331776 | tf_op jit(solution)/shard_map/all_gather | solution.py:108
  58.4 0.9 constant_dynamic-update-slice_fusion.12
  59.4 2.4 collective-permute-start.9
  62.4 1.0 collective-permute-start.10
  63.4 2.6 collective-permute-done.9
  66.0 1.5 collective-permute-done.10
  69.1 3.3 %fusion.20 = f32[3456,384]{1,0:T(8,128)} fusion(bf16[128,3456]{1,0:T(8,128)(2,1)S(1)} %constant_dynamic-update-slice_fusion.14, f32[128,384]{1,0:T(8,128)S(1)} %fusion.67, bf16[128,384]{1,0:T(8,128)(2,1)S(1)} %bitcast.195), kind=kOutput, calls=%fused_computation.64 | convolution fusion | flops 340279296 | bytes 6488064 | tf_op jit(solution)/shard_map/dot_general | solution.py:208
  73.2 2.1 fusion.22
  75.3 159.3 %conditional.1 = (f32[1728,384]{1,0:T(8,128)}, bf16[1,1,8,16,384]{4,3,2,1,0:T(8,128)(2,1)}, f32[]{:T(128)}) conditional(s32[]{:T(128)} %convert_element_type.61, () %tuple.20, (bf16[10,18,192]{2,0,1:T(8,128)(2,1)S(1)}, f32[128,3456]{1,0:T(8,128)}, s32[]{:T(128)}, (), (), /*index=5*/s32[1,4]{1,0:T(1,128)}, s32[4]{0:T(128)}, (), (), ...), branch_computations={%region_2.3_spmd, %region_3.7_spmd} | conditional | flops 5893907456 | bytes 165973952 | solution.py:260
  75.4 22.9 %all-gather = bf16[80,18,192]{2,1,0:T(8,128)(2,1)S(1)} all-gather(bf16[10,18,192]{2,1,0:T(8,128)(2,1)S(1)} %copy.176), channel_id=2, replica_groups=mesh['face'=4,'tile'=8] {'tile'}, dimensions={0}, use_global_device_ids=true | all-gather | bytes 622080 | tf_op jit(solution)/shard_map/cond/branch_1_fun/all_gather | solution.py:176
  98.3 1.1 constant_dynamic-update-slice_fusion.3
  99.4 1.0 collective-permute-start.1
  100.4 2.6 collective-permute-start
  103.0 0.9 collective-permute-start.2
  106.8 0.8 maximum_bitcast_fusion
  107.6 17.8 %all-gather.1 = f32[8,52,384]{2,1,0:T(8,128)} all-gather(f32[1,52,384]{2,1,0:T(8,128)S(1)} %maximum_bitcast_fusion), channel_id=1, replica_groups=mesh['face'=4,'tile'=8] {'tile'}, dimensions={0}, use_global_device_ids=true | all-gather | bytes 718848 | tf_op jit(solution)/shard_map/cond/branch_1_fun/all_gather | solution.py:139
  125.4 2.0 reshape.244
  127.4 1.6 fusion
  129.0 18.9 %all_gather.14 = f32[512,384]{1,0:T(8,128)} all-gather(f32[128,384]{1,0:T(8,128)S(1)} %fusion), channel_id=1, replica_groups=mesh['face'=4,'tile'=8] {'face'}, dimensions={0}, use_global_device_ids=true | all-gather | bytes 983040 | tf_op jit(solution)/shard_map/cond/branch_1_fun/all_gather | solution.py:145
  148.6 1.5 fusion.8
  150.1 0.8 select_reduce_fusion.1
  151.5 1.5 convolution_add_fusion
  153.1 0.8 fusion.6
  153.9 17.5 %all_gather.15 = bf16[8,128,384]{2,1,0:T(8,128)(2,1)} all-gather(bf16[1,128,384]{2,1,0:T(8,128)(2,1)} %bitcast.20), channel_id=1, replica_groups=mesh['face'=4,'tile'=8] {'tile'}, dimensions={0}, use_global_device_ids=true | all-gather | bytes 884736 | tf_op jit(solution)/shard_map/cond/branch_1_fun/all_gather | solution.py:176
  171.4 1.9 collective-permute-start.5
  173.3 1.4 collective-permute-start.4
  175.4 1.2 constant_dynamic-update-slice_fusion.2
  176.6 1.2 constant_dynamic-update-slice_fusion.1
  177.8 1.2 constant_dynamic-update-slice_fusion
  179.0 3.6 %fusion.57 = (bf16[32,8,16,192]{3,0,2,1:T(8,128)(2,1)}, bf16[32,8,16,192]{3,0,2,1:T(8,128)(2,1)}, bf16[32,8,16,192]{3,0,2,1:T(8,128)(2,1)}, bf16[32,8,16,192]{3,...) fusion(bf16[32,10,18,192]{3,0,2,1:T(8,128)(2,1)S(1)} %constant_, ...), kind=kLoop, calls=%fused_computation.166 | loop fusion | bytes 28311552 | tf_op jit(solution)/shard_map/cond/branch_1_fun/slice | solution.py:243
  182.7 2.9 %copy.152 = bf16[32,8,16,192]{3,2,1,0:T(8,128)(2,1)S(1)} copy(bf16[32,8,16,192]{3,0,2,1:T(8,128)(2,1)} %get-tuple-element.160) | data formatting | bytes 3145728 | tf_op jit(solution)/shard_map/cond/branch_1_fun/slice | solution.py:243
  185.6 1.2 copy.151
  187.2 1.2 copy.150
  188.4 1.2 copy.149
  189.6 1.2 copy.148
  190.8 1.2 copy.147
  192.0 1.2 copy.146
  193.2 1.2 copy.145
  194.4 1.2 copy.144
  195.6 17.2 %collective-permute-done.4 = bf16[8,128,384]{2,1,0:T(8,128)(2,1)} collective-permute-done((bf16[8,128,384]{2,1,0:T(8,128)(2,1)}, bf16[8,128,384]{2,1,0:T(8,128)(2,1)}, u32[]{:S(2)}, u32[]{:S(2)}) %collective-permute-start.4) | collective-permute-done | bytes 786464 | tf_op jit(solution)/shard_map/cond/branch_1_fun/ppermute | solution.py:180
  212.7 2.3 pad_maximum_fusion
  215.1 1.8 convolution_dynamic-update-slice_fusion.8
  216.8 1.8 convolution_dynamic-update-slice_fusion.7
  218.6 1.8 convolution_dynamic-update-slice_fusion.6
  220.3 1.8 convolution_dynamic-update-slice_fusion.5
  222.1 1.8 convolution_dynamic-update-slice_fusion.4
  223.8 1.8 convolution_dynamic-update-slice_fusion.3
  225.6 1.8 convolution_dynamic-update-slice_fusion.2
  227.3 1.8 convolution_dynamic-update-slice_fusion.1
  229.1 1.8 convolution_dynamic-update-slice_fusion
  230.8 3.1 %multiply_reduce_fusion = f32[]{:T(128)} fusion(f32[1728,384]{1,0:T(8,128)} %convolution_dynamic-update-slice_fusion), kind=kLoop, calls=%fused_computation.1 | loop fusion | flops 1327103 | bytes 2654212 | tf_op jit(solution)/shard_map/reduce_sum | solution.py:273
  234.6 23.9 %all-reduce.15.cloned.1.call-done = f32[3456,384]{1,0:T(8,128)} async-done(((f32[3456,384]{1,0:T(8,128)}), f32[3456,384]{1,0:T(8,128)}) %all-reduce.15.cloned.1.call-update) | async-done | bytes 5308432 | tf_op jit(solution)/shard_map/psum | solution.py:233
  258.5 4.5 %multiply_reduce_fusion.1 = f32[]{:T(128)} fusion(f32[3456,384]{1,0:T(8,128)} %all-reduce.15.cloned.1.call-done), kind=kLoop, calls=%fused_computation.50 | loop fusion | flops 2654207 | bytes 5308420 | tf_op jit(solution)/shard_map/reduce_sum | solution.py:273
  263.6 3.2 %multiply_convert_fusion.1 = bf16[1728,384]{1,0:T(8,128)(2,1)} fusion(f32[1728,384]{1,0:T(8,128)} %get-tuple-element.92, f32[]{:T(128)S(6)} %rsqrt.3), kind=kLoop, calls=%fused_computation.51 | loop fusion | flops 1327104 | bytes 3981316 | tf_op jit(solution)/shard_map/convert_element_type | solution.py:275
  266.8 4.4 %multiply_convert_fusion = bf16[3456,384]{1,0:T(8,128)(2,1)} fusion(f32[3456,384]{1,0:T(8,128)} %all-reduce.15.cloned.1.call-done, f32[]{:T(128)S(6)} %rsqrt.3), kind=kLoop, calls=%fused_computation.49 | loop fusion | flops 2654208 | bytes 7962628 | tf_op jit(solution)/shard_map/convert_element_type | solution.py:276
  (119 shorter events, 18.3 us)
Async XLA Ops:
  7.2 61.3 %copy-start = (bf16[3,3,384,384]{3,2,1,0:T(8,128)(2,1)S(1)}, bf16[3,3,384,384]{3,2,1,0:T(8,128)(2,1)}, u32[]{:S(2)}) copy-start(bf16[3,3,384,384]{3,2,1,0:T(8,128)(2,1)} %param.19) | copy-start | bytes 7962628
  7.2 33.9 %copy-start.6 = (bf16[1,1,8,16,192]{4,3,2,1,0:T(8,128)(2,1)S(1)}, bf16[1,1,8,16,192]{4,3,2,1,0:T(8,128)(2,1)}, u32[]{:S(2)}) copy-start(bf16[1,1,8,16,192]{4,3,2,1,0:T(8,128)(2,1)} %param.16) | copy-start | bytes 147460
  7.2 251.3 %all-reduce.15.cloned.1.call-start = ((), (), s32[]{:S(2)}) async-start(), calls=%async_computation | async-start | bytes 10616832 | tf_op jit(solution)/shard_map/psum | solution.py:233
  25.8 10.0 %collective-permute-start.8 = (bf16[128,192]{0,1:T(8,128)(2,1)S(1)}, bf16[128,192]{0,1:T(8,128)(2,1)S(1)}, u32[]{:S(2)}, u32[]{:S(2)}) collective-permute-start(bf16[128,192]{0,1:T(8,128)(2,1)S(1)} %convolution_convert_fusion.1), channel_id=1, source_target_pairs={{0,24},{8,0},{16,8},{24,16},{1,25},{9,1},{17,9},{25,17},{2,26},{10... | collective-permute-start | bytes 147464 | tf_op jit(solution)/shard_map/ppermute | solution.py:118
  28.3 6.8 %collective-permute-start.7 = (bf16[128,192]{0,1:T(8,128)(2,1)S(1)}, bf16[128,192]{0,1:T(8,128)(2,1)S(1)}, u32[]{:S(2)}, u32[]{:S(2)}) collective-permute-start(bf16[128,192]{0,1:T(8,128)(2,1)S(1)} %convolution_convert_fusion.1), channel_id=1, source_target_pairs={{0,16},{8,24},{16,0},{24,8},{1,17},{9,25},{17,1},{25,9},{2,18},{10... | collective-permute-start | bytes 147464 | tf_op jit(solution)/shard_map/ppermute | solution.py:118
  28.8 5.5 %collective-permute-start.6 = (bf16[128,192]{0,1:T(8,128)(2,1)S(1)}, bf16[128,192]{0,1:T(8,128)(2,1)S(1)}, u32[]{:S(2)}, u32[]{:S(2)}) collective-permute-start(bf16[128,192]{0,1:T(8,128)(2,1)S(1)} %convolution_convert_fusion.1), channel_id=1, source_target_pairs={{0,8},{8,16},{16,24},{24,0},{1,9},{9,17},{17,25},{25,1},{2,10},{10... | collective-permute-start | bytes 147464 | tf_op jit(solution)/shard_map/ppermute | solution.py:118
  30.9 3.4 %copy-start.14 = (s32[4]{0:T(128)}, s32[4]{0:T(128)S(1)}, u32[]{:S(2)}) copy-start(s32[4]{0:T(128)S(1)} %fusion.41) | copy-start | bytes 52
  33.7 4.3 %copy-start.11 = (s32[52]{0:T(128)}, s32[52]{0:T(128)S(1)}, u32[]{:S(2)}) copy-start(s32[52]{0:T(128)S(1)} %compare_select_fusion.2) | copy-start | bytes 628
  37.9 0.6 copy-start.7
  37.9 0.6 copy-start.9
  42.2 25.3 %copy-start.12 = (s32[52]{0:T(128)S(1)}, s32[52]{0:T(128)}, u32[]{:S(2)}) copy-start(s32[52]{0:T(128)} %copy-done.11) | copy-start | bytes 628
  59.4 6.6 %collective-permute-start.9 = (bf16[128,384]{1,0:T(8,128)(2,1)S(1)}, bf16[128,384]{1,0:T(8,128)(2,1)S(1)}, u32[]{:S(2)}, u32[]{:S(2)}) collective-permute-start(bf16[128,384]{1,0:T(8,128)(2,1)S(1)} %get-tuple-element.227), channel_id=1, source_target_pairs={{0,8},{8,16},{16,24},{24,0},{1,9},{9,17},{17,25},{25,1},{2,10},{10... | collective-permute-start | bytes 294920 | tf_op jit(solution)/shard_map/ppermute | solution.py:118
  61.8 5.7 %collective-permute-start.11 = (bf16[128,384]{1,0:T(8,128)(2,1)S(1)}, bf16[128,384]{1,0:T(8,128)(2,1)S(1)}, u32[]{:S(2)}, u32[]{:S(2)}) collective-permute-start(bf16[128,384]{1,0:T(8,128)(2,1)S(1)} %get-tuple-element.227), channel_id=1, source_target_pairs={{0,24},{8,0},{16,8},{24,16},{1,25},{9,1},{17,9},{25,17},{2,26},{10... | collective-permute-start | bytes 294920 | tf_op jit(solution)/shard_map/ppermute | solution.py:118
  62.4 5.1 %collective-permute-start.10 = (bf16[128,384]{1,0:T(8,128)(2,1)S(1)}, bf16[128,384]{1,0:T(8,128)(2,1)S(1)}, u32[]{:S(2)}, u32[]{:S(2)}) collective-permute-start(bf16[128,384]{1,0:T(8,128)(2,1)S(1)} %get-tuple-element.227), channel_id=1, source_target_pairs={{0,16},{8,24},{16,0},{24,8},{1,17},{9,25},{17,1},{25,9},{2,18},{10... | collective-permute-start | bytes 294920 | tf_op jit(solution)/shard_map/ppermute | solution.py:118
  68.2 0.9 copy-start.5
  72.4 0.7 copy-start.8
  72.4 0.7 copy-start.10
  75.3 28.6 %copy-start.4 = (f32[128,3456]{1,0:T(8,128)S(1)}, f32[128,3456]{1,0:T(8,128)}, u32[]{:S(2)}) copy-start(f32[128,3456]{1,0:T(8,128)} %get-tuple-element.76) | copy-start | bytes 5308420 | tf_op jit(solution)/shard_map/cond
  99.4 77.2 %collective-permute-start.1 = (bf16[8,10,18,192]{3,0,2,1:T(8,128)(2,1)}, bf16[8,10,18,192]{3,0,2,1:T(8,128)(2,1)}, u32[]{:S(2)}, u32[]{:S(2)}) collective-permute-start(bf16[8,10,18,192]{3,0,2,1:T(8,128)(2,1)} %get-tuple-element.157), channel_id=1, source_target_pairs={{0,16},{8,24},{16,0},{24,8},{1,17},{9,25},{17,1},{25,9},{2,18},{10... | collective-permute-start | bytes 1658888 | tf_op jit(solution)/shard_map/cond/branch_1_fun/ppermute | solution.py:180
  100.4 74.4 %collective-permute-start = (bf16[8,10,18,192]{3,0,2,1:T(8,128)(2,1)}, bf16[8,10,18,192]{3,0,2,1:T(8,128)(2,1)}, u32[]{:S(2)}, u32[]{:S(2)}) collective-permute-start(bf16[8,10,18,192]{3,0,2,1:T(8,128)(2,1)} %get-tuple-element.157), channel_id=1, source_target_pairs={{0,8},{8,16},{16,24},{24,0},{1,9},{9,17},{17,25},{25,1},{2,10},{10... | collective-permute-start | bytes 1658888 | tf_op jit(solution)/shard_map/cond/branch_1_fun/ppermute | solution.py:180
  103.0 74.8 %collective-permute-start.2 = (bf16[8,10,18,192]{3,0,2,1:T(8,128)(2,1)}, bf16[8,10,18,192]{3,0,2,1:T(8,128)(2,1)}, u32[]{:S(2)}, u32[]{:S(2)}) collective-permute-start(bf16[8,10,18,192]{3,0,2,1:T(8,128)(2,1)} %get-tuple-element.157), channel_id=1, source_target_pairs={{0,24},{8,0},{16,8},{24,16},{1,25},{9,1},{17,9},{25,17},{2,26},{10... | collective-permute-start | bytes 1658888 | tf_op jit(solution)/shard_map/cond/branch_1_fun/ppermute | solution.py:180
  104.2 44.3 %copy-start.13 = (s32[416]{0:T(512)S(1)}, s32[416]{0:T(512)}, u32[]{:S(2)}) copy-start(s32[416]{0:T(512)} %constant.147.clone.1) | copy-start | bytes 4996 | tf_op jit(solution)/shard_map/cond
  107.5 41.0 %copy-start.15 = (s32[48]{0:T(128)S(1)}, s32[48]{0:T(128)}, u32[]{:S(2)}) copy-start(s32[48]{0:T(128)} %iota_add_fusion) | copy-start | bytes 580 | tf_op jit(solution)/shard_map/cond
  171.4 24.1 %collective-permute-start.5 = (bf16[8,128,384]{2,1,0:T(8,128)(2,1)}, bf16[8,128,384]{2,1,0:T(8,128)(2,1)}, u32[]{:S(2)}, u32[]{:S(2)}) collective-permute-start(bf16[8,128,384]{2,1,0:T(8,128)(2,1)} %all_gather.15), channel_id=1, source_target_pairs={{0,24},{8,0},{16,8},{24,16},{1,25},{9,1},{17,9},{25,17},{2,26},{10... | collective-permute-start | bytes 2359304 | tf_op jit(solution)/shard_map/cond/branch_1_fun/ppermute | solution.py:180
  173.3 39.4 %collective-permute-start.4 = (bf16[8,128,384]{2,1,0:T(8,128)(2,1)}, bf16[8,128,384]{2,1,0:T(8,128)(2,1)}, u32[]{:S(2)}, u32[]{:S(2)}) collective-permute-start(bf16[8,128,384]{2,1,0:T(8,128)(2,1)} %all_gather.15), channel_id=1, source_target_pairs={{0,16},{8,24},{16,0},{24,8},{1,17},{9,25},{17,1},{25,9},{2,18},{10... | collective-permute-start | bytes 2359304 | tf_op jit(solution)/shard_map/cond/branch_1_fun/ppermute | solution.py:180
  174.7 38.0 %collective-permute-start.3 = (bf16[8,128,384]{2,1,0:T(8,128)(2,1)}, bf16[8,128,384]{2,1,0:T(8,128)(2,1)}, u32[]{:S(2)}, u32[]{:S(2)}) collective-permute-start(bf16[8,128,384]{2,1,0:T(8,128)(2,1)} %all_gather.15), channel_id=1, source_target_pairs={{0,8},{8,16},{16,24},{24,0},{1,9},{9,17},{17,25},{25,1},{2,10},{10... | collective-permute-start | bytes 2359304 | tf_op jit(solution)/shard_map/cond/branch_1_fun/ppermute | solution.py:180
  182.7 2.9 %copy-start.3 = (bf16[32,8,16,192]{3,0,2,1:T(8,128)(2,1)S(1)}, bf16[32,8,16,192]{3,0,2,1:T(8,128)(2,1)}, u32[]{:S(2)}) copy-start(bf16[32,8,16,192]{3,0,2,1:T(8,128)(2,1)} %get-tuple-element.161) | copy-start | bytes 4718596 | tf_op jit(solution)/shard_map/cond
  185.6 1.6 copy-start.2
  263.6 7.6 %copy-start.1 = (bf16[3,3,384,384]{3,2,1,0:T(8,128)(2,1)S(1)}, bf16[3,3,384,384]{3,2,1,0:T(8,128)(2,1)}, u32[]{:S(2)}) copy-start(bf16[3,3,384,384]{3,2,1,0:T(8,128)(2,1)} %param.19) | copy-start | bytes 7962628
Sparse Core Ops, SparseCore 0:
  72.6 185.8 all-reduce.14

commit v13 on v11

--- a/solution.py
+++ b/solution.py
@@ -3,11 +3,23 @@
 import jax.numpy as jnp
 from jax import lax
 from jax.sharding import PartitionSpec as P
+from jax.experimental import pallas as pl
 
 root_half = 0.7071067811865476
 inv_root_tau = 0.3989422804014327
 epsilon = 1e-06
 factor_budget = 48 * 2**20
+
+
+def scale_kernel(in_ref, out_ref, update_in_ref, update_out_ref):
+    grad_in = in_ref[...]
+    grad_out = out_ref[...]
+    squares = jnp.sum(grad_in * grad_in, axis=(0, 1), keepdims=True) + jnp.sum(
+        grad_out * grad_out, axis=(0, 1), keepdims=True
+    )
+    factor = lax.rsqrt(squares / (grad_in.size + grad_out.size) + epsilon)
+    update_in_ref[...] = (grad_in * factor).astype(update_in_ref.dtype)
+    update_out_ref[...] = (grad_out * factor).astype(update_out_ref.dtype)
 
 
 def gelu_value(pre):
@@ -264,10 +276,13 @@
         total = lax.psum(jnp.concatenate([grad_w_in, grad_w_out], axis=0), ("face", "tile"))
         total_in = total[:size_in]
         total_out = total[size_in:]
-    squares = jnp.sum(total_in * total_in) + jnp.sum(total_out * total_out)
-    factor = lax.rsqrt(squares / (total_in.size + total_out.size) + epsilon)
-    update_in = (total_in * factor).astype(jnp.bfloat16)
-    update_out = (total_out * factor).astype(jnp.bfloat16)
+    update_in, update_out = pl.pallas_call(
+        scale_kernel,
+        out_shape=(
+            jax.ShapeDtypeStruct(total_in.shape, jnp.bfloat16),
+            jax.ShapeDtypeStruct(total_out.shape, jnp.bfloat16),
+        ),
+    )(total_in, total_out)
     update_in = update_in.reshape(3, 3, width_in, width_out)
     update_out = update_out.reshape(3, 3, width_out, width_out)
     return (grad_one[None, None], update_in, update_out)

time: 278 us -> 271 us (0.975)
  other arithmetic: 22.3 us -> 7.27 us
  Pallas kernels: 0 us -> 7.41 us
  waiting for transfers between devices: 41.2 us -> 44.6 us
    convert_element_type x2 -> x0, other arithmetic: 7.58 us -> none  [the longest x1 4.42 us: body(): update_out = (total_out * factor).astype(jnp.bfloat16)]
    reduce_sum x2 -> x0, other arithmetic: 7.54 us -> none  [body(): squares = jnp.sum(total_in * total_in) + jnp.sum(total_out * total_out)]
    pallas_call x0 -> x1, Pallas kernels: none -> 7.41 us  [body(): pl.pallas_call(scale_kernel, out_shape=(jax.ShapeDtypeStruct(total_in.sha...]
    cond x15 -> x13, local copies, waits for them, and re-layouts: 6.69 us -> 6.71 us
  transfers between devices with their start and end apart: 7 -> 7, of which waited for: 2 -> 2; matrix products, arithmetic and copies ran while one was open for 21% -> 20% of each run, Pallas kernels for 0% -> 0%
where the time goes in v13:
time: 271 us; the launch traced here: 270 us
  blocking collectives  124 us (46%)
  waiting for transfers between devices  44.6 us (16%)
  local copies, waits for them, and re-layouts  35.1 us (13%)
  matrix products  29.9 us (11%)
  between operations  14.4 us (5%)
  Pallas kernels  7.41 us (3%)
  other arithmetic  7.27 us (3%)
  starting transfers between devices  6.99 us (3%)
    all_gather x2, blocking collectives, gather_all(): local = lax.all_gather(block, 'tile', axis=0, tiled=True)  39.9 us
    all_gather x2, blocking collectives, padded_tile(): rims = lax.all_gather(rim_of(cells), 'tile', axis=0, tiled=True)  30.2 us
    psum x1, waiting for transfers between devices, body(): total_out = lax.psum(grad_w_out, ('face', 'tile'))  25.9 us
    ppermute x6, waiting for transfers between devices, gather_all(): parts.append(lax.ppermute(local, 'face', pairs))  18.7 us
    all_gather x1, blocking collectives, return_border(): borders = lax.all_gather(border, 'tile', axis=0, tiled=True)  18.3 us
    all_gather x2, blocking collectives, padded_tile(): edge_set = lax.all_gather(edges, 'face', axis=0, tiled=True)  18.2 us
    all_gather x1, blocking collectives, return_border(): seam_set = lax.all_gather(seam_sum, 'face', axis=0, tiled=True)  17.6 us
    slice x10, local copies, waits for them, and re-layouts, rest(): every_pad[:, down_step:down_step + height, side_step:side_step + breadth]  16.1 us
  transfers between devices with their start and end apart: 7, of which 2 were waited for; matrix products, arithmetic and copies ran while one was open for 20% of the time, Pallas kernels for 0%

profile of v13, /device:TPU:0, one launch (start us, length us, event | category | flops | bytes accessed | tf_op | source)
XLA Modules:
  0.0 270.2 jit_solution(2581227879942629230)
XLA Ops:
  7.2 0.9 slice_bitcast_fusion.9
  8.1 0.9 copy.170
  9.0 15.9 %all_gather.24 = bf16[384,192]{1,0:T(8,128)(2,1)S(1)} all-gather(bf16[48,192]{1,0:T(8,128)(2,1)S(1)} %pad_maximum_fusion.9), channel_id=1, replica_groups=mesh['face'=4,'tile'=8] {'tile'}, dimensions={0}, use_global_device_ids=true | all-gather | bytes 165888 | tf_op jit(solution)/shard_map/all_gather | solution.py:120
  25.0 0.9 convolution_convert_fusion.1
  26.0 8.7 %all_gather.25 = bf16[512,192]{0,1:T(8,128)(2,1)S(1)} all-gather(bf16[128,192]{0,1:T(8,128)(2,1)S(1)} %convolution_convert_fusion.1), channel_id=1, replica_groups=mesh['face'=4,'tile'=8] {'face'}, dimensions={0}, use_global_device_ids=true | all-gather | bytes 245760 | tf_op jit(solution)/shard_map/all_gather | solution.py:126
  34.7 0.7 fusion.45
  35.4 0.7 fusion.46
  36.7 0.7 compare_select_fusion.2
  40.9 1.1 concatenate.80
  42.1 1.7 multiply_convert_fusion
  43.9 14.3 %all_gather.26 = bf16[384,384]{1,0:T(8,128)(2,1)S(1)} all-gather(bf16[48,384]{1,0:T(8,128)(2,1)S(1)} %pad_maximum_fusion.8), channel_id=1, replica_groups=mesh['face'=4,'tile'=8] {'tile'}, dimensions={0}, use_global_device_ids=true | all-gather | bytes 331776 | tf_op jit(solution)/shard_map/all_gather | solution.py:120
  58.2 0.9 convolution_convert_fusion
  59.2 9.5 %all_gather.27 = bf16[512,384]{1,0:T(8,128)(2,1)S(1)} all-gather(bf16[128,384]{1,0:T(8,128)(2,1)S(1)} %convolution_convert_fusion), channel_id=1, replica_groups=mesh['face'=4,'tile'=8] {'face'}, dimensions={0}, use_global_device_ids=true | all-gather | bytes 491520 | tf_op jit(solution)/shard_map/all_gather | solution.py:126
  68.7 0.9 convolution_convert_fusion.2
  70.8 3.3 %fusion.26 = f32[3456,384]{1,0:T(8,128)} fusion(bf16[128,3456]{1,0:T(8,128)(2,1)S(1)} %constant_dynamic-update-slice_fusion.4, f32[128,384]{1,0:T(8,128)S(1)} %fusion.72, bf16[128,384]{1,0:T(8,128)(2,1)S(1)} %bitcast.190), kind=kOutput, calls=%fused_computation.66 | convolution fusion | flops 340279296 | bytes 6488064 | tf_op jit(solution)/shard_map/dot_general | solution.py:214
  74.1 0.7 copy-done.7
  74.9 0.9 fusion.28
  75.8 154.3 %conditional.1 = (f32[1728,384]{1,0:T(8,128)}, bf16[1,1,8,16,384]{4,3,2,1,0:T(8,128)(2,1)}) conditional(s32[]{:T(128)} %convert_element_type.55, () %tuple.27, (bf16[10,18,192]{2,0,1:T(8,128)(2,1)S(1)}, f32[128,3456]{1,0:T(8,128)S(1)}, s32[]{:T(128)}, (), (), /*index=5*/s32[4]{0:T(128)}, s32[4]{0:T(128)}, (), (), f32[128,384]{1,0:T(8,128)S(1)}) %tuple.96), branch_computations={%region_2.3_spmd, %region_3.6_spmd} | conditional | flops 5892580352 | bytes 156235216 | solution.py:266
  75.8 22.0 %all-gather = bf16[80,18,192]{2,1,0:T(8,128)(2,1)S(1)} all-gather(bf16[10,18,192]{2,1,0:T(8,128)(2,1)S(1)} %copy.159), channel_id=2, replica_groups=mesh['face'=4,'tile'=8] {'tile'}, dimensions={0}, use_global_device_ids=true | all-gather | bytes 622080 | tf_op jit(solution)/shard_map/cond/branch_1_fun/all_gather | solution.py:184
  97.9 1.1 constant_dynamic-update-slice_fusion.3
  99.0 0.9 collective-permute-start.1
  99.9 1.5 collective-permute-start
  101.4 1.4 collective-permute-start.2
  105.0 0.7 copy_bitcast_fusion
  105.7 0.8 maximum_bitcast_fusion
  106.5 18.3 %all-gather.1 = f32[8,52,384]{2,1,0:T(8,128)} all-gather(f32[1,52,384]{2,1,0:T(8,128)S(1)} %maximum_bitcast_fusion), channel_id=1, replica_groups=mesh['face'=4,'tile'=8] {'tile'}, dimensions={0}, use_global_device_ids=true | all-gather | bytes 718848 | tf_op jit(solution)/shard_map/cond/branch_1_fun/all_gather | solution.py:147
  124.8 2.0 reshape.244
  126.8 1.6 fusion
  128.4 17.6 %all_gather.18 = f32[512,384]{1,0:T(8,128)} all-gather(f32[128,384]{1,0:T(8,128)S(1)} %fusion), channel_id=1, replica_groups=mesh['face'=4,'tile'=8] {'face'}, dimensions={0}, use_global_device_ids=true | all-gather | bytes 983040 | tf_op jit(solution)/shard_map/cond/branch_1_fun/all_gather | solution.py:153
  146.0 0.7 dynamic-slice_bitcast_fusion
  146.7 1.5 fusion.8
  148.2 0.8 select_reduce_fusion.1
  148.9 0.7 compare_select_fusion.1
  149.6 1.5 convolution_add_fusion
  151.2 0.8 fusion.6
  152.0 17.9 %all_gather.19 = bf16[8,128,384]{2,1,0:T(8,128)(2,1)} all-gather(bf16[1,128,384]{2,1,0:T(8,128)(2,1)} %bitcast.19), channel_id=1, replica_groups=mesh['face'=4,'tile'=8] {'tile'}, dimensions={0}, use_global_device_ids=true | all-gather | bytes 884736 | tf_op jit(solution)/shard_map/cond/branch_1_fun/all_gather | solution.py:184
  169.9 1.4 collective-permute-start.5
  171.3 1.2 collective-permute-start.4
  173.0 1.2 constant_dynamic-update-slice_fusion.2
  174.3 1.2 constant_dynamic-update-slice_fusion.1
  175.5 1.2 constant_dynamic-update-slice_fusion
  176.7 3.6 %fusion.62 = (bf16[32,8,16,192]{3,0,2,1:T(8,128)(2,1)}, bf16[32,8,16,192]{3,0,2,1:T(8,128)(2,1)}, bf16[32,8,16,192]{3,0,2,1:T(8,128)(2,1)}, bf16[32,8,16,192]{3,...) fusion(bf16[32,10,18,192]{3,0,2,1:T(8,128)(2,1)S(1)} %constant_, ...), kind=kLoop, calls=%fused_computation.149 | loop fusion | bytes 28311552 | tf_op jit(solution)/shard_map/cond/branch_1_fun/slice | solution.py:249
  180.3 2.9 %copy.138 = bf16[32,8,16,192]{3,2,1,0:T(8,128)(2,1)S(1)} copy(bf16[32,8,16,192]{3,0,2,1:T(8,128)(2,1)} %get-tuple-element.158) | data formatting | bytes 3145728 | tf_op jit(solution)/shard_map/cond/branch_1_fun/slice | solution.py:249
  183.3 1.2 copy.137
  184.9 1.2 copy.136
  186.0 1.2 copy.135
  187.2 1.2 copy.134
  188.4 1.2 copy.133
  189.6 1.2 copy.132
  190.8 1.2 copy.131
  192.0 1.2 copy.130
  193.2 18.7 %collective-permute-done.4 = bf16[8,128,384]{2,1,0:T(8,128)(2,1)} collective-permute-done((bf16[8,128,384]{2,1,0:T(8,128)(2,1)}, bf16[8,128,384]{2,1,0:T(8,128)(2,1)}, u32[]{:S(2)}, u32[]{:S(2)}) %collective-permute-start.4) | collective-permute-done | bytes 786464 | tf_op jit(solution)/shard_map/cond/branch_1_fun/ppermute | solution.py:188
  212.0 2.3 pad_maximum_fusion
  214.3 1.7 convolution_dynamic-update-slice_fusion.8
  216.0 1.7 convolution_dynamic-update-slice_fusion.7
  217.8 1.7 convolution_dynamic-update-slice_fusion.6
  219.5 1.7 convolution_dynamic-update-slice_fusion.5
  221.3 1.8 convolution_dynamic-update-slice_fusion.4
  223.0 1.8 convolution_dynamic-update-slice_fusion.3
  224.8 1.8 convolution_dynamic-update-slice_fusion.2
  226.6 1.8 convolution_dynamic-update-slice_fusion.1
  228.3 1.8 convolution_dynamic-update-slice_fusion
  230.1 25.9 %all-reduce.15.cloned.1.call-done.out_ref = f32[3456,384]{1,0:T(8,128)} async-done(((f32[3456,384]{1,0:T(8,128)}), f32[3456,384]{1,0:T(8,128)}) %all-reduce.15.cloned.1.call-update) | async-done | bytes 5308432 | tf_op jit(solution)/shard_map/psum | solution.py:239
  255.9 7.4 %shard_map.161 = (bf16[1728,384]{1,0:T(8,128)(2,1)}, bf16[3456,384]{1,0:T(8,128)(2,1)}) custom-call(f32[1728,384]{1,0:T(8,128)} %get-tuple-element.91.in_ref, f32[3456,384]{1,0:T(8,128)} %all-reduce.15.cloned.1.call-done.out_ref), custom_call_target="tpu_custom_call" | custom-call | tf_op jit(solution)/shard_map/pallas_call | solution.py:279
  (92 shorter events, 8.6 us)
Async XLA Ops:
  7.2 63.0 %copy-start = (bf16[3,3,384,384]{3,2,1,0:T(8,128)(2,1)S(1)}, bf16[3,3,384,384]{3,2,1,0:T(8,128)(2,1)}, u32[]{:S(2)}) copy-start(bf16[3,3,384,384]{3,2,1,0:T(8,128)(2,1)} %param.19) | copy-start | bytes 7962628
  7.2 33.7 %copy-start.5 = (bf16[1,1,8,16,192]{4,3,2,1,0:T(8,128)(2,1)S(1)}, bf16[1,1,8,16,192]{4,3,2,1,0:T(8,128)(2,1)}, u32[]{:S(2)}) copy-start(bf16[1,1,8,16,192]{4,3,2,1,0:T(8,128)(2,1)} %param.16) | copy-start | bytes 147460
  7.2 248.8 %all-reduce.15.cloned.1.call-start = ((), (), s32[]{:S(2)}) async-start(), calls=%async_computation | async-start | bytes 10616832 | tf_op jit(solution)/shard_map/psum | solution.py:239
  36.1 0.5 copy-start.10
  36.1 0.6 copy-start.12
  37.4 0.5 copy-start.14
  37.7 0.6 copy-start.6
  37.7 0.6 copy-start.8
  69.9 0.9 copy-start.4
  74.1 0.7 copy-start.7
  74.1 0.7 copy-start.9
  99.0 75.2 %collective-permute-start.1 = (bf16[8,10,18,192]{3,0,2,1:T(8,128)(2,1)}, bf16[8,10,18,192]{3,0,2,1:T(8,128)(2,1)}, u32[]{:S(2)}, u32[]{:S(2)}) collective-permute-start(bf16[8,10,18,192]{3,0,2,1:T(8,128)(2,1)} %get-tuple-element.157), channel_id=1, source_target_pairs={{0,16},{8,24},{16,0},{24,8},{1,17},{9,25},{17,1},{25,9},{2,18},{10... | collective-permute-start | bytes 1658888 | tf_op jit(solution)/shard_map/cond/branch_1_fun/ppermute | solution.py:188
  99.9 72.6 %collective-permute-start = (bf16[8,10,18,192]{3,0,2,1:T(8,128)(2,1)}, bf16[8,10,18,192]{3,0,2,1:T(8,128)(2,1)}, u32[]{:S(2)}, u32[]{:S(2)}) collective-permute-start(bf16[8,10,18,192]{3,0,2,1:T(8,128)(2,1)} %get-tuple-element.157), channel_id=1, source_target_pairs={{0,8},{8,16},{16,24},{24,0},{1,9},{9,17},{17,25},{25,1},{2,10},{10... | collective-permute-start | bytes 1658888 | tf_op jit(solution)/shard_map/cond/branch_1_fun/ppermute | solution.py:188
  101.4 74.0 %collective-permute-start.2 = (bf16[8,10,18,192]{3,0,2,1:T(8,128)(2,1)}, bf16[8,10,18,192]{3,0,2,1:T(8,128)(2,1)}, u32[]{:S(2)}, u32[]{:S(2)}) collective-permute-start(bf16[8,10,18,192]{3,0,2,1:T(8,128)(2,1)} %get-tuple-element.157), channel_id=1, source_target_pairs={{0,24},{8,0},{16,8},{24,16},{1,25},{9,1},{17,9},{25,17},{2,26},{10... | collective-permute-start | bytes 1658888 | tf_op jit(solution)/shard_map/cond/branch_1_fun/ppermute | solution.py:188
  103.2 45.0 %copy-start.11 = (s32[4]{0:T(128)S(1)}, s32[4]{0:T(128)}, u32[]{:S(2)}) copy-start(s32[4]{0:T(128)} %get-tuple-element.78) | copy-start | bytes 52 | tf_op jit(solution)/shard_map/cond
  106.5 40.2 %copy-start.13 = (s32[48]{0:T(128)S(1)}, s32[48]{0:T(128)}, u32[]{:S(2)}) copy-start(s32[48]{0:T(128)} %iota_add_fusion) | copy-start | bytes 580 | tf_op jit(solution)/shard_map/cond
  169.9 23.3 %collective-permute-start.5 = (bf16[8,128,384]{2,1,0:T(8,128)(2,1)}, bf16[8,128,384]{2,1,0:T(8,128)(2,1)}, u32[]{:S(2)}, u32[]{:S(2)}) collective-permute-start(bf16[8,128,384]{2,1,0:T(8,128)(2,1)} %all_gather.19), channel_id=1, source_target_pairs={{0,24},{8,0},{16,8},{24,16},{1,25},{9,1},{17,9},{25,17},{2,26},{10... | collective-permute-start | bytes 2359304 | tf_op jit(solution)/shard_map/cond/branch_1_fun/ppermute | solution.py:188
  171.3 40.7 %collective-permute-start.4 = (bf16[8,128,384]{2,1,0:T(8,128)(2,1)}, bf16[8,128,384]{2,1,0:T(8,128)(2,1)}, u32[]{:S(2)}, u32[]{:S(2)}) collective-permute-start(bf16[8,128,384]{2,1,0:T(8,128)(2,1)} %all_gather.19), channel_id=1, source_target_pairs={{0,16},{8,24},{16,0},{24,8},{1,17},{9,25},{17,1},{25,9},{2,18},{10... | collective-permute-start | bytes 2359304 | tf_op jit(solution)/shard_map/cond/branch_1_fun/ppermute | solution.py:188
  172.5 39.4 %collective-permute-start.3 = (bf16[8,128,384]{2,1,0:T(8,128)(2,1)}, bf16[8,128,384]{2,1,0:T(8,128)(2,1)}, u32[]{:S(2)}, u32[]{:S(2)}) collective-permute-start(bf16[8,128,384]{2,1,0:T(8,128)(2,1)} %all_gather.19), channel_id=1, source_target_pairs={{0,8},{8,16},{16,24},{24,0},{1,9},{9,17},{17,25},{25,1},{2,10},{10... | collective-permute-start | bytes 2359304 | tf_op jit(solution)/shard_map/cond/branch_1_fun/ppermute | solution.py:188
  180.3 2.9 %copy-start.3 = (bf16[32,8,16,192]{3,0,2,1:T(8,128)(2,1)S(1)}, bf16[32,8,16,192]{3,0,2,1:T(8,128)(2,1)}, u32[]{:S(2)}) copy-start(bf16[32,8,16,192]{3,0,2,1:T(8,128)(2,1)} %get-tuple-element.159) | copy-start | bytes 4718596 | tf_op jit(solution)/shard_map/cond
  183.3 1.6 copy-start.2
  255.9 7.4 %copy-start.1 = (bf16[3,3,384,384]{3,2,1,0:T(8,128)(2,1)S(1)}, bf16[3,3,384,384]{3,2,1,0:T(8,128)(2,1)}, u32[]{:S(2)}) copy-start(bf16[3,3,384,384]{3,2,1,0:T(8,128)(2,1)} %param.19) | copy-start | bytes 7962628
Sparse Core Ops, SparseCore 0:
  74.3 181.6 all-reduce.14

commit v14 on v13

--- a/solution.py
+++ b/solution.py
@@ -123,8 +123,12 @@
         rims,
         preferred_element_type=jnp.float32,
     ).astype(cells.dtype)
-    edge_set = lax.all_gather(edges, "face", axis=0, tiled=True)
-    pool = jnp.concatenate([rims, edge_set], axis=0)
+    faces = lax.axis_size("face")
+    parts = [edges]
+    for shift in range(1, faces):
+        pairs = [(i, (i + shift) % faces) for i in range(faces)]
+        parts.append(lax.ppermute(edges, "face", pairs))
+    pool = jnp.concatenate([rims] + parts, axis=0)
     halo = jnp.dot(
         one_hot(source, jnp.arange(pool.shape[0]), cells.dtype),
         pool,
@@ -199,7 +203,9 @@
     link_row = lax.dynamic_index_in_dim(seam_link, face_pos, 0, False)
     turn_row = lax.dynamic_index_in_dim(seam_turn, face_pos, 0, False)
     maps = face_maps(tiles, height, breadth)
-    source = halo_source(maps, place, link_row, turn_row)
+    faces = lax.axis_size("face")
+    offset_row = ((face_pos - link_row // 4) % faces) * 4 + link_row % 4
+    source = halo_source(maps, place, offset_row, turn_row)
     padded_tile_in = padded_tile(cells, maps, source)
     unfolded_in = unfold(padded_tile_in, height, breadth)
     pre_one = jnp.dot(

time: 271 us -> 272 us (level)
  blocking collectives: 124 us -> 107 us
  starting transfers between devices: 6.99 us -> 15.8 us
  waiting for transfers between devices: 44.6 us -> 49.1 us
  local copies, waits for them, and re-layouts: 35.1 us -> 38.2 us
    all_gather x2 -> x0, blocking collectives: 18.2 us -> none  [padded_tile(): edge_set = lax.all_gather(edges, 'face', axis=0, tiled=True)]
    ppermute x0 -> x6, starting transfers between devices: none -> 7.59 us  [padded_tile(): parts.append(lax.ppermute(edges, 'face', pairs))]
    ppermute x0 -> x6, waiting for transfers between devices: none -> 4.1 us  [padded_tile(): parts.append(lax.ppermute(edges, 'face', pairs))]
  transfers between devices with their start and end apart: 7 -> 13, of which waited for: 2 -> 4; matrix products, arithmetic and copies ran while one was open for 20% -> 22% of each run, Pallas kernels for 0% -> 0%
where the time goes in v14:
time: 272 us; the launch traced here: 271 us
  blocking collectives  107 us (39%)
  waiting for transfers between devices  49.1 us (18%)
  local copies, waits for them, and re-layouts  38.2 us (14%)
  matrix products  30.4 us (11%)
  starting transfers between devices  15.8 us (6%)
  between operations  14.5 us (5%)
  other arithmetic  8.5 us (3%)
  Pallas kernels  7.41 us (3%)
    all_gather x2, blocking collectives, gather_all(): local = lax.all_gather(block, 'tile', axis=0, tiled=True)  40.1 us
    all_gather x2, blocking collectives, padded_tile(): rims = lax.all_gather(rim_of(cells), 'tile', axis=0, tiled=True)  30.2 us
    psum x1, waiting for transfers between devices, body(): total_out = lax.psum(grad_w_out, ('face', 'tile'))  27 us
    all_gather x1, blocking collectives, return_border(): seam_set = lax.all_gather(seam_sum, 'face', axis=0, tiled=True)  18.8 us
    all_gather x1, blocking collectives, return_border(): borders = lax.all_gather(border, 'tile', axis=0, tiled=True)  18 us
    ppermute x6, waiting for transfers between devices, gather_all(): parts.append(lax.ppermute(local, 'face', pairs))  18 us
    slice x10, local copies, waits for them, and re-layouts, rest(): every_pad[:, down_step:down_step + height, side_step:side_step + breadth]  16.1 us
    dot_general x9, matrix products, rest(): lax.dot_general(window.reshape(-1, width_in), every_grad, (((0,), (0,)),...  15.8 us
  transfers between devices with their start and end apart: 13, of which 4 were waited for; matrix products, arithmetic and copies ran while one was open for 22% of the time, Pallas kernels for 0%

profile of v14, /device:TPU:0, one launch (start us, length us, event | category | flops | bytes accessed | tf_op | source)
XLA Modules:
  0.0 271.3 jit_solution(2779409253141448182)
XLA Ops:
  7.2 0.9 slice_bitcast_fusion.9
  8.1 0.9 copy.187
  9.0 15.9 %all_gather.18 = bf16[384,192]{1,0:T(8,128)(2,1)S(1)} all-gather(bf16[48,192]{1,0:T(8,128)(2,1)S(1)} %pad_maximum_fusion.9), channel_id=1, replica_groups=mesh['face'=4,'tile'=8] {'tile'}, dimensions={0}, use_global_device_ids=true | all-gather | bytes 165888 | tf_op jit(solution)/shard_map/all_gather | solution.py:120
  24.9 0.9 convolution_convert_fusion.1
  25.8 2.5 collective-permute-start.8
  30.9 1.2 fusion.46
  32.9 0.7 compare_select_fusion.2
  36.6 1.3 convolution_convert_fusion.3
  41.1 1.1 concatenate.80
  42.2 1.7 multiply_convert_fusion
  44.0 14.4 %all_gather.19 = bf16[384,384]{1,0:T(8,128)(2,1)S(1)} all-gather(bf16[48,384]{1,0:T(8,128)(2,1)S(1)} %pad_maximum_fusion.8), channel_id=1, replica_groups=mesh['face'=4,'tile'=8] {'tile'}, dimensions={0}, use_global_device_ids=true | all-gather | bytes 331776 | tf_op jit(solution)/shard_map/all_gather | solution.py:120
  58.4 0.9 constant_dynamic-update-slice_fusion.12
  59.4 2.4 collective-permute-start.9
  62.3 1.0 collective-permute-start.10
  63.4 2.6 collective-permute-done.9
  66.0 1.5 collective-permute-done.10
  69.1 3.3 %fusion.20 = f32[3456,384]{1,0:T(8,128)} fusion(bf16[128,3456]{1,0:T(8,128)(2,1)S(1)} %constant_dynamic-update-slice_fusion.14, f32[128,384]{1,0:T(8,128)S(1)} %fusion.67, bf16[128,384]{1,0:T(8,128)(2,1)S(1)} %bitcast.193), kind=kOutput, calls=%fused_computation.60 | convolution fusion | flops 340279296 | bytes 6488064 | tf_op jit(solution)/shard_map/dot_general | solution.py:220
  73.2 0.9 fusion.22
  74.1 156.0 %conditional.1 = (f32[1728,384]{1,0:T(8,128)}, bf16[1,1,8,16,384]{4,3,2,1,0:T(8,128)(2,1)}) conditional(s32[]{:T(128)} %convert_element_type.55, () %tuple.27, (bf16[10,18,192]{2,0,1:T(8,128)(2,1)S(1)}, f32[128,3456]{1,0:T(8,128)S(1)}, s32[]{:T(128)}, (), (), /*index=5*/s32[1,4]{1,0:T(1,128)}, s32[4]{0:T(128)}, (), (), f32[128,384]{1,0:T(8,128)S(1)}) %tuple.99), branch_computations={%region_2.3_spmd, %region_3.6_spmd} | conditional | flops 5892580352 | bytes 156241808 | solution.py:272
  74.1 22.2 %all-gather = bf16[80,18,192]{2,1,0:T(8,128)(2,1)S(1)} all-gather(bf16[10,18,192]{2,1,0:T(8,128)(2,1)S(1)} %copy.176), channel_id=2, replica_groups=mesh['face'=4,'tile'=8] {'tile'}, dimensions={0}, use_global_device_ids=true | all-gather | bytes 622080 | tf_op jit(solution)/shard_map/cond/branch_1_fun/all_gather | solution.py:188
  96.4 1.1 constant_dynamic-update-slice_fusion.3
  97.7 3.5 %collective-permute-start = (bf16[8,10,18,192]{3,0,2,1:T(8,128)(2,1)}, bf16[8,10,18,192]{3,0,2,1:T(8,128)(2,1)}, u32[]{:S(2)}, u32[]{:S(2)}) collective-permute-start(bf16[8,10,18,192]{3,0,2,1:T(8,128)(2,1)} %get-tuple-element.158), channel_id=1, source_target_pairs={{0,8},{8,16},{16,24},{24,0},{1,9},{9,17},{17,25},{25,1},{2,10},{10... | collective-permute-start | bytes 1658888 | tf_op jit(solution)/shard_map/cond/branch_1_fun/ppermute | solution.py:192
  101.2 1.2 collective-permute-start.2
  104.5 0.7 copy_bitcast_fusion
  105.2 0.8 maximum_bitcast_fusion
  106.0 18.0 %all-gather.1 = f32[8,52,384]{2,1,0:T(8,128)} all-gather(f32[1,52,384]{2,1,0:T(8,128)S(1)} %maximum_bitcast_fusion), channel_id=1, replica_groups=mesh['face'=4,'tile'=8] {'tile'}, dimensions={0}, use_global_device_ids=true | all-gather | bytes 718848 | tf_op jit(solution)/shard_map/cond/branch_1_fun/all_gather | solution.py:151
  124.1 2.0 reshape.244
  126.1 1.6 fusion
  127.6 18.8 %all_gather.14 = f32[512,384]{1,0:T(8,128)} all-gather(f32[128,384]{1,0:T(8,128)S(1)} %fusion), channel_id=1, replica_groups=mesh['face'=4,'tile'=8] {'face'}, dimensions={0}, use_global_device_ids=true | all-gather | bytes 983040 | tf_op jit(solution)/shard_map/cond/branch_1_fun/all_gather | solution.py:157
  146.4 0.7 dynamic-slice_bitcast_fusion
  147.1 1.5 fusion.8
  148.6 0.7 select_reduce_fusion.1
  149.4 0.7 compare_select_fusion.1
  150.1 1.5 convolution_add_fusion
  151.7 0.8 fusion.6
  152.4 17.9 %all_gather.15 = bf16[8,128,384]{2,1,0:T(8,128)(2,1)} all-gather(bf16[1,128,384]{2,1,0:T(8,128)(2,1)} %bitcast.20), channel_id=1, replica_groups=mesh['face'=4,'tile'=8] {'tile'}, dimensions={0}, use_global_device_ids=true | all-gather | bytes 884736 | tf_op jit(solution)/shard_map/cond/branch_1_fun/all_gather | solution.py:188
  170.3 1.5 collective-permute-start.5
  171.8 1.2 collective-permute-start.4
  173.6 1.2 constant_dynamic-update-slice_fusion.2
  174.9 1.2 constant_dynamic-update-slice_fusion.1
  176.1 1.2 constant_dynamic-update-slice_fusion
  177.3 3.6 %fusion.57 = (bf16[32,8,16,192]{3,0,2,1:T(8,128)(2,1)}, bf16[32,8,16,192]{3,0,2,1:T(8,128)(2,1)}, bf16[32,8,16,192]{3,0,2,1:T(8,128)(2,1)}, bf16[32,8,16,192]{3,...) fusion(bf16[32,10,18,192]{3,0,2,1:T(8,128)(2,1)S(1)} %constant_, ...), kind=kLoop, calls=%fused_computation.162 | loop fusion | bytes 28311552 | tf_op jit(solution)/shard_map/cond/branch_1_fun/slice | solution.py:255
  181.0 2.9 %copy.152 = bf16[32,8,16,192]{3,2,1,0:T(8,128)(2,1)S(1)} copy(bf16[32,8,16,192]{3,0,2,1:T(8,128)(2,1)} %get-tuple-element.161) | data formatting | bytes 3145728 | tf_op jit(solution)/shard_map/cond/branch_1_fun/slice | solution.py:255
  183.9 1.2 copy.151
  185.5 1.2 copy.150
  186.7 1.2 copy.149
  187.9 1.2 copy.148
  189.1 1.2 copy.147
  190.3 1.2 copy.146
  191.5 1.2 copy.145
  192.7 1.2 copy.144
  193.9 18.0 %collective-permute-done.4 = bf16[8,128,384]{2,1,0:T(8,128)(2,1)} collective-permute-done((bf16[8,128,384]{2,1,0:T(8,128)(2,1)}, bf16[8,128,384]{2,1,0:T(8,128)(2,1)}, u32[]{:S(2)}, u32[]{:S(2)}) %collective-permute-start.4) | collective-permute-done | bytes 786464 | tf_op jit(solution)/shard_map/cond/branch_1_fun/ppermute | solution.py:192
  211.9 2.3 pad_maximum_fusion
  214.2 1.8 convolution_dynamic-update-slice_fusion.8
  216.0 1.8 convolution_dynamic-update-slice_fusion.7
  217.7 1.7 convolution_dynamic-update-slice_fusion.6
  219.5 1.8 convolution_dynamic-update-slice_fusion.5
  221.2 1.8 convolution_dynamic-update-slice_fusion.4
  223.0 1.8 convolution_dynamic-update-slice_fusion.3
  224.7 1.8 convolution_dynamic-update-slice_fusion.2
  226.5 1.8 convolution_dynamic-update-slice_fusion.1
  228.3 1.8 convolution_dynamic-update-slice_fusion
  230.1 27.0 %all-reduce.15.cloned.1.call-done.out_ref = f32[3456,384]{1,0:T(8,128)} async-done(((f32[3456,384]{1,0:T(8,128)}), f32[3456,384]{1,0:T(8,128)}) %all-reduce.15.cloned.1.call-update) | async-done | bytes 5308432 | tf_op jit(solution)/shard_map/psum | solution.py:245
  257.0 7.4 %shard_map.161 = (bf16[1728,384]{1,0:T(8,128)(2,1)}, bf16[3456,384]{1,0:T(8,128)(2,1)}) custom-call(f32[1728,384]{1,0:T(8,128)} %get-tuple-element.92.in_ref, f32[3456,384]{1,0:T(8,128)} %all-reduce.15.cloned.1.call-done.out_ref), custom_call_target="tpu_custom_call" | custom-call | tf_op jit(solution)/shard_map/pallas_call | solution.py:285
  (114 shorter events, 15.6 us)
Async XLA Ops:
  7.2 61.3 %copy-start = (bf16[3,3,384,384]{3,2,1,0:T(8,128)(2,1)S(1)}, bf16[3,3,384,384]{3,2,1,0:T(8,128)(2,1)}, u32[]{:S(2)}) copy-start(bf16[3,3,384,384]{3,2,1,0:T(8,128)(2,1)} %param.19) | copy-start | bytes 7962628
  7.2 33.9 %copy-start.5 = (bf16[1,1,8,16,192]{4,3,2,1,0:T(8,128)(2,1)S(1)}, bf16[1,1,8,16,192]{4,3,2,1,0:T(8,128)(2,1)}, u32[]{:S(2)}) copy-start(bf16[1,1,8,16,192]{4,3,2,1,0:T(8,128)(2,1)} %param.16) | copy-start | bytes 147460
  7.2 249.8 %all-reduce.15.cloned.1.call-start = ((), (), s32[]{:S(2)}) async-start(), calls=%async_computation | async-start | bytes 10616832 | tf_op jit(solution)/shard_map/psum | solution.py:245
  25.8 10.0 %collective-permute-start.8 = (bf16[128,192]{0,1:T(8,128)(2,1)S(1)}, bf16[128,192]{0,1:T(8,128)(2,1)S(1)}, u32[]{:S(2)}, u32[]{:S(2)}) collective-permute-start(bf16[128,192]{0,1:T(8,128)(2,1)S(1)} %convolution_convert_fusion.1), channel_id=1, source_target_pairs={{0,24},{8,0},{16,8},{24,16},{1,25},{9,1},{17,9},{25,17},{2,26},{10... | collective-permute-start | bytes 147464 | tf_op jit(solution)/shard_map/ppermute | solution.py:130
  28.3 6.8 %collective-permute-start.7 = (bf16[128,192]{0,1:T(8,128)(2,1)S(1)}, bf16[128,192]{0,1:T(8,128)(2,1)S(1)}, u32[]{:S(2)}, u32[]{:S(2)}) collective-permute-start(bf16[128,192]{0,1:T(8,128)(2,1)S(1)} %convolution_convert_fusion.1), channel_id=1, source_target_pairs={{0,16},{8,24},{16,0},{24,8},{1,17},{9,25},{17,1},{25,9},{2,18},{10... | collective-permute-start | bytes 147464 | tf_op jit(solution)/shard_map/ppermute | solution.py:130
  28.8 5.5 %collective-permute-start.6 = (bf16[128,192]{0,1:T(8,128)(2,1)S(1)}, bf16[128,192]{0,1:T(8,128)(2,1)S(1)}, u32[]{:S(2)}, u32[]{:S(2)}) collective-permute-start(bf16[128,192]{0,1:T(8,128)(2,1)S(1)} %convolution_convert_fusion.1), channel_id=1, source_target_pairs={{0,8},{8,16},{16,24},{24,0},{1,9},{9,17},{17,25},{25,1},{2,10},{10... | collective-permute-start | bytes 147464 | tf_op jit(solution)/shard_map/ppermute | solution.py:130
  30.9 3.4 %copy-start.13 = (s32[4]{0:T(128)}, s32[4]{0:T(128)S(1)}, u32[]{:S(2)}) copy-start(s32[4]{0:T(128)S(1)} %fusion.41) | copy-start | bytes 52
  33.7 4.3 %copy-start.10 = (s32[52]{0:T(128)}, s32[52]{0:T(128)S(1)}, u32[]{:S(2)}) copy-start(s32[52]{0:T(128)S(1)} %compare_select_fusion.2) | copy-start | bytes 628
  37.9 0.6 copy-start.6
  37.9 0.6 copy-start.8
  42.2 25.3 %copy-start.11 = (s32[52]{0:T(128)S(1)}, s32[52]{0:T(128)}, u32[]{:S(2)}) copy-start(s32[52]{0:T(128)} %copy-done.10) | copy-start | bytes 628
  59.4 6.6 %collective-permute-start.9 = (bf16[128,384]{1,0:T(8,128)(2,1)S(1)}, bf16[128,384]{1,0:T(8,128)(2,1)S(1)}, u32[]{:S(2)}, u32[]{:S(2)}) collective-permute-start(bf16[128,384]{1,0:T(8,128)(2,1)S(1)} %get-tuple-element.228), channel_id=1, source_target_pairs={{0,8},{8,16},{16,24},{24,0},{1,9},{9,17},{17,25},{25,1},{2,10},{10... | collective-permute-start | bytes 294920 | tf_op jit(solution)/shard_map/ppermute | solution.py:130
  61.8 5.7 %collective-permute-start.11 = (bf16[128,384]{1,0:T(8,128)(2,1)S(1)}, bf16[128,384]{1,0:T(8,128)(2,1)S(1)}, u32[]{:S(2)}, u32[]{:S(2)}) collective-permute-start(bf16[128,384]{1,0:T(8,128)(2,1)S(1)} %get-tuple-element.228), channel_id=1, source_target_pairs={{0,24},{8,0},{16,8},{24,16},{1,25},{9,1},{17,9},{25,17},{2,26},{10... | collective-permute-start | bytes 294920 | tf_op jit(solution)/shard_map/ppermute | solution.py:130
  62.3 5.1 %collective-permute-start.10 = (bf16[128,384]{1,0:T(8,128)(2,1)S(1)}, bf16[128,384]{1,0:T(8,128)(2,1)S(1)}, u32[]{:S(2)}, u32[]{:S(2)}) collective-permute-start(bf16[128,384]{1,0:T(8,128)(2,1)S(1)} %get-tuple-element.228), channel_id=1, source_target_pairs={{0,16},{8,24},{16,0},{24,8},{1,17},{9,25},{17,1},{25,9},{2,18},{10... | collective-permute-start | bytes 294920 | tf_op jit(solution)/shard_map/ppermute | solution.py:130
  68.2 0.9 copy-start.4
  72.4 0.7 copy-start.7
  72.4 0.7 copy-start.9
  97.5 77.4 %collective-permute-start.1 = (bf16[8,10,18,192]{3,0,2,1:T(8,128)(2,1)}, bf16[8,10,18,192]{3,0,2,1:T(8,128)(2,1)}, u32[]{:S(2)}, u32[]{:S(2)}) collective-permute-start(bf16[8,10,18,192]{3,0,2,1:T(8,128)(2,1)} %get-tuple-element.158), channel_id=1, source_target_pairs={{0,16},{8,24},{16,0},{24,8},{1,17},{9,25},{17,1},{25,9},{2,18},{10... | collective-permute-start | bytes 1658888 | tf_op jit(solution)/shard_map/cond/branch_1_fun/ppermute | solution.py:192
  97.7 75.4 %collective-permute-start = (bf16[8,10,18,192]{3,0,2,1:T(8,128)(2,1)}, bf16[8,10,18,192]{3,0,2,1:T(8,128)(2,1)}, u32[]{:S(2)}, u32[]{:S(2)}) collective-permute-start(bf16[8,10,18,192]{3,0,2,1:T(8,128)(2,1)} %get-tuple-element.158), channel_id=1, source_target_pairs={{0,8},{8,16},{16,24},{24,0},{1,9},{9,17},{17,25},{25,1},{2,10},{10... | collective-permute-start | bytes 1658888 | tf_op jit(solution)/shard_map/cond/branch_1_fun/ppermute | solution.py:192
  101.2 74.9 %collective-permute-start.2 = (bf16[8,10,18,192]{3,0,2,1:T(8,128)(2,1)}, bf16[8,10,18,192]{3,0,2,1:T(8,128)(2,1)}, u32[]{:S(2)}, u32[]{:S(2)}) collective-permute-start(bf16[8,10,18,192]{3,0,2,1:T(8,128)(2,1)} %get-tuple-element.158), channel_id=1, source_target_pairs={{0,24},{8,0},{16,8},{24,16},{1,25},{9,1},{17,9},{25,17},{2,26},{10... | collective-permute-start | bytes 1658888 | tf_op jit(solution)/shard_map/cond/branch_1_fun/ppermute | solution.py:192
  102.7 44.4 %copy-start.12 = (s32[416]{0:T(512)S(1)}, s32[416]{0:T(512)}, u32[]{:S(2)}) copy-start(s32[416]{0:T(512)} %constant.137.clone.1) | copy-start | bytes 4996 | tf_op jit(solution)/shard_map/cond
  106.0 41.1 %copy-start.14 = (s32[48]{0:T(128)S(1)}, s32[48]{0:T(128)}, u32[]{:S(2)}) copy-start(s32[48]{0:T(128)} %iota_add_fusion) | copy-start | bytes 580 | tf_op jit(solution)/shard_map/cond
  170.3 23.5 %collective-permute-start.5 = (bf16[8,128,384]{2,1,0:T(8,128)(2,1)}, bf16[8,128,384]{2,1,0:T(8,128)(2,1)}, u32[]{:S(2)}, u32[]{:S(2)}) collective-permute-start(bf16[8,128,384]{2,1,0:T(8,128)(2,1)} %all_gather.15), channel_id=1, source_target_pairs={{0,24},{8,0},{16,8},{24,16},{1,25},{9,1},{17,9},{25,17},{2,26},{10... | collective-permute-start | bytes 2359304 | tf_op jit(solution)/shard_map/cond/branch_1_fun/ppermute | solution.py:192
  171.8 40.1 %collective-permute-start.4 = (bf16[8,128,384]{2,1,0:T(8,128)(2,1)}, bf16[8,128,384]{2,1,0:T(8,128)(2,1)}, u32[]{:S(2)}, u32[]{:S(2)}) collective-permute-start(bf16[8,128,384]{2,1,0:T(8,128)(2,1)} %all_gather.15), channel_id=1, source_target_pairs={{0,16},{8,24},{16,0},{24,8},{1,17},{9,25},{17,1},{25,9},{2,18},{10... | collective-permute-start | bytes 2359304 | tf_op jit(solution)/shard_map/cond/branch_1_fun/ppermute | solution.py:192
  173.0 38.8 %collective-permute-start.3 = (bf16[8,128,384]{2,1,0:T(8,128)(2,1)}, bf16[8,128,384]{2,1,0:T(8,128)(2,1)}, u32[]{:S(2)}, u32[]{:S(2)}) collective-permute-start(bf16[8,128,384]{2,1,0:T(8,128)(2,1)} %all_gather.15), channel_id=1, source_target_pairs={{0,8},{8,16},{16,24},{24,0},{1,9},{9,17},{17,25},{25,1},{2,10},{10... | collective-permute-start | bytes 2359304 | tf_op jit(solution)/shard_map/cond/branch_1_fun/ppermute | solution.py:192
  181.0 2.9 %copy-start.3 = (bf16[32,8,16,192]{3,0,2,1:T(8,128)(2,1)S(1)}, bf16[32,8,16,192]{3,0,2,1:T(8,128)(2,1)}, u32[]{:S(2)}) copy-start(bf16[32,8,16,192]{3,0,2,1:T(8,128)(2,1)} %get-tuple-element.162) | copy-start | bytes 4718596 | tf_op jit(solution)/shard_map/cond
  183.9 1.6 copy-start.2
  257.0 7.4 %copy-start.1 = (bf16[3,3,384,384]{3,2,1,0:T(8,128)(2,1)S(1)}, bf16[3,3,384,384]{3,2,1,0:T(8,128)(2,1)}, u32[]{:S(2)}) copy-start(bf16[3,3,384,384]{3,2,1,0:T(8,128)(2,1)} %param.19) | copy-start | bytes 7962628
Sparse Core Ops, SparseCore 0:
  72.6 184.4 all-reduce.14
